TPU v7x, 128 devices: a whole 4x4x4 slice. The times are simulated.
128 devices in a mesh: batch: 8 (over y, core), seq: 16 (over x, z).
Axes of the slice: x: 4, y: 4, z: 4, core: 2. Of those that a mesh axis runs over, the one named last changes fastest.
Arguments:
- frames: bfloat16 [8, 3072, 1024], P('batch', 'seq'), may hold values from -6 to 6
- lengths: int32 [8], P('batch'), may hold values from 768 to 3072, as said below
- w_qkv: bfloat16 [1024, 3072], replicated, may hold values from -0.25 to 0.25
- w_out: bfloat16 [1024, 1024], replicated, may hold values from -0.1875 to 0.1875
- cotangent: bfloat16 [8, 3072, 1024], P('batch', 'seq'), may hold values from -6 to 6
Outputs:
- output: bfloat16 [8, 3072, 1024], P('batch', 'seq')
- grad_input: bfloat16 [8, 3072, 1024], P('batch', 'seq')
- grad_qkv: float32 [1024, 3072], P('seq')
- grad_out: float32 [1024, 1024], P('seq')
Inputs may be any that keep to these rules, and one draw needn't show every extreme that they name: `lengths`: at least one utterance has all 3072 frames valid.
All inputs are finite; a program needn't handle non-finite values.
Results may differ from a plain program's by a relative error of at most 0.012.
The roundings to bfloat16 on the way count: a program that leaves them out, or rounds other values in their place, can miss the bound.
Values may be sent and summed in bfloat16 or wider, within the bound.
No kernel may reach another device: no remote copies, remote signals or barrier semaphores. Data moves between devices by JAX's collectives and lax.ppermute only.
A program may use at most 128 MiB of HBM per device.

v0:
```python
import jax
import jax.numpy as jnp
from jax import lax
from jax.sharding import PartitionSpec as P

H = 8


def from_partner(array, axis, stride):
    return lax.ppermute(array, axis, [(i, i ^ 1 << stride) for i in range(lax.axis_size(axis))])


def layer_norm(values):
    mean = jnp.mean(values, axis=-1, keepdims=True)
    centred = values - mean
    var = jnp.mean(centred * centred, axis=-1, keepdims=True)
    return centred * lax.rsqrt(var + 1e-05)


def block_forward(query_rows, keys, values, bias, scale):
    scores = jnp.dot(query_rows, keys.T, preferred_element_type=jnp.float32) * scale + bias[None, :]
    top = jnp.max(scores, axis=1, keepdims=True)
    expo = jnp.exp(scores - top)
    probs = expo / jnp.sum(expo, axis=1, keepdims=True)
    p_half = probs.astype(jnp.bfloat16)
    return (probs, p_half, jnp.dot(p_half, values, preferred_element_type=jnp.float32))


def head_backward(query, keys, values, dcontext, bias, scale):
    total, width = query.shape
    rows = min(512, total)
    qblocks = query.reshape(total // rows, rows, width)
    dblocks = dcontext.reshape(total // rows, rows, width)
    key_count = keys.shape[0]

    def step(carry, item):
        dkeys, dvalues = carry
        query_rows, d_rows = item
        probs, p_half, unused = block_forward(query_rows, keys, values, bias, scale)
        dprobs = jnp.dot(d_rows, values.T, preferred_element_type=jnp.float32)
        delta = jnp.sum(probs * dprobs, axis=1, keepdims=True)
        dscores = (probs * (dprobs - delta)).astype(jnp.bfloat16)
        dquery = jnp.dot(dscores, keys, preferred_element_type=jnp.float32) * scale
        dkeys = dkeys + jnp.dot(dscores.T, query_rows, preferred_element_type=jnp.float32) * scale
        dvalues = dvalues + jnp.dot(p_half.T, d_rows, preferred_element_type=jnp.float32)
        return ((dkeys, dvalues), dquery.astype(jnp.bfloat16))

    start = (jnp.zeros((key_count, width), jnp.float32), jnp.zeros((key_count, width), jnp.float32))
    (dkeys, dvalues), dquery = lax.scan(step, start, (qblocks, dblocks))
    return (dquery.reshape(total, width), dkeys, dvalues)


def to_heads(rows_array, groups, head_blocks):
    tok_rows, heads, head_size = rows_array.shape
    local_heads = heads // head_blocks
    part_rows = tok_rows // groups
    shaped = rows_array.reshape(groups, part_rows, head_blocks, local_heads, head_size)
    return shaped.transpose(2, 0, 1, 3, 4).reshape(
        head_blocks * groups, part_rows, local_heads, head_size
    )


def per_device(frames, lengths, w_qkv, w_out, cotangent):
    width = w_out.shape[0]
    head_size = width // H
    scale = float(head_size) ** (-0.5)
    tok_rows = frames.shape[1]
    seq_count = lax.axis_size("seq")
    groups = max(1, seq_count // H)
    local_heads = max(1, H // seq_count)
    head_blocks = H // local_heads
    part_rows = tok_rows // groups
    frame_total = tok_rows * seq_count
    group_index = lax.axis_index("seq") % groups
    length = lengths[0]
    inputs = frames[0].astype(jnp.float32)
    normed = layer_norm(inputs).astype(jnp.bfloat16)
    qkv = jnp.dot(normed, w_qkv, preferred_element_type=jnp.float32).astype(jnp.bfloat16)
    qkv_local = qkv.reshape(tok_rows, 3, H, head_size)
    query_send = to_heads(qkv_local[:, 0], groups, head_blocks)
    paired = (
        qkv_local[:, 1:]
        .reshape(tok_rows, 2, head_blocks, local_heads, head_size)
        .transpose(2, 0, 1, 3, 4)
    )
    paired_send = jnp.broadcast_to(
        paired[:, None], (head_blocks, groups, tok_rows, 2, local_heads, head_size)
    )
    paired_send = paired_send.reshape(seq_count, tok_rows, 2, local_heads, head_size)
    query_recv, paired_recv = (
        lax.all_to_all(query_send, "seq", split_axis=0, concat_axis=0, tiled=True),
        lax.all_to_all(paired_send, "seq", split_axis=0, concat_axis=0, tiled=True),
    )
    queries = query_recv.reshape(seq_count * part_rows, local_heads, head_size)
    keys = paired_recv[:, :, 0].reshape(frame_total, local_heads, head_size)
    values = paired_recv[:, :, 1].reshape(frame_total, local_heads, head_size)
    position = jnp.arange(frame_total, dtype=jnp.int32)
    bias = jnp.where(position < length, 0.0, -1000000000.0).astype(jnp.float32)
    offset = lax.axis_index("seq") * tok_rows
    own_pos = offset + jnp.arange(tok_rows, dtype=jnp.int32)
    valid = (own_pos < length).astype(jnp.float32)
    query = qkv_local[:, 0]
    top = jnp.full((H, tok_rows), -1e30, jnp.float32)
    key_piece = lax.all_gather(qkv_local[:, 1], "seq", axis=0, tiled=True)
    value_piece = lax.all_gather(qkv_local[:, 2], "seq", axis=0, tiled=True)
    key_pos = jnp.arange(key_piece.shape[0], dtype=jnp.int32)
    key_bias = jnp.where(key_pos < length, 0.0, -1000000000.0).astype(jnp.float32)
    scores = (
        jnp.einsum("qhd,khd->hqk", query, key_piece, preferred_element_type=jnp.float32) * scale
    )
    scores = scores + key_bias[None, None, :]
    new_top = jnp.maximum(top, jnp.max(scores, axis=2))
    expo = jnp.exp(scores - new_top[:, :, None])
    total = jnp.sum(expo, axis=2)
    accum = jnp.einsum(
        "hqk,khd->hqd", expo.astype(jnp.bfloat16), value_piece, preferred_element_type=jnp.float32
    )
    top, total, accum = (new_top, total, accum)
    context = (
        (accum / total[:, :, None]).astype(jnp.bfloat16).transpose(1, 0, 2).reshape(tok_rows, width)
    )
    branch = jnp.dot(context, w_out, preferred_element_type=jnp.float32)
    output = (inputs + valid[:, None] * branch).astype(jnp.bfloat16)
    grad_rows = (cotangent[0].astype(jnp.float32) * valid[:, None]).astype(jnp.bfloat16)
    columns = context
    out_share = lax.psum_scatter(
        jnp.dot(columns.T, grad_rows, preferred_element_type=jnp.float32),
        "seq",
        scatter_dimension=0,
        tiled=True,
    )
    dcontext = jnp.dot(grad_rows, w_out.T, preferred_element_type=jnp.float32).astype(jnp.bfloat16)
    dcontext_send = to_heads(dcontext.reshape(tok_rows, H, head_size), groups, head_blocks)
    dcontext_heads = lax.all_to_all(dcontext_send, "seq", split_axis=0, concat_axis=0, tiled=True)
    dcontext_heads = dcontext_heads.reshape(seq_count * part_rows, local_heads, head_size)
    dquery, dkeys, dvalues = head_backward(
        queries[:, 0], keys[:, 0], values[:, 0], dcontext_heads[:, 0], bias, scale
    )
    query_grads = [dquery]
    paired_grads = [jnp.stack([dkeys, dvalues], axis=1)]
    query_block = jnp.stack(query_grads, axis=1).reshape(
        seq_count, part_rows, 1, local_heads, head_size
    )
    paired_block = jnp.stack(paired_grads, axis=2)
    split_grads = paired_block.reshape(seq_count, groups, part_rows, 2, local_heads, head_size)
    own_half = lax.dynamic_index_in_dim(split_grads, group_index, 1, keepdims=False)
    other_half = lax.dynamic_index_in_dim(split_grads, 1 - group_index, 1, keepdims=False)
    partner_half = from_partner(other_half, "seq", 0)
    paired_rows = (own_half + partner_half).astype(jnp.bfloat16)
    dtrio = jnp.concatenate([query_block, paired_rows], axis=2)
    returned_grads = lax.all_to_all(dtrio, "seq", split_axis=0, concat_axis=0, tiled=True)
    dqkv = returned_grads.reshape(head_blocks, groups, part_rows, 3, local_heads, head_size)
    dqkv = dqkv.transpose(1, 2, 3, 0, 4, 5).reshape(tok_rows, 3 * width)
    columns = normed
    qkv_share = lax.psum_scatter(
        jnp.dot(columns.T, dqkv, preferred_element_type=jnp.float32),
        "seq",
        scatter_dimension=0,
        tiled=True,
    )
    grad_qkv, grad_out = lax.psum((qkv_share, out_share), "batch")
    dnormed = jnp.dot(dqkv, w_qkv.T, preferred_element_type=jnp.float32)
    unused, pull = jax.vjp(layer_norm, inputs)
    grad_input = (cotangent[0].astype(jnp.float32) + pull(dnormed)[0]).astype(jnp.bfloat16)
    return (output[None], grad_input[None], grad_qkv, grad_out)


def solution(mesh):
    return jax.shard_map(
        per_device,
        mesh=mesh,
        in_specs=(P("batch", "seq", None), P("batch"), P(), P(), P("batch", "seq", None)),
        out_specs=(
            P("batch", "seq", None),
            P("batch", "seq", None),
            P("seq", None),
            P("seq", None),
        ),
        check_vma=False,
    )
```

profile of v0, /device:TPU:1, one launch (start us, length us, event | category | flops | bytes accessed | tf_op | source)
XLA Modules:
  0.0 484.2 jit_solution(13089522208990970412)
XLA Ops:
  7.2 1.3 convert_reduce_fusion
  8.5 1.2 fusion.73
  10.3 4.4 fusion.38
  15.0 1.1 fusion.104
  16.1 0.8 copy.42
  16.9 1.8 copy.43
  19.1 1.5 broadcast_in_dim.61
  20.6 8.5 %all-to-all-start.1 = ((bf16[16,192,2,1,128]{4,1,3,2,0:T(8,128)(2,1)}), bf16[16,192,2,1,128]{4,1,3,2,0:T(8,128)(2,1)}, u32[]{:S(2)}, u32[]{:S(2)}) async-start(bf16[16,192,2,1,128]{4,1,3,2,0:T(8,128)(2,1)} %bitcast.192), calls=%async_computation.1 | async-start | bytes 3145728 | tf_op jit(solution)/shard_map/all_to_all | solution.py:92
  29.2 0.8 copy.41
  30.7 0.9 fusion.47
  31.6 0.8 copy.35
  32.5 21.2 %all-to-all-done.1 = bf16[16,192,2,1,128]{4,1,3,2,0:T(8,128)(2,1)} async-done(((bf16[16,192,2,1,128]{4,1,3,2,0:T(8,128)(2,1)}), bf16[16,192,2,1,128]{4,1,3,2,0:T(8,128)(2,1)}, u32[]{:S(2)}, u32[]{:S(2)}) %all-to-all-start.1) | async-done | bytes 1572896 | tf_op jit(solution)/shard_map/all_to_all | solution.py:92
  53.7 7.1 %all-to-all-start = ((bf16[16,96,1,128]{3,1,2,0:T(8,128)(2,1)}), bf16[16,96,1,128]{3,1,2,0:T(8,128)(2,1)S(1)}, u32[]{:S(2)}, u32[]{:S(2)}) async-start(bf16[16,96,1,128]{3,1,2,0:T(8,128)(2,1)} %bitcast.11), calls=%async_computation | async-start | bytes 786432 | tf_op jit(solution)/shard_map/all_to_all | solution.py:91
  60.8 2.4 fusion.103
  63.2 33.5 %all-gather.5.cloned.1.call-done = bf16[3072,1,8,128]{3,0,2,1:T(8,128)(2,1)} async-done(((bf16[192,1,8,128]{3,0,2,1:T(8,128)(2,1)}), bf16[3072,1,8,128]{3,0,2,1:T(8,128)(2,1)}) %all-gather.5.cloned.1.call-update) | async-done | bytes 6291472 | tf_op jit(solution)/shard_map/all_gather | solution.py:104
  96.7 12.2 %fusion.26 = (f32[8,192]{1,0:T(8,128)S(1)}, f32[8,192,3072]{2,1,0:T(8,128)}) fusion(f32[3072]{0:T(1024)S(1)} %fusion.98, bf16[3072,1,8,128]{3,0,2,1:T(8,128)(2,1)} %all-gather.5.cloned.1.call-done, bf16[192,1,8,128]{3,2,1,0:T(8,128)(2,1)} %get-tuple-element.117), kind=kOutput, calls=%fused_computation.34 | convolution fusion | flops 1222113792 | bytes 25577472 | tf_op jit(solution)/shard_map/qhd,khd->hqk/dot_general | solution.py:109
  108.9 10.3 %fusion.27 = f32[8,192]{1,0:T(8,128)S(1)} fusion(f32[8,192,3072]{2,1,0:T(8,128)} %get-tuple-element.121, f32[8,192]{1,0:T(8,128)S(1)} %broadcast_maximum_fusion, f32[3072]{0:T(1024)S(1)} %fusion.98), kind=kLoop, calls=%fused_computation.35 | loop fusion | flops 18872832 | bytes 18898944 | tf_op jit(solution)/shard_map/reduce_sum | solution.py:114
  119.2 4.4 all-to-all-start.2
  123.8 35.6 %all-gather.7.cloned.1.call-done = bf16[3072,1,8,128]{3,0,2,1:T(8,128)(2,1)} async-done(((bf16[192,1,8,128]{3,0,2,1:T(8,128)(2,1)}), bf16[3072,1,8,128]{3,0,2,1:T(8,128)(2,1)}) %all-gather.7.cloned.1.call-update) | async-done | bytes 6291472 | tf_op jit(solution)/shard_map/all_gather | solution.py:105
  159.4 10.5 %fusion.65 = bf16[8,24,8,128]{3,2,1,0:T(8,128)(2,1)S(1)} fusion(bf16[3072,1,8,128]{3,0,2,1:T(8,128)(2,1)} %all-gather.7.cloned.1.call-done, f32[8,192,3072]{2,1,0:T(8,128)} %get-tuple-element.121, f32[8,192]{1,0:T(8,128)S(1)} %broadcast_maximum_fusion, f32[3072]{0:T(1024)S(1)} %fusion.98, f32[192,8]{0,1:T(8,128)S(1)} %bitcast.199), kind=kOutput, calls=%fused_computation.76 | convolution fusion | flops 1227227136 | bytes 25583616 | tf_op jit(solution)/shard_map/hqk,khd->hqd/dot_general | solution.py:115
  169.9 0.7 copy-done.10
  170.6 2.7 fusion.83
  173.4 69.0 %while.15 = (s32[]{:T(128)}, f32[3072,128]{1,0:T(8,128)}, f32[3072,128]{1,0:T(8,128)}, bf16[3,512,128]{2,1,0:T(8,128)(2,1)}, bf16[3,512,128]{2,1,0:T(8,128)(2,1)...) while((s32[]{:T(128)}, f32[3072,128]{1,0:T(8,128)}, ...), condition=%wide.region_8.9_spmd.clone, body=%wide.region_4.0_spmd.clone.sunk | while | flops 2054689280 | bytes 116358872 | solution.py:49
  173.5 0.7 fusion.137
  174.1 1.1 fusion.138
  175.2 2.7 copy-done.1
  177.9 1.4 fusion.139
  179.2 5.8 %convolution_add_fusion.2 = f32[3072,128]{1,0:T(8,128)} fusion(f32[3072,128]{1,0:T(8,128)} %get-tuple-element.200, pred[]{:T(512)S(6)} %compare.4, bf16[3,512,128]{2,1,0:T(8,128)(2,1)} %get-tuple-element.215, s32[]{:T(128)} %get-tuple-element.198, f32[512,3072]{1,0:T(8,128)} %copy-done.1, f32[512]{0:T(512)S(1)} %fusion.139, ...), kind=kOutput, calls=%fused_computation.8.clone.1 | convolution fusion | flops 411303936 | bytes 9585153 | tf_op jit(solution)/shard_map/while/body/eval_jaxpr/dot_general | solution.py:45
  185.1 3.2 multiply_reduce_fusion.2
  188.3 2.9 multiply_convert_fusion.2
  191.2 2.2 fusion.140
  193.4 1.6 fusion.141
  195.7 1.1 fusion.138
  196.8 2.7 copy-done.1
  199.5 1.4 fusion.139
  200.9 6.5 %convolution_add_fusion.2 = f32[3072,128]{1,0:T(8,128)} fusion(f32[3072,128]{1,0:T(8,128)} %get-tuple-element.200, pred[]{:T(512)S(6)} %compare.4, bf16[3,512,128]{2,1,0:T(8,128)(2,1)} %get-tuple-element.215, s32[]{:T(128)} %get-tuple-element.198, f32[512,3072]{1,0:T(8,128)} %copy-done.1, f32[512]{0:T(512)S(1)} %fusion.139, ...), kind=kOutput, calls=%fused_computation.8.clone.1 | convolution fusion | flops 411303936 | bytes 9585153 | tf_op jit(solution)/shard_map/while/body/eval_jaxpr/dot_general | solution.py:45
  207.4 3.2 multiply_reduce_fusion.2
  210.6 2.9 multiply_convert_fusion.2
  213.5 3.6 fusion.140
  217.1 1.6 fusion.141
  219.4 1.1 fusion.138
  220.5 2.7 copy-done.1
  223.2 1.4 fusion.139
  224.6 6.3 %convolution_add_fusion.2 = f32[3072,128]{1,0:T(8,128)} fusion(f32[3072,128]{1,0:T(8,128)} %get-tuple-element.200, pred[]{:T(512)S(6)} %compare.4, bf16[3,512,128]{2,1,0:T(8,128)(2,1)} %get-tuple-element.215, s32[]{:T(128)} %get-tuple-element.198, f32[512,3072]{1,0:T(8,128)} %copy-done.1, f32[512]{0:T(512)S(1)} %fusion.139, ...), kind=kOutput, calls=%fused_computation.8.clone.1 | convolution fusion | flops 411303936 | bytes 9585153 | tf_op jit(solution)/shard_map/while/body/eval_jaxpr/dot_general | solution.py:45
  230.9 3.2 multiply_reduce_fusion.2
  234.1 2.9 multiply_convert_fusion.2
  237.0 3.8 fusion.140
  240.8 1.6 fusion.141
  242.4 2.1 fusion.35
  244.6 1.0 collective-permute-start
  245.7 35.7 %collective-permute-done = f32[16,96,2,1,128]{4,1,3,2,0:T(8,128)S(1)} collective-permute-done((f32[16,96,2,1,128]{4,1,3,2,0:T(8,128)S(1)}, f32[16,96,2,1,128]{4,1,3,2,0:T(8,128)S(1)}, u32[]{:S(2)}, u32[]{:S(2)}) %collective-permute-start) | collective-permute-done | bytes 1572896 | tf_op jit(solution)/shard_map/ppermute | solution.py:10
  281.7 1.1 pad_maximum_fusion
  282.8 21.5 %all_to_all.20 = bf16[16,96,3,1,128]{4,1,3,2,0:T(8,128)(2,1)S(1)} all-to-all(bf16[16,96,3,1,128]{4,1,3,2,0:T(8,128)(2,1)S(1)} %pad_maximum_fusion), channel_id=1, replica_groups=mesh['batch'=8,'seq'=16] {'seq'}, dimensions={0} | all-to-all | bytes 2359296 | tf_op jit(solution)/shard_map/all_to_all | solution.py:151
  304.2 1.8 copy.39
  306.0 3.0 reshape.115
  309.0 7.7 %fusion.79 = f32[1024,3072]{1,0:T(8,128)} fusion(bf16[192,3072]{1,0:T(8,128)(2,1)} %reshape.115, bf16[1,192,1024]{2,1,0:T(8,128)(2,1)S(1)} %copy-done.3, f32[192]{0:T(256)S(1)} %copy-done.15, f32[192]{0:T(256)S(1)} %copy-done.13), kind=kOutput, calls=%fused_computation.87 | convolution fusion | flops 1208745984 | bytes 14157312 | tf_op jit(solution)/shard_map/dot_general | solution.py:156
  316.9 5.5 %fusion.75 = (f32[192]{0:T(256)S(1)}, f32[192,1024]{1,0:T(8,128)S(1)}) fusion(bf16[1,192,1024]{2,1,0:T(8,128)(2,1)S(1)} %copy-done.3, f32[192]{0:T(256)S(1)} %copy-done.13, bf16[192,3072]{1,0:T(8,128)(2,1)} %reshape.115, bf16[1024,3072]{1,0:T(8,128)(2,1)} %param.9), kind=kOutput, calls=%fused_computation.82 | convolution fusion | flops 1208745728 | bytes 8652288 | tf_op jit(solution)/shard_map/dot_general | solution.py:162
  322.4 0.8 copy-done.8
  323.7 87.8 %reduce-scatter.3.cloned.1.call-done = f32[64,3072]{1,0:T(8,128)} async-done(((f32[1024,3072]{1,0:T(8,128)}), f32[64,3072]{1,0:T(8,128)}) %reduce-scatter.3.cloned.1.call-update) | async-done | bytes 786448 | tf_op jit(solution)/shard_map/reduce_scatter | solution.py:155
  411.5 2.2 fusion.85
  413.8 1.3 fusion.46
  415.1 58.9 %all-reduce.3.cloned.1.call-done = (f32[64,3072]{1,0:T(8,128)}, f32[64,1024]{1,0:T(8,128)}) async-done(((f32[64,3072]{1,0:T(8,128)}, f32[64,1024]{1,0:T(8,128)}), (f32[64,3072]{1,0:T(8,128)}, f32[64,1024]{1,0:T(8,128)})) %all-reduce.3.cloned.1.call-update) | async-done | bytes 1048592 | tf_op jit(solution)/shard_map/psum | solution.py:161
  474.0 2.1 copy.86
  476.0 1.7 copy.87
  (79 shorter events, 3.8 us)
Async XLA Ops:
  7.2 23.5 %copy-start = (bf16[1024,1024]{1,0:T(8,128)(2,1)S(1)}, bf16[1024,1024]{1,0:T(8,128)(2,1)}, u32[]{:S(2)}) copy-start(bf16[1024,1024]{1,0:T(8,128)(2,1)} %param.10) | copy-start | bytes 6291460
  7.2 89.5 %all-gather.5.cloned.1.call-start = ((), (), s32[]{:S(2)}) async-start(), calls=%async_computation.8 | async-start | bytes 6684672 | tf_op jit(solution)/shard_map/all_gather | solution.py:104
  8.5 6.2 %copy-start.12 = (f32[192]{0:T(256)}, f32[192]{0:T(256)S(1)}, u32[]{:S(2)}) copy-start(f32[192]{0:T(256)S(1)} %broadcast_multiply_fusion) | copy-start | bytes 2308
  9.8 0.5 copy-start.16
  10.3 4.4 copy-start.14
  16.9 142.5 %all-gather.7.cloned.1.call-start = ((), (), s32[]{:S(2)}) async-start(), calls=%async_computation.9 | async-start | bytes 6684672 | tf_op jit(solution)/shard_map/all_gather | solution.py:105
  18.9 10.3 %copy-start.4 = (bf16[192,1,8,128]{3,2,1,0:T(8,128)(2,1)S(1)}, bf16[192,1,8,128]{3,2,1,0:T(8,128)(2,1)}, u32[]{:S(2)}) copy-start(bf16[192,1,8,128]{3,2,1,0:T(8,128)(2,1)} %get-tuple-element.117) | copy-start | bytes 1179652
  18.9 11.7 %copy-start.5 = (bf16[1,192,1024]{2,1,0:T(8,128)(2,1)S(1)}, bf16[1,192,1024]{2,1,0:T(8,128)(2,1)}, u32[]{:S(2)}) copy-start(bf16[1,192,1024]{2,1,0:T(8,128)(2,1)} %param.11) | copy-start | bytes 1179652
  20.6 33.1 %all-to-all-start.1 = ((bf16[16,192,2,1,128]{4,1,3,2,0:T(8,128)(2,1)}), bf16[16,192,2,1,128]{4,1,3,2,0:T(8,128)(2,1)}, u32[]{:S(2)}, u32[]{:S(2)}) async-start(bf16[16,192,2,1,128]{4,1,3,2,0:T(8,128)(2,1)} %bitcast.192), calls=%async_computation.1 | async-start | bytes 3145728 | tf_op jit(solution)/shard_map/all_to_all | solution.py:92
  30.7 139.2 %copy-start.18 = (f32[192]{0:T(256)}, f32[192]{0:T(256)S(1)}, u32[]{:S(2)}) copy-start(f32[192]{0:T(256)S(1)} %compare_convert_fusion) | copy-start | bytes 2308
  53.7 65.5 %all-to-all-start = ((bf16[16,96,1,128]{3,1,2,0:T(8,128)(2,1)}), bf16[16,96,1,128]{3,1,2,0:T(8,128)(2,1)S(1)}, u32[]{:S(2)}, u32[]{:S(2)}) async-start(bf16[16,96,1,128]{3,1,2,0:T(8,128)(2,1)} %bitcast.11), calls=%async_computation | async-start | bytes 786432 | tf_op jit(solution)/shard_map/all_to_all | solution.py:91
  119.2 54.2 %all-to-all-start.2 = ((bf16[16,96,1,128]{3,1,2,0:T(8,128)(2,1)}), bf16[16,96,1,128]{3,1,2,0:T(8,128)(2,1)}, u32[]{:S(2)}, u32[]{:S(2)}) async-start(bf16[16,96,1,128]{3,1,2,0:T(8,128)(2,1)} %bitcast.195), calls=%async_computation.2 | async-start | bytes 786432 | tf_op jit(solution)/shard_map/all_to_all | solution.py:134
  123.6 200.1 %reduce-scatter.5.cloned.1.call-start = ((), (), s32[]{:S(2)}) async-start(), calls=%async_computation.7 | async-start | bytes 4456448 | tf_op jit(solution)/shard_map/reduce_scatter | solution.py:126
  159.3 11.3 %copy-start.6 = (bf16[1,192,1024]{2,1,0:T(8,128)(2,1)S(1)}, bf16[1,192,1024]{2,1,0:T(8,128)(2,1)}, u32[]{:S(2)}) copy-start(bf16[1,192,1024]{2,1,0:T(8,128)(2,1)} %param.11) | copy-start | bytes 1179652
  169.9 0.7 copy-start.10
  173.4 238.1 %reduce-scatter.3.cloned.1.call-start = ((), (), s32[]{:S(2)}) async-start(), calls=%async_computation.6 | async-start | bytes 13369344 | tf_op jit(solution)/shard_map/reduce_scatter | solution.py:155
  175.2 2.7 copy-start.1
  179.2 5.9 %copy-start.2 = (f32[512,3072]{1,0:T(8,128)S(1)}, f32[512,3072]{1,0:T(8,128)}, u32[]{:S(2)}) copy-start(f32[512,3072]{1,0:T(8,128)} %copy-done.1) | copy-start | bytes 18874372 | tf_op jit(solution)/shard_map/while
  179.2 5.8 %copy-start.9 = (bf16[3072,128]{1,0:T(8,128)(2,1)S(1)}, bf16[3072,128]{1,0:T(8,128)(2,1)}, u32[]{:S(2)}) copy-start(bf16[3072,128]{1,0:T(8,128)(2,1)} %get-tuple-element.216) | copy-start | bytes 2359300 | tf_op jit(solution)/shard_map/while
  196.8 2.7 copy-start.1
  200.9 6.5 %copy-start.2 = (f32[512,3072]{1,0:T(8,128)S(1)}, f32[512,3072]{1,0:T(8,128)}, u32[]{:S(2)}) copy-start(f32[512,3072]{1,0:T(8,128)} %copy-done.1) | copy-start | bytes 18874372 | tf_op jit(solution)/shard_map/while
  200.9 6.5 %copy-start.9 = (bf16[3072,128]{1,0:T(8,128)(2,1)S(1)}, bf16[3072,128]{1,0:T(8,128)(2,1)}, u32[]{:S(2)}) copy-start(bf16[3072,128]{1,0:T(8,128)(2,1)} %get-tuple-element.216) | copy-start | bytes 2359300 | tf_op jit(solution)/shard_map/while
  220.5 2.7 copy-start.1
  224.5 6.3 %copy-start.2 = (f32[512,3072]{1,0:T(8,128)S(1)}, f32[512,3072]{1,0:T(8,128)}, u32[]{:S(2)}) copy-start(f32[512,3072]{1,0:T(8,128)} %copy-done.1) | copy-start | bytes 18874372 | tf_op jit(solution)/shard_map/while
  224.5 6.3 %copy-start.9 = (bf16[3072,128]{1,0:T(8,128)(2,1)S(1)}, bf16[3072,128]{1,0:T(8,128)(2,1)}, u32[]{:S(2)}) copy-start(bf16[3072,128]{1,0:T(8,128)(2,1)} %get-tuple-element.216) | copy-start | bytes 2359300 | tf_op jit(solution)/shard_map/while
  244.6 36.7 %collective-permute-start = (f32[16,96,2,1,128]{4,1,3,2,0:T(8,128)S(1)}, f32[16,96,2,1,128]{4,1,3,2,0:T(8,128)S(1)}, u32[]{:S(2)}, u32[]{:S(2)}) collective-permute-start(f32[16,96,2,1,128]{4,1,3,2,0:T(8,128)S(1)} %bitcast.194), channel_id=1, source_target_pairs={{0,1},{1,0},{2,3},{3,2},{4,5},{5,4},{6,7},{7,6},{8,9},{9,8},{10,11... | collective-permute-start | bytes 4718600 | tf_op jit(solution)/shard_map/ppermute | solution.py:10
  281.4 27.7 %copy-start.3 = (bf16[1,192,1024]{2,1,0:T(8,128)(2,1)S(1)}, bf16[1,192,1024]{2,1,0:T(8,128)(2,1)}, u32[]{:S(2)}) copy-start(bf16[1,192,1024]{2,1,0:T(8,128)(2,1)} %param.7) | copy-start | bytes 1179652
  281.4 27.7 %copy-start.13 = (f32[192]{0:T(256)S(1)}, f32[192]{0:T(256)}, u32[]{:S(2)}) copy-start(f32[192]{0:T(256)} %copy-done.12) | copy-start | bytes 2308
  281.4 27.7 %copy-start.15 = (f32[192]{0:T(256)S(1)}, f32[192]{0:T(256)}, u32[]{:S(2)}) copy-start(f32[192]{0:T(256)} %copy-done.14) | copy-start | bytes 2308
  316.8 5.6 %copy-start.17 = (f32[192]{0:T(256)S(1)}, f32[192]{0:T(256)}, u32[]{:S(2)}) copy-start(f32[192]{0:T(256)} %copy-done.16) | copy-start | bytes 2308
  316.8 94.7 %copy-start.7 = (bf16[1,192,1024]{2,1,0:T(8,128)(2,1)S(1)}, bf16[1,192,1024]{2,1,0:T(8,128)(2,1)}, u32[]{:S(2)}) copy-start(bf16[1,192,1024]{2,1,0:T(8,128)(2,1)} %param.11) | copy-start | bytes 1179652
  316.8 96.9 %copy-start.11 = (bf16[8,24,8,128]{3,2,1,0:T(8,128)(2,1)S(1)}, bf16[8,24,8,128]{3,2,1,0:T(8,128)(2,1)}, u32[]{:S(2)}) copy-start(bf16[8,24,8,128]{3,2,1,0:T(8,128)(2,1)} %copy-done.10) | copy-start | bytes 1179652
  316.8 96.9 %copy-start.19 = (f32[192]{0:T(256)S(1)}, f32[192]{0:T(256)}, u32[]{:S(2)}) copy-start(f32[192]{0:T(256)} %copy-done.18) | copy-start | bytes 2308
  316.8 157.1 %all-reduce.3.cloned.1.call-start = ((), (), s32[]{:S(2)}) async-start(), calls=%async_computation.10 | async-start | bytes 2097152 | tf_op jit(solution)/shard_map/psum | solution.py:161
  322.4 0.9 copy-start.8
Sparse Core Ops, SparseCore 0:
  17.0 79.6 all-gather.4
  98.8 60.4 all-gather.6
  173.5 76.2 reduce-scatter.4
  316.9 94.5 reduce-scatter.2
  413.8 60.1 all-reduce.2
where the time goes:
time: 487 us; the launch traced here: 484 us
  waiting for transfers between devices  273 us (56%)
  matrix products  91.3 us (19%)
  other arithmetic  33.6 us (7%)
  local copies, waits for them, and re-layouts  28.7 us (6%)
  blocking collectives  21.5 us (4%)
  starting transfers between devices  21.3 us (4%)
  between operations  14.8 us (3%)
    reduce_scatter x1, waiting for transfers between devices, per_device(): lax.psum_scatter(jnp.dot(columns.T, dqkv, preferred_element_type=jnp.floa...  87.8 us
    psum x1, waiting for transfers between devices, per_device(): grad_qkv, grad_out = lax.psum((qkv_share, out_share), 'batch')  58.9 us
    ppermute x1, waiting for transfers between devices, from_partner(): lax.ppermute(array, axis, [(i, i ^ 1 << stride) for i in range(lax.axis_s...  35.7 us
    all_gather x1, waiting for transfers between devices, per_device(): value_piece = lax.all_gather(qkv_local[:, 2], 'seq', axis=0, tiled=True)  35.6 us
    all_gather x1, waiting for transfers between devices, per_device(): key_piece = lax.all_gather(qkv_local[:, 1], 'seq', axis=0, tiled=True)  33.5 us
    all_to_all x1, blocking collectives, per_device(): lax.all_to_all(dtrio, 'seq', split_axis=0, concat_axis=0, tiled=True)  21.5 us
    all_to_all x1, waiting for transfers between devices, per_device(): lax.all_to_all(paired_send, 'seq', split_axis=0, concat_axis=0, tiled=True)  21.2 us
    dot_general x3, matrix products, step(): jnp.dot(p_half.T, d_rows, preferred_element_type=jnp.float32)  18.6 us
  transfers between devices with their start and end apart: 9, of which 6 were waited for; matrix products, arithmetic and copies ran while one was open for 27% of the time, Pallas kernels for 0%

commit v1 on v0

v1 whole, which is shorter than its diff:
```python
import jax
import jax.numpy as jnp
from jax import lax
from jax.sharding import PartitionSpec as P

H = 8


def from_partner(array, axis, stride):
    return lax.ppermute(array, axis, [(i, i ^ 1 << stride) for i in range(lax.axis_size(axis))])


def layer_norm(values):
    mean = jnp.mean(values, axis=-1, keepdims=True)
    centred = values - mean
    var = jnp.mean(centred * centred, axis=-1, keepdims=True)
    return centred * lax.rsqrt(var + 1e-05)


def head_pass(query, keys, values, dcontext, bias, scale):
    total, width = query.shape
    rows = min(512, total)
    qblocks = query.reshape(total // rows, rows, width)
    dblocks = dcontext.reshape(total // rows, rows, width)
    key_count = keys.shape[0]

    def step(carry, item):
        dkeys, dvalues = carry
        query_rows, d_rows = item
        scores = jnp.dot(query_rows, keys.T, preferred_element_type=jnp.float32) * scale + bias[None, :]
        top = jnp.max(scores, axis=1, keepdims=True)
        expo = jnp.exp(scores - top)
        probs = expo / jnp.sum(expo, axis=1, keepdims=True)
        p_half = probs.astype(jnp.bfloat16)
        context = jnp.dot(p_half, values, preferred_element_type=jnp.float32).astype(jnp.bfloat16)
        dprobs = jnp.dot(d_rows, values.T, preferred_element_type=jnp.float32)
        delta = jnp.sum(probs * dprobs, axis=1, keepdims=True)
        dscores = (probs * (dprobs - delta)).astype(jnp.bfloat16)
        dquery = jnp.dot(dscores, keys, preferred_element_type=jnp.float32) * scale
        dkeys = dkeys + jnp.dot(dscores.T, query_rows, preferred_element_type=jnp.float32) * scale
        dvalues = dvalues + jnp.dot(p_half.T, d_rows, preferred_element_type=jnp.float32)
        return ((dkeys, dvalues), (context, dquery.astype(jnp.bfloat16)))

    start = (jnp.zeros((key_count, width), jnp.float32), jnp.zeros((key_count, width), jnp.float32))
    (dkeys, dvalues), (context, dquery) = lax.scan(step, start, (qblocks, dblocks))
    return context.reshape(total, width), dquery.reshape(total, width), dkeys, dvalues


def per_device(frames, lengths, w_qkv, w_out, cotangent):
    width = w_out.shape[0]
    head_size = width // H
    scale = float(head_size) ** (-0.5)
    tok_rows = frames.shape[1]
    seq_count = lax.axis_size("seq")
    groups = seq_count // H
    part_rows = tok_rows // groups
    frame_total = tok_rows * seq_count
    group_index = lax.axis_index("seq") % groups
    length = lengths[0]
    inputs = frames[0].astype(jnp.float32)
    normed = layer_norm(inputs).astype(jnp.bfloat16)
    qkv = jnp.dot(normed, w_qkv, preferred_element_type=jnp.float32).astype(jnp.bfloat16)
    qkv_local = qkv.reshape(tok_rows, 3, H, head_size)
    offset = lax.axis_index("seq") * tok_rows
    own_pos = offset + jnp.arange(tok_rows, dtype=jnp.int32)
    valid = (own_pos < length).astype(jnp.float32)
    grad_rows = (cotangent[0].astype(jnp.float32) * valid[:, None]).astype(jnp.bfloat16)
    dcontext = jnp.dot(grad_rows, w_out.T, preferred_element_type=jnp.float32).astype(jnp.bfloat16)

    qd = jnp.stack([qkv_local[:, 0], dcontext.reshape(tok_rows, H, head_size)], axis=1)
    qd_send = (
        qd.reshape(groups, part_rows, 2, H, head_size)
        .transpose(3, 0, 1, 2, 4)
        .reshape(seq_count, part_rows, 2, head_size)
    )
    paired = qkv_local[:, 1:].transpose(2, 0, 1, 3)
    paired_send = jnp.broadcast_to(paired[:, None], (H, groups, tok_rows, 2, head_size))
    paired_send = paired_send.reshape(seq_count, tok_rows, 2, head_size)
    qd_recv = lax.all_to_all(qd_send, "seq", split_axis=0, concat_axis=0, tiled=True)
    paired_recv = lax.all_to_all(paired_send, "seq", split_axis=0, concat_axis=0, tiled=True)
    queries = qd_recv[:, :, 0].reshape(seq_count * part_rows, head_size)
    dcontext_heads = qd_recv[:, :, 1].reshape(seq_count * part_rows, head_size)
    keys = paired_recv[:, :, 0].reshape(frame_total, head_size)
    values = paired_recv[:, :, 1].reshape(frame_total, head_size)
    position = jnp.arange(frame_total, dtype=jnp.int32)
    bias = jnp.where(position < length, 0.0, -1000000000.0).astype(jnp.float32)

    context_h, dquery, dkeys, dvalues = head_pass(queries, keys, values, dcontext_heads, bias, scale)

    context_back = lax.all_to_all(
        context_h.reshape(seq_count, part_rows, head_size), "seq", split_axis=0, concat_axis=0, tiled=True
    )
    context = (
        context_back.reshape(H, groups, part_rows, head_size).transpose(1, 2, 0, 3).reshape(tok_rows, width)
    )
    branch = jnp.dot(context, w_out, preferred_element_type=jnp.float32)
    output = (inputs + valid[:, None] * branch).astype(jnp.bfloat16)
    out_share = lax.psum_scatter(
        jnp.dot(context.T, grad_rows, preferred_element_type=jnp.float32),
        "seq",
        scatter_dimension=0,
        tiled=True,
    )

    split_grads = jnp.stack([dkeys, dvalues], axis=1).reshape(seq_count, groups, part_rows, 2, head_size)
    own_half = lax.dynamic_index_in_dim(split_grads, group_index, 1, keepdims=False)
    other_half = lax.dynamic_index_in_dim(split_grads, 1 - group_index, 1, keepdims=False)
    partner_half = from_partner(other_half, "seq", 0)
    paired_rows = (own_half + partner_half).astype(jnp.bfloat16)
    dtrio = jnp.concatenate([dquery.reshape(seq_count, part_rows, 1, head_size), paired_rows], axis=2)
    returned_grads = lax.all_to_all(dtrio, "seq", split_axis=0, concat_axis=0, tiled=True)
    dqkv = returned_grads.reshape(H, groups, part_rows, 3, head_size)
    dqkv = dqkv.transpose(1, 2, 3, 0, 4).reshape(tok_rows, 3 * width)
    qkv_share = lax.psum_scatter(
        jnp.dot(normed.T, dqkv, preferred_element_type=jnp.float32),
        "seq",
        scatter_dimension=0,
        tiled=True,
    )
    grad_qkv, grad_out = lax.psum((qkv_share, out_share), "batch")
    dnormed = jnp.dot(dqkv, w_qkv.T, preferred_element_type=jnp.float32)
    unused, pull = jax.vjp(layer_norm, inputs)
    grad_input = (cotangent[0].astype(jnp.float32) + pull(dnormed)[0]).astype(jnp.bfloat16)
    return (output[None], grad_input[None], grad_qkv, grad_out)


def solution(mesh):
    return jax.shard_map(
        per_device,
        mesh=mesh,
        in_specs=(P("batch", "seq", None), P("batch"), P(), P(), P("batch", "seq", None)),
        out_specs=(
            P("batch", "seq", None),
            P("batch", "seq", None),
            P("seq", None),
            P("seq", None),
        ),
        check_vma=False,
    )
```

time: 487 us -> 413 us (0.85)
  waiting for transfers between devices: 273 us -> 230 us
  matrix products: 91.3 us -> 72.2 us
  blocking collectives: 21.5 us -> 29.6 us
  starting transfers between devices: 21.3 us -> 13.3 us
  other arithmetic: 33.6 us -> 25.9 us
    all_gather x2 -> x0, waiting for transfers between devices: 69.1 us -> none  [the longest x1 35.6 us: per_device(): value_piece = lax.all_gather(qkv_local[:, 2], 'seq', axis=0, tiled=True)]
    dot_general x7 -> x8, matrix products: 36.4 us -> 19.6 us  [the longest x1 7.73 us: per_device(): jnp.dot(normed.T, dqkv, preferred_element_type=jnp.float32)]
    all_to_all x0 -> x1, blocking collectives: none -> 13.1 us  [per_device(): lax.all_to_all(context_h.reshape(seq_count, part_rows, head_size), 'seq',...]
    all_to_all x2 -> x1, waiting for transfers between devices: 0.01 us -> 12.5 us  [per_device(): lax.all_to_all(qd_send, 'seq', split_axis=0, concat_axis=0, tiled=True)]
    ppermute x1, waiting for transfers between devices: 35.7 us -> 46.2 us  [from_partner(): lax.ppermute(array, axis, [(i, i ^ 1 << stride) for i in range(lax.axis_s...]
    reduce_sum x4 -> x3, other arithmetic: 14.4 us -> 4.02 us  [step(): probs = expo / jnp.sum(expo, axis=1, keepdims=True)]
    dot_general x3, matrix products: 18.6 us -> 10.8 us  [step(): jnp.dot(p_half.T, d_rows, preferred_element_type=jnp.float32)]
    reduce_scatter x2, waiting for transfers between devices: 87.9 us -> 94.2 us  [the longest x1 94.1 us: per_device(): lax.psum_scatter(jnp.dot(normed.T, dqkv, preferred_element_type=jnp.float...]
  transfers between devices with their start and end apart: 9 -> 6, of which waited for: 6 -> 5; matrix products, arithmetic and copies ran while one was open for 27% -> 7% of each run, Pallas kernels for 0% -> 0%
where the time goes in v1:
time: 413 us; the launch traced here: 411 us
  waiting for transfers between devices  230 us (56%)
  matrix products  72.2 us (17%)
  blocking collectives  29.6 us (7%)
  other arithmetic  25.9 us (6%)
  local copies, waits for them, and re-layouts  24.9 us (6%)
  between operations  14.7 us (4%)
  starting transfers between devices  13.3 us (3%)
    reduce_scatter x1, waiting for transfers between devices, per_device(): lax.psum_scatter(jnp.dot(normed.T, dqkv, preferred_element_type=jnp.float...  94.1 us
    psum x1, waiting for transfers between devices, per_device(): grad_qkv, grad_out = lax.psum((qkv_share, out_share), 'batch')  58.8 us
    ppermute x1, waiting for transfers between devices, from_partner(): lax.ppermute(array, axis, [(i, i ^ 1 << stride) for i in range(lax.axis_s...  46.2 us
    all_to_all x1, waiting for transfers between devices, per_device(): lax.all_to_all(paired_send, 'seq', split_axis=0, concat_axis=0, tiled=True)  18 us
    all_to_all x1, blocking collectives, per_device(): lax.all_to_all(dtrio, 'seq', split_axis=0, concat_axis=0, tiled=True)  16.5 us
    dot_general x3, matrix products, step(): jnp.dot(dscores.T, query_rows, preferred_element_type=jnp.float32) * scale  13.6 us
    all_to_all x1, blocking collectives, per_device(): lax.all_to_all(context_h.reshape(seq_count, part_rows, head_size), 'seq',...  13.1 us
    all_to_all x1, waiting for transfers between devices, per_device(): lax.all_to_all(qd_send, 'seq', split_axis=0, concat_axis=0, tiled=True)  12.5 us
  transfers between devices with their start and end apart: 6, of which 5 were waited for; matrix products, arithmetic and copies ran while one was open for 7% of the time, Pallas kernels for 0%

profile of v1, /device:TPU:1, one launch (start us, length us, event | category | flops | bytes accessed | tf_op | source)
XLA Modules:
  0.0 410.5 jit_solution(17482741365465413994)
XLA Ops:
  7.2 1.3 convert_reduce_fusion
  8.5 1.2 fusion.55
  9.7 0.6 copy-done.14
  10.3 4.4 %fusion.40 = bf16[24,8,24,128]{3,1,2,0:T(8,128)(2,1)S(1)} fusion(bf16[1024,3072]{1,0:T(8,128)(2,1)} %param.9, bf16[1,192,1024]{2,1,0:T(8,128)(2,1)} %param.7, f32[192]{0:T(256)S(1)} %fusion.79, f32[192]{0:T(256)S(1)} %broadcast_multiply_fusion), kind=kOutput, calls=%fused_computation.48 | convolution fusion | flops 1209335808 | bytes 7865856 | tf_op jit(solution)/shard_map/dot_general | solution.py:62
  15.0 0.8 copy.20
  16.5 1.9 fusion.44
  18.5 1.0 pad_maximum_fusion.1
  19.5 8.5 %all-to-all-start = ((bf16[16,96,2,128]{3,1,2,0:T(8,128)(2,1)}), bf16[16,96,2,128]{3,1,2,0:T(8,128)(2,1)}, u32[]{:S(2)}, u32[]{:S(2)}) async-start(bf16[16,96,2,128]{3,1,2,0:T(8,128)(2,1)} %bitcast.168), calls=%async_computation | async-start | bytes 1572864 | tf_op jit(solution)/shard_map/all_to_all | solution.py:79
  28.3 12.5 %all-to-all-done = bf16[16,96,2,128]{3,1,2,0:T(8,128)(2,1)} async-done(((bf16[16,96,2,128]{3,1,2,0:T(8,128)(2,1)}), bf16[16,96,2,128]{3,1,2,0:T(8,128)(2,1)}, u32[]{:S(2)}, u32[]{:S(2)}) %all-to-all-start) | async-done | bytes 786464 | tf_op jit(solution)/shard_map/all_to_all | solution.py:79
  40.8 1.6 broadcast_in_dim.43
  42.4 4.4 %all-to-all-start.1 = ((bf16[16,192,2,128]{3,1,2,0:T(8,128)(2,1)}), bf16[16,192,2,128]{3,1,2,0:T(8,128)(2,1)}, u32[]{:S(2)}, u32[]{:S(2)}) async-start(bf16[16,192,2,128]{3,1,2,0:T(8,128)(2,1)} %bitcast.164), calls=%async_computation.1 | async-start | bytes 3145728 | tf_op jit(solution)/shard_map/all_to_all | solution.py:80
  46.8 0.2 reduce-scatter.5.cloned.1.call-start
  47.1 2.0 fusion.83
  49.0 18.0 %all-to-all-done.1 = bf16[16,192,2,128]{3,1,2,0:T(8,128)(2,1)} async-done(((bf16[16,192,2,128]{3,1,2,0:T(8,128)(2,1)}), bf16[16,192,2,128]{3,1,2,0:T(8,128)(2,1)}, u32[]{:S(2)}, u32[]{:S(2)}) %all-to-all-start.1) | async-done | bytes 1572896 | tf_op jit(solution)/shard_map/all_to_all | solution.py:80
  67.1 2.4 fusion.82
  69.4 71.6 %while.17 = (s32[]{:T(128)}, f32[3072,128]{1,0:T(8,128)}, f32[3072,128]{1,0:T(8,128)}, bf16[3,512,128]{2,1,0:T(8,128)(2,1)}, bf16[3,512,128]{2,1,0:T(8,128)(2,1)...) while((s32[]{:T(128)}, f32[3072,128]{1,0:T(8,128)}, ...), condition=%wide.region_6.7_spmd.clone, body=%wide.region_2.6_spmd.clone.sunk | while | flops 2446397952 | bytes 139264304 | solution.py:45
  69.4 0.6 fusion.122
  70.1 1.1 fusion.123
  71.2 1.3 fusion.124
  72.5 3.2 multiply_reduce_fusion.2
  75.8 2.6 copy-done.1
  78.4 3.4 multiply_convert_fusion.2
  81.9 4.2 %fusion.125 = f32[3072,128]{1,0:T(8,128)} fusion(bf16[512,3072]{1,0:T(8,128)(2,1)} %multiply_convert_fusion.2, f32[3072,128]{1,0:T(8,128)} %get-tuple-element.218, pred[]{:T(512)S(6)} %compare.4, bf16[3,512,128]{2,1,0:T(8,128)(2,1)S(1)} %get-tuple-element.234, s32[]{:T(128)} %get-tuple-element.217), kind=kOutput, calls=%fused_computation.10.clone.1 | convolution fusion | flops 403832832 | bytes 6422533 | tf_op jit(solution)/shard_map/while/body/eval_jaxpr/dot_general | solution.py:40
  86.1 1.6 fusion.127
  87.7 3.2 convolution_add_fusion.2
  91.0 1.6 fusion.126
  92.6 0.6 fusion.122
  93.2 1.1 fusion.123
  94.3 1.3 fusion.124
  95.7 3.2 multiply_reduce_fusion.2
  98.9 2.6 copy-done.1
  101.6 3.4 multiply_convert_fusion.2
  105.0 4.7 %fusion.125 = f32[3072,128]{1,0:T(8,128)} fusion(bf16[512,3072]{1,0:T(8,128)(2,1)} %multiply_convert_fusion.2, f32[3072,128]{1,0:T(8,128)} %get-tuple-element.218, pred[]{:T(512)S(6)} %compare.4, bf16[3,512,128]{2,1,0:T(8,128)(2,1)S(1)} %get-tuple-element.234, s32[]{:T(128)} %get-tuple-element.217), kind=kOutput, calls=%fused_computation.10.clone.1 | convolution fusion | flops 403832832 | bytes 6422533 | tf_op jit(solution)/shard_map/while/body/eval_jaxpr/dot_general | solution.py:40
  109.7 1.6 fusion.127
  111.4 3.8 convolution_add_fusion.2
  115.2 1.6 fusion.126
  116.8 0.6 fusion.122
  117.4 1.1 fusion.123
  118.5 1.3 fusion.124
  119.9 3.2 multiply_reduce_fusion.2
  123.1 2.6 copy-done.1
  125.8 3.4 multiply_convert_fusion.2
  129.2 4.7 %fusion.125 = f32[3072,128]{1,0:T(8,128)} fusion(bf16[512,3072]{1,0:T(8,128)(2,1)} %multiply_convert_fusion.2, f32[3072,128]{1,0:T(8,128)} %get-tuple-element.218, pred[]{:T(512)S(6)} %compare.4, bf16[3,512,128]{2,1,0:T(8,128)(2,1)S(1)} %get-tuple-element.234, s32[]{:T(128)} %get-tuple-element.217), kind=kOutput, calls=%fused_computation.10.clone.1 | convolution fusion | flops 403832832 | bytes 6422533 | tf_op jit(solution)/shard_map/while/body/eval_jaxpr/dot_general | solution.py:40
  133.9 1.6 fusion.127
  135.6 3.8 convolution_add_fusion.2
  139.3 1.6 fusion.126
  141.0 13.1 %all_to_all.20 = bf16[16,96,128]{2,1,0:T(8,128)(2,1)S(1)} all-to-all(bf16[16,96,128]{2,1,0:T(8,128)(2,1)} %bitcast.12), channel_id=1, replica_groups=mesh['batch'=8,'seq'=16] {'seq'}, dimensions={0} | all-to-all | bytes 786432 | tf_op jit(solution)/shard_map/all_to_all | solution.py:90
  154.1 0.3 copy.23
  154.4 3.7 fusion.65
  158.2 2.1 fusion.37
  160.5 46.2 %collective-permute-done = f32[16,96,2,128]{3,1,2,0:T(8,128)S(1)} collective-permute-done((f32[16,96,2,128]{3,1,2,0:T(8,128)S(1)}, f32[16,96,2,128]{3,1,2,0:T(8,128)S(1)}, u32[]{:S(2)}, u32[]{:S(2)}) %collective-permute-start) | collective-permute-done | bytes 1572896 | tf_op jit(solution)/shard_map/ppermute | solution.py:10
  206.7 0.3 fusion.39
  207.1 16.5 %all_to_all.21 = bf16[16,96,3,128]{3,1,2,0:T(8,128)(2,1)S(1)} all-to-all(bf16[16,96,3,128]{3,1,2,0:T(8,128)(2,1)S(1)} %pad_maximum_fusion), channel_id=1, replica_groups=mesh['batch'=8,'seq'=16] {'seq'}, dimensions={0} | all-to-all | bytes 2359296 | tf_op jit(solution)/shard_map/all_to_all | solution.py:111
  223.6 1.8 copy.26
  225.4 3.0 reshape.105
  228.4 7.7 %fusion.61 = f32[1024,3072]{1,0:T(8,128)} fusion(bf16[192,3072]{1,0:T(8,128)(2,1)} %reshape.105, bf16[1,192,1024]{2,1,0:T(8,128)(2,1)S(1)} %copy-done.5, f32[192]{0:T(256)S(1)} %copy-done.13, f32[192]{0:T(256)S(1)} %copy-done.11), kind=kOutput, calls=%fused_computation.80 | convolution fusion | flops 1208745984 | bytes 14157312 | tf_op jit(solution)/shard_map/dot_general | solution.py:115
  236.2 1.3 fusion.43
  237.6 5.9 %fusion.57 = (f32[192]{0:T(256)S(1)}, f32[192,1024]{1,0:T(8,128)}) fusion(bf16[1,192,1024]{2,1,0:T(8,128)(2,1)S(1)} %copy-done.5, f32[192]{0:T(256)S(1)} %copy-done.11, bf16[192,3072]{1,0:T(8,128)(2,1)S(1)} %copy-done.6, bf16[1024,3072]{1,0:T(8,128)(2,1)} %param.9), kind=kOutput, calls=%fused_computation.74 | convolution fusion | flops 1208745728 | bytes 8652288 | tf_op jit(solution)/shard_map/dot_general | solution.py:121
  243.5 94.1 %reduce-scatter.3.cloned.1.call-done = f32[64,3072]{1,0:T(8,128)} async-done(((f32[1024,3072]{1,0:T(8,128)}), f32[64,3072]{1,0:T(8,128)}) %reduce-scatter.3.cloned.1.call-update) | async-done | bytes 786448 | tf_op jit(solution)/shard_map/reduce_scatter | solution.py:114
  337.7 1.5 fusion.80
  339.2 2.2 fusion.67
  341.4 58.8 %all-reduce.3.cloned.1.call-done = (f32[64,3072]{1,0:T(8,128)}, f32[64,1024]{1,0:T(8,128)}) async-done(((f32[64,3072]{1,0:T(8,128)}, f32[64,1024]{1,0:T(8,128)}), (f32[64,3072]{1,0:T(8,128)}, f32[64,1024]{1,0:T(8,128)})) %all-reduce.3.cloned.1.call-update) | async-done | bytes 1048592 | tf_op jit(solution)/shard_map/psum | solution.py:120
  400.3 2.1 copy.68
  402.3 1.7 copy.69
  (83 shorter events, 1.4 us)
Async XLA Ops:
  7.2 9.3 %copy-start = (bf16[1024,1024]{1,0:T(8,128)(2,1)S(1)}, bf16[1024,1024]{1,0:T(8,128)(2,1)}, u32[]{:S(2)}) copy-start(bf16[1024,1024]{1,0:T(8,128)(2,1)} %param.10) | copy-start | bytes 6291460
  8.5 6.3 %copy-start.10 = (f32[192]{0:T(256)}, f32[192]{0:T(256)S(1)}, u32[]{:S(2)}) copy-start(f32[192]{0:T(256)S(1)} %broadcast_multiply_fusion) | copy-start | bytes 2308
  9.7 0.6 copy-start.14
  10.3 4.4 %copy-start.12 = (f32[192]{0:T(256)}, f32[192]{0:T(256)S(1)}, u32[]{:S(2)}) copy-start(f32[192]{0:T(256)S(1)} %fusion.79) | copy-start | bytes 2308
  16.5 2.1 copy-start.8
  19.5 21.3 %all-to-all-start = ((bf16[16,96,2,128]{3,1,2,0:T(8,128)(2,1)}), bf16[16,96,2,128]{3,1,2,0:T(8,128)(2,1)}, u32[]{:S(2)}, u32[]{:S(2)}) async-start(bf16[16,96,2,128]{3,1,2,0:T(8,128)(2,1)} %bitcast.168), calls=%async_computation | async-start | bytes 1572864 | tf_op jit(solution)/shard_map/all_to_all | solution.py:79
  42.4 24.6 %all-to-all-start.1 = ((bf16[16,192,2,128]{3,1,2,0:T(8,128)(2,1)}), bf16[16,192,2,128]{3,1,2,0:T(8,128)(2,1)}, u32[]{:S(2)}, u32[]{:S(2)}) async-start(bf16[16,192,2,128]{3,1,2,0:T(8,128)(2,1)} %bitcast.164), calls=%async_computation.1 | async-start | bytes 3145728 | tf_op jit(solution)/shard_map/all_to_all | solution.py:80
  46.8 196.7 %reduce-scatter.5.cloned.1.call-start = ((), (), s32[]{:S(2)}) async-start(), calls=%async_computation.7 | async-start | bytes 4456448 | tf_op jit(solution)/shard_map/reduce_scatter | solution.py:98
  71.1 1.4 copy-start.3
  75.8 2.6 copy-start.1
  81.8 5.9 %slice-start = ((s8[6291456]{0:T(1024)(128)(4,1)}), s8[4194304]{0:T(1024)(128)(4,1)S(1)}, s32[]{:S(2)}) async-start(s8[6291456]{0:T(1024)(128)(4,1)} %bitcast.158), calls=%async_computation.9 | async-start | bytes 8388608 | tf_op jit(solution)/shard_map/while
  81.8 4.2 %copy-start.2 = (bf16[512,3072]{1,0:T(8,128)(2,1)S(1)}, bf16[512,3072]{1,0:T(8,128)(2,1)}, u32[]{:S(2)}) copy-start(bf16[512,3072]{1,0:T(8,128)(2,1)} %multiply_convert_fusion.2) | copy-start | bytes 9437188 | tf_op jit(solution)/shard_map/while
  81.9 5.9 %slice-start.1 = ((s8[6291456]{0:T(1024)(128)(4,1)}), s8[2097152]{0:T(1024)(128)(4,1)S(1)}, s32[]{:S(2)}) async-start(s8[6291456]{0:T(1024)(128)(4,1)} %bitcast.158), calls=%async_computation.10 | async-start | bytes 4194304 | tf_op jit(solution)/shard_map/while
  87.7 3.2 copy-start.4
  94.3 1.4 copy-start.3
  98.9 2.6 copy-start.1
  105.0 6.3 %slice-start = ((s8[6291456]{0:T(1024)(128)(4,1)}), s8[4194304]{0:T(1024)(128)(4,1)S(1)}, s32[]{:S(2)}) async-start(s8[6291456]{0:T(1024)(128)(4,1)} %bitcast.158), calls=%async_computation.9 | async-start | bytes 8388608 | tf_op jit(solution)/shard_map/while
  105.0 4.7 %copy-start.2 = (bf16[512,3072]{1,0:T(8,128)(2,1)S(1)}, bf16[512,3072]{1,0:T(8,128)(2,1)}, u32[]{:S(2)}) copy-start(bf16[512,3072]{1,0:T(8,128)(2,1)} %multiply_convert_fusion.2) | copy-start | bytes 9437188 | tf_op jit(solution)/shard_map/while
  105.0 6.3 %slice-start.1 = ((s8[6291456]{0:T(1024)(128)(4,1)}), s8[2097152]{0:T(1024)(128)(4,1)S(1)}, s32[]{:S(2)}) async-start(s8[6291456]{0:T(1024)(128)(4,1)} %bitcast.158), calls=%async_computation.10 | async-start | bytes 4194304 | tf_op jit(solution)/shard_map/while
  111.4 3.8 copy-start.4
  118.5 1.4 copy-start.3
  123.1 2.6 copy-start.1
  129.2 6.3 %slice-start = ((s8[6291456]{0:T(1024)(128)(4,1)}), s8[4194304]{0:T(1024)(128)(4,1)S(1)}, s32[]{:S(2)}) async-start(s8[6291456]{0:T(1024)(128)(4,1)} %bitcast.158), calls=%async_computation.9 | async-start | bytes 8388608 | tf_op jit(solution)/shard_map/while
  129.2 4.7 %copy-start.2 = (bf16[512,3072]{1,0:T(8,128)(2,1)S(1)}, bf16[512,3072]{1,0:T(8,128)(2,1)}, u32[]{:S(2)}) copy-start(bf16[512,3072]{1,0:T(8,128)(2,1)} %multiply_convert_fusion.2) | copy-start | bytes 9437188 | tf_op jit(solution)/shard_map/while
  129.2 6.3 %slice-start.1 = ((s8[6291456]{0:T(1024)(128)(4,1)}), s8[2097152]{0:T(1024)(128)(4,1)S(1)}, s32[]{:S(2)}) async-start(s8[6291456]{0:T(1024)(128)(4,1)} %bitcast.158), calls=%async_computation.10 | async-start | bytes 4194304 | tf_op jit(solution)/shard_map/while
  135.6 3.8 copy-start.4
  158.1 179.6 %reduce-scatter.3.cloned.1.call-start = ((), (), s32[]{:S(2)}) async-start(), calls=%async_computation.6 | async-start | bytes 13369344 | tf_op jit(solution)/shard_map/reduce_scatter | solution.py:114
  160.4 46.6 %copy-start.9 = (bf16[3,512,128]{2,1,0:T(8,128)(2,1)S(1)}, bf16[3,512,128]{2,1,0:T(8,128)(2,1)}, u32[]{:S(2)}) copy-start(bf16[3,512,128]{2,1,0:T(8,128)(2,1)} %get-tuple-element.60) | copy-start | bytes 1179652
  160.4 46.3 %collective-permute-start = (f32[16,96,2,128]{3,1,2,0:T(8,128)S(1)}, f32[16,96,2,128]{3,1,2,0:T(8,128)S(1)}, u32[]{:S(2)}, u32[]{:S(2)}) collective-permute-start(f32[16,96,2,128]{3,1,2,0:T(8,128)S(1)} %bitcast.170), channel_id=1, source_target_pairs={{0,1},{1,0},{2,3},{3,2},{4,5},{5,4},{6,7},{7,6},{8,9},{9,8},{10,11... | collective-permute-start | bytes 4718600 | tf_op jit(solution)/shard_map/ppermute | solution.py:10
  223.6 4.8 %copy-start.5 = (bf16[1,192,1024]{2,1,0:T(8,128)(2,1)S(1)}, bf16[1,192,1024]{2,1,0:T(8,128)(2,1)}, u32[]{:S(2)}) copy-start(bf16[1,192,1024]{2,1,0:T(8,128)(2,1)} %param.7) | copy-start | bytes 1179652
  223.6 4.8 %copy-start.11 = (f32[192]{0:T(256)S(1)}, f32[192]{0:T(256)}, u32[]{:S(2)}) copy-start(f32[192]{0:T(256)} %copy-done.10) | copy-start | bytes 2308
  223.6 4.8 %copy-start.13 = (f32[192]{0:T(256)S(1)}, f32[192]{0:T(256)}, u32[]{:S(2)}) copy-start(f32[192]{0:T(256)} %copy-done.12) | copy-start | bytes 2308
  236.2 164.1 %all-reduce.3.cloned.1.call-start = ((), (), s32[]{:S(2)}) async-start(), calls=%async_computation.8 | async-start | bytes 2097152 | tf_op jit(solution)/shard_map/psum | solution.py:120
  236.2 1.4 copy-start.6
  237.6 5.9 %copy-start.15 = (f32[192]{0:T(256)S(1)}, f32[192]{0:T(256)}, u32[]{:S(2)}) copy-start(f32[192]{0:T(256)} %copy-done.14) | copy-start | bytes 2308
  243.5 95.7 %copy-start.7 = (bf16[1,192,1024]{2,1,0:T(8,128)(2,1)S(1)}, bf16[1,192,1024]{2,1,0:T(8,128)(2,1)}, u32[]{:S(2)}) copy-start(bf16[1,192,1024]{2,1,0:T(8,128)(2,1)} %param.11) | copy-start | bytes 1179652
Sparse Core Ops, SparseCore 0:
  158.2 80.5 reduce-scatter.4
  242.3 95.3 reduce-scatter.2
  340.1 60.1 all-reduce.2

commit v2 on v1

--- a/solution.py
+++ b/solution.py
@@ -2,6 +2,9 @@
 import jax.numpy as jnp
 from jax import lax
 from jax.sharding import PartitionSpec as P
+from jax.experimental import pallas as pl
+from jax.experimental.pallas import tpu as pltpu
+import functools
 
 H = 8
 
@@ -17,33 +20,64 @@
     return centred * lax.rsqrt(var + 1e-05)
 
 
-def head_pass(query, keys, values, dcontext, bias, scale):
-    total, width = query.shape
-    rows = min(512, total)
-    qblocks = query.reshape(total // rows, rows, width)
-    dblocks = dcontext.reshape(total // rows, rows, width)
-    key_count = keys.shape[0]
+def _attn_kernel(q_ref, do_ref, k_ref, v_ref, bias_ref, ctx_ref, dq_ref, dk_ref, dv_ref, *, scale):
+    i = pl.program_id(0)
 
-    def step(carry, item):
-        dkeys, dvalues = carry
-        query_rows, d_rows = item
-        scores = jnp.dot(query_rows, keys.T, preferred_element_type=jnp.float32) * scale + bias[None, :]
-        top = jnp.max(scores, axis=1, keepdims=True)
-        expo = jnp.exp(scores - top)
-        probs = expo / jnp.sum(expo, axis=1, keepdims=True)
-        p_half = probs.astype(jnp.bfloat16)
-        context = jnp.dot(p_half, values, preferred_element_type=jnp.float32).astype(jnp.bfloat16)
-        dprobs = jnp.dot(d_rows, values.T, preferred_element_type=jnp.float32)
-        delta = jnp.sum(probs * dprobs, axis=1, keepdims=True)
-        dscores = (probs * (dprobs - delta)).astype(jnp.bfloat16)
-        dquery = jnp.dot(dscores, keys, preferred_element_type=jnp.float32) * scale
-        dkeys = dkeys + jnp.dot(dscores.T, query_rows, preferred_element_type=jnp.float32) * scale
-        dvalues = dvalues + jnp.dot(p_half.T, d_rows, preferred_element_type=jnp.float32)
-        return ((dkeys, dvalues), (context, dquery.astype(jnp.bfloat16)))
+    @pl.when(i == 0)
+    def _():
+        dk_ref[...] = jnp.zeros_like(dk_ref)
+        dv_ref[...] = jnp.zeros_like(dv_ref)
 
-    start = (jnp.zeros((key_count, width), jnp.float32), jnp.zeros((key_count, width), jnp.float32))
-    (dkeys, dvalues), (context, dquery) = lax.scan(step, start, (qblocks, dblocks))
-    return context.reshape(total, width), dquery.reshape(total, width), dkeys, dvalues
+    q = q_ref[...]
+    do = do_ref[...]
+    k = k_ref[...]
+    v = v_ref[...]
+    nt = (((1,), (1,)), ((), ()))
+    tn = (((0,), (0,)), ((), ()))
+    s = lax.dot_general(q, k, nt, preferred_element_type=jnp.float32) * scale + bias_ref[...]
+    m = jnp.max(s, axis=1, keepdims=True)
+    e = jnp.exp(s - m)
+    p = e / jnp.sum(e, axis=1, keepdims=True)
+    p16 = p.astype(jnp.bfloat16)
+    ctx_ref[...] = jnp.dot(p16, v, preferred_element_type=jnp.float32).astype(ctx_ref.dtype)
+    dp = lax.dot_general(do, v, nt, preferred_element_type=jnp.float32)
+    delta = jnp.sum(p * dp, axis=1, keepdims=True)
+    ds = (p * (dp - delta)).astype(jnp.bfloat16)
+    dq_ref[...] = (jnp.dot(ds, k, preferred_element_type=jnp.float32) * scale).astype(dq_ref.dtype)
+    dk_ref[...] += lax.dot_general(ds, q, tn, preferred_element_type=jnp.float32) * scale
+    dv_ref[...] += lax.dot_general(p16, do, tn, preferred_element_type=jnp.float32)
+
+
+def attn_pass(query, keys, values, dcontext, bias, scale, block=256, interpret=False):
+    nq, hd = query.shape
+    nk = keys.shape[0]
+    grid = (nq // block,)
+    kernel = functools.partial(_attn_kernel, scale=scale)
+    return pl.pallas_call(
+        kernel,
+        grid=grid,
+        in_specs=[
+            pl.BlockSpec((block, hd), lambda i: (i, 0)),
+            pl.BlockSpec((block, hd), lambda i: (i, 0)),
+            pl.BlockSpec((nk, hd), lambda i: (0, 0)),
+            pl.BlockSpec((nk, hd), lambda i: (0, 0)),
+            pl.BlockSpec((1, nk), lambda i: (0, 0)),
+        ],
+        out_specs=[
+            pl.BlockSpec((block, hd), lambda i: (i, 0)),
+            pl.BlockSpec((block, hd), lambda i: (i, 0)),
+            pl.BlockSpec((nk, hd), lambda i: (0, 0)),
+            pl.BlockSpec((nk, hd), lambda i: (0, 0)),
+        ],
+        out_shape=[
+            jax.ShapeDtypeStruct((nq, hd), jnp.bfloat16),
+            jax.ShapeDtypeStruct((nq, hd), jnp.bfloat16),
+            jax.ShapeDtypeStruct((nk, hd), jnp.float32),
+            jax.ShapeDtypeStruct((nk, hd), jnp.float32),
+        ],
+        compiler_params=pltpu.CompilerParams(dimension_semantics=("arbitrary",)),
+        interpret=interpret,
+    )(query, dcontext, keys, values, bias.reshape(1, nk))
 
 
 def per_device(frames, lengths, w_qkv, w_out, cotangent):
@@ -85,7 +119,7 @@
     position = jnp.arange(frame_total, dtype=jnp.int32)
     bias = jnp.where(position < length, 0.0, -1000000000.0).astype(jnp.float32)
 
-    context_h, dquery, dkeys, dvalues = head_pass(queries, keys, values, dcontext_heads, bias, scale)
+    context_h, dquery, dkeys, dvalues = attn_pass(queries, keys, values, dcontext_heads, bias, scale)
 
     context_back = lax.all_to_all(
         context_h.reshape(seq_count, part_rows, head_size), "seq", split_axis=0, concat_axis=0, tiled=True

time: 413 us -> 365 us (0.88)
  matrix products: 72.2 us -> 23.9 us
  Pallas kernels: 0 us -> 24.9 us
  other arithmetic: 25.9 us -> 8.16 us
  local copies, waits for them, and re-layouts: 24.9 us -> 18.7 us
    dot_general x18 -> x0, matrix products: 47.2 us -> none  [the longest x3 13.6 us: step(): jnp.dot(dscores.T, query_rows, preferred_element_type=jnp.float32) * scale]
    pallas_call x0 -> x1, Pallas kernels: none -> 24.9 us  [attn_pass(): pl.pallas_call(kernel, grid=grid, in_specs=[pl.BlockSpec((block, hd), lam...]
    convert_element_type x3 -> x0, other arithmetic: 10.3 us -> none  [step(): dscores = (probs * (dprobs - delta)).astype(jnp.bfloat16)]
    while x36 -> x0, local copies, waits for them, and re-layouts: 7.97 us -> none
  transfers between devices with their start and end apart: 6 -> 6, of which waited for: 5 -> 5; matrix products, arithmetic and copies ran while one was open for 7% -> 8% of each run, Pallas kernels for 0% -> 0%
where the time goes in v2:
time: 365 us; the launch traced here: 363 us
  waiting for transfers between devices  229 us (63%)
  blocking collectives  29.7 us (8%)
  Pallas kernels  24.9 us (7%)
  matrix products  23.9 us (7%)
  local copies, waits for them, and re-layouts  18.7 us (5%)
  between operations  14.8 us (4%)
  starting transfers between devices  13.1 us (4%)
  other arithmetic  8.16 us (2%)
    reduce_scatter x1, waiting for transfers between devices, per_device(): lax.psum_scatter(jnp.dot(normed.T, dqkv, preferred_element_type=jnp.float...  94.2 us
    psum x1, waiting for transfers between devices, per_device(): grad_qkv, grad_out = lax.psum((qkv_share, out_share), 'batch')  59.9 us
    ppermute x1, waiting for transfers between devices, from_partner(): lax.ppermute(array, axis, [(i, i ^ 1 << stride) for i in range(lax.axis_s...  46.2 us
    pallas_call x1, Pallas kernels, attn_pass(): pl.pallas_call(kernel, grid=grid, in_specs=[pl.BlockSpec((block, hd), lam...  24.9 us
    all_to_all x1, waiting for transfers between devices, per_device(): lax.all_to_all(paired_send, 'seq', split_axis=0, concat_axis=0, tiled=True)  18.6 us
    all_to_all x1, blocking collectives, per_device(): lax.all_to_all(dtrio, 'seq', split_axis=0, concat_axis=0, tiled=True)  16.5 us
    all_to_all x1, blocking collectives, per_device(): lax.all_to_all(context_h.reshape(seq_count, part_rows, head_size), 'seq',...  13.1 us
    all_to_all x1, waiting for transfers between devices, per_device(): lax.all_to_all(qd_send, 'seq', split_axis=0, concat_axis=0, tiled=True)  10.4 us
  transfers between devices with their start and end apart: 6, of which 5 were waited for; matrix products, arithmetic and copies ran while one was open for 8% of the time, Pallas kernels for 0%

profile of v2, /device:TPU:1, one launch (start us, length us, event | category | flops | bytes accessed | tf_op | source)
XLA Modules:
  0.0 362.6 jit_solution(191461625527491265)
XLA Ops:
  7.2 0.0 copy-start
  8.0 1.1 convert_reduce_fusion
  9.1 1.2 fusion.18
  10.4 0.0 copy-done
  10.4 0.0 copy-start.1
  10.4 1.9 fusion.7
  12.3 0.1 copy.28
  12.4 0.0 copy-done.1
  12.4 4.3 %fusion.3 = bf16[24,8,24,128]{3,1,2,0:T(8,128)(2,1)S(1)} fusion(bf16[1024,3072]{1,0:T(8,128)(2,1)} %param.7, bf16[1,192,1024]{2,1,0:T(8,128)(2,1)S(1)} %copy-done.1, f32[192]{0:T(256)S(1)} %fusion.42, f32[192]{0:T(256)S(1)} %broadcast_multiply_fusion), kind=kOutput, calls=%fused_computation.10 | convolution fusion | flops 1209335808 | bytes 7865856 | tf_op jit(solution)/shard_map/dot_general | solution.py:96
  16.7 0.2 copy.27
  16.9 0.0 copy-start.2
  16.9 0.1 maximum_bitcast_fusion
  17.0 1.1 copy.20
  18.2 0.0 copy-done.2
  18.2 8.4 %all-to-all-start = ((bf16[16,96,2,128]{3,1,2,0:T(8,128)(2,1)}), bf16[16,96,2,128]{3,1,2,0:T(8,128)(2,1)S(1)}, u32[]{:S(2)}, u32[]{:S(2)}) async-start(bf16[16,96,2,128]{3,1,2,0:T(8,128)(2,1)} %bitcast.111), calls=%async_computation | async-start | bytes 1572864 | tf_op jit(solution)/shard_map/all_to_all | solution.py:113
  26.6 1.3 slice_bitcast_fusion
  27.9 1.1 copy.21
  29.0 10.4 %all-to-all-done = bf16[16,96,2,128]{3,1,2,0:T(8,128)(2,1)S(1)} async-done(((bf16[16,96,2,128]{3,1,2,0:T(8,128)(2,1)}), bf16[16,96,2,128]{3,1,2,0:T(8,128)(2,1)S(1)}, u32[]{:S(2)}, u32[]{:S(2)}) %all-to-all-start) | async-done | bytes 786464 | tf_op jit(solution)/shard_map/all_to_all | solution.py:113
  39.4 2.6 broadcast_in_dim.32
  42.0 4.4 %all-to-all-start.1 = ((bf16[16,192,2,128]{3,1,2,0:T(8,128)(2,1)}), bf16[16,192,2,128]{3,1,2,0:T(8,128)(2,1)}, u32[]{:S(2)}, u32[]{:S(2)}) async-start(bf16[16,192,2,128]{3,1,2,0:T(8,128)(2,1)} %bitcast.107), calls=%async_computation.1 | async-start | bytes 3145728 | tf_op jit(solution)/shard_map/all_to_all | solution.py:114
  46.4 0.0 reduce-scatter.5.cloned.1.call-start
  46.5 0.6 compare_select_fusion.bias_ref
  47.1 0.9 fusion.45
  48.0 18.6 %all-to-all-done.1 = bf16[16,192,2,128]{3,1,2,0:T(8,128)(2,1)} async-done(((bf16[16,192,2,128]{3,1,2,0:T(8,128)(2,1)}), bf16[16,192,2,128]{3,1,2,0:T(8,128)(2,1)}, u32[]{:S(2)}, u32[]{:S(2)}) %all-to-all-start.1) | async-done | bytes 1572896 | tf_op jit(solution)/shard_map/all_to_all | solution.py:114
  66.7 2.6 fusion.44
  69.3 0.0 copy-start.4
  69.3 24.9 %shard_map.84 = (bf16[1536,128]{1,0:T(8,128)(2,1)}, bf16[1536,128]{1,0:T(8,128)(2,1)}, f32[3072,128]{1,0:T(8,128)}, f32[3072,128]{1,0:T(8,128)}) custom-call(bf16[1536,128]{1,0:T(8,128)(2,1)} %bitcast.116, bf16[1536,128]{1,0:T(8,128)(2,1)} %bitcast.115, bf16[3072,128]{1,0:T(8,128)(2,1)} %bitcast.113, bf16[3072,128]{1,0:T(8,128)(2,1)} %bitcast.112, ...), custom_call_target="tpu_custom_call" | custom-call | tf_op jit(solution)/shard_map/pallas_call | solution.py:56
  94.2 13.1 %all_to_all.20 = bf16[16,96,128]{2,1,0:T(8,128)(2,1)S(1)} all-to-all(bf16[16,96,128]{2,1,0:T(8,128)(2,1)} %bitcast.125), channel_id=1, replica_groups=mesh['batch'=8,'seq'=16] {'seq'}, dimensions={0} | all-to-all | bytes 786432 | tf_op jit(solution)/shard_map/all_to_all | solution.py:124
  107.3 0.3 copy.22
  107.6 0.0 copy-done.4
  107.6 2.7 fusion.28
  110.3 0.0 reduce-scatter.5.cloned.1.call-update
  110.3 0.0 reduce-scatter.3.cloned.1.call-start
  110.4 2.1 fusion.1
  112.5 0.1 copy.40
  112.6 0.1 collective-permute-start
  112.7 46.2 %collective-permute-done = f32[16,96,2,128]{3,1,2,0:T(8,128)S(1)} collective-permute-done((f32[16,96,2,128]{3,1,2,0:T(8,128)S(1)}, f32[16,96,2,128]{3,1,2,0:T(8,128)S(1)}, u32[]{:S(2)}, u32[]{:S(2)}) %collective-permute-start) | collective-permute-done | bytes 1572896 | tf_op jit(solution)/shard_map/ppermute | solution.py:13
  158.9 0.0 copy-start.6
  158.9 0.3 fusion.2
  159.2 0.7 copy-done.6
  159.9 0.1 pad_maximum_fusion
  160.0 16.5 %all_to_all.21 = bf16[16,96,3,128]{3,1,2,0:T(8,128)(2,1)S(1)} all-to-all(bf16[16,96,3,128]{3,1,2,0:T(8,128)(2,1)S(1)} %pad_maximum_fusion), channel_id=1, replica_groups=mesh['batch'=8,'seq'=16] {'seq'}, dimensions={0} | all-to-all | bytes 2359296 | tf_op jit(solution)/shard_map/all_to_all | solution.py:145
  176.6 1.8 copy.26
  178.3 3.0 reshape.120
  181.4 7.7 %fusion.24 = f32[1024,3072]{1,0:T(8,128)} fusion(bf16[192,3072]{1,0:T(8,128)(2,1)} %reshape.120, bf16[1,192,1024]{2,1,0:T(8,128)(2,1)S(1)} %copy-done.1, f32[192]{0:T(256)S(1)} %fusion.42, f32[192]{0:T(256)S(1)} %broadcast_multiply_fusion), kind=kOutput, calls=%fused_computation.42 | convolution fusion | flops 1208745984 | bytes 14157312 | tf_op jit(solution)/shard_map/dot_general | solution.py:149
  189.1 0.0 reduce-scatter.3.cloned.1.call-update
  189.1 0.0 all-reduce.3.cloned.1.call-start
  189.2 0.0 copy-start.3
  189.2 1.3 fusion.6
  190.5 0.0 copy-done.3
  190.5 5.9 %fusion.20 = (f32[192]{0:T(256)S(1)}, f32[192,1024]{1,0:T(8,128)}) fusion(bf16[1,192,1024]{2,1,0:T(8,128)(2,1)S(1)} %copy-done.1, f32[192]{0:T(256)S(1)} %broadcast_multiply_fusion, bf16[192,3072]{1,0:T(8,128)(2,1)S(1)} %copy-done.3, bf16[1024,3072]{1,0:T(8,128)(2,1)} %param.7), kind=kOutput, calls=%fused_computation.36 | convolution fusion | flops 1208745728 | bytes 8652288 | tf_op jit(solution)/shard_map/dot_general | solution.py:155
  196.5 0.0 reduce-scatter.5.cloned.1.call-done
  196.5 94.2 %reduce-scatter.3.cloned.1.call-done = f32[64,3072]{1,0:T(8,128)} async-done(((f32[1024,3072]{1,0:T(8,128)}), f32[64,3072]{1,0:T(8,128)}) %reduce-scatter.3.cloned.1.call-update) | async-done | bytes 786448 | tf_op jit(solution)/shard_map/reduce_scatter | solution.py:148
  290.7 0.0 all-reduce.3.cloned.1.call-update
  290.7 0.0 copy-start.5
  290.7 1.5 fusion.43
  292.3 0.0 copy-done.5
  292.3 1.1 fusion.30
  293.3 59.9 %all-reduce.3.cloned.1.call-done = (f32[64,3072]{1,0:T(8,128)}, f32[64,1024]{1,0:T(8,128)}) async-done(((f32[64,3072]{1,0:T(8,128)}, f32[64,1024]{1,0:T(8,128)}), (f32[64,3072]{1,0:T(8,128)}, f32[64,1024]{1,0:T(8,128)})) %all-reduce.3.cloned.1.call-update) | async-done | bytes 1048592 | tf_op jit(solution)/shard_map/psum | solution.py:154
  353.2 0.0 copy-start.7
  353.2 2.1 copy.44
  355.3 0.0 copy-done.7
  355.3 0.7 copy.45
  (6 shorter events, 0.1 us)
Async XLA Ops:
  7.2 3.2 copy-start
  10.4 2.0 copy-start.1
  16.9 1.3 copy-start.2
  18.2 21.2 %all-to-all-start = ((bf16[16,96,2,128]{3,1,2,0:T(8,128)(2,1)}), bf16[16,96,2,128]{3,1,2,0:T(8,128)(2,1)S(1)}, u32[]{:S(2)}, u32[]{:S(2)}) async-start(bf16[16,96,2,128]{3,1,2,0:T(8,128)(2,1)} %bitcast.111), calls=%async_computation | async-start | bytes 1572864 | tf_op jit(solution)/shard_map/all_to_all | solution.py:113
  42.0 24.6 %all-to-all-start.1 = ((bf16[16,192,2,128]{3,1,2,0:T(8,128)(2,1)}), bf16[16,192,2,128]{3,1,2,0:T(8,128)(2,1)}, u32[]{:S(2)}, u32[]{:S(2)}) async-start(bf16[16,192,2,128]{3,1,2,0:T(8,128)(2,1)} %bitcast.107), calls=%async_computation.1 | async-start | bytes 3145728 | tf_op jit(solution)/shard_map/all_to_all | solution.py:114
  46.4 150.0 %reduce-scatter.5.cloned.1.call-start = ((), (), s32[]{:S(2)}) async-start(), calls=%async_computation.7 | async-start | bytes 4456448 | tf_op jit(solution)/shard_map/reduce_scatter | solution.py:132
  69.3 38.3 %copy-start.4 = (bf16[1,192,1024]{2,1,0:T(8,128)(2,1)S(1)}, bf16[1,192,1024]{2,1,0:T(8,128)(2,1)}, u32[]{:S(2)}) copy-start(bf16[1,192,1024]{2,1,0:T(8,128)(2,1)} %param.9) | copy-start | bytes 1179652
  110.3 180.4 %reduce-scatter.3.cloned.1.call-start = ((), (), s32[]{:S(2)}) async-start(), calls=%async_computation.6 | async-start | bytes 13369344 | tf_op jit(solution)/shard_map/reduce_scatter | solution.py:148
  112.6 46.3 %collective-permute-start = (f32[16,96,2,128]{3,1,2,0:T(8,128)S(1)}, f32[16,96,2,128]{3,1,2,0:T(8,128)S(1)}, u32[]{:S(2)}, u32[]{:S(2)}) collective-permute-start(f32[16,96,2,128]{3,1,2,0:T(8,128)S(1)} %bitcast.114), channel_id=1, source_target_pairs={{0,1},{1,0},{2,3},{3,2},{4,5},{5,4},{6,7},{7,6},{8,9},{9,8},{10,11... | collective-permute-start | bytes 4718600 | tf_op jit(solution)/shard_map/ppermute | solution.py:13
  158.9 1.0 copy-start.6
  189.1 164.1 %all-reduce.3.cloned.1.call-start = ((), (), s32[]{:S(2)}) async-start(), calls=%async_computation.8 | async-start | bytes 2097152 | tf_op jit(solution)/shard_map/psum | solution.py:154
  189.2 1.4 copy-start.3
  290.7 1.6 copy-start.5
  353.2 2.1 copy-start.7
Sparse Core Ops, SparseCore 0:
  110.4 81.1 reduce-scatter.4
  195.0 95.5 reduce-scatter.2
  293.1 60.1 all-reduce.2

commit v3 on v2

--- a/solution.py
+++ b/solution.py
@@ -105,13 +105,16 @@
     qd_send = (
         qd.reshape(groups, part_rows, 2, H, head_size)
         .transpose(3, 0, 1, 2, 4)
-        .reshape(seq_count, part_rows, 2, head_size)
+        .reshape(seq_count, part_rows * 2, head_size)
     )
     paired = qkv_local[:, 1:].transpose(2, 0, 1, 3)
     paired_send = jnp.broadcast_to(paired[:, None], (H, groups, tok_rows, 2, head_size))
-    paired_send = paired_send.reshape(seq_count, tok_rows, 2, head_size)
-    qd_recv = lax.all_to_all(qd_send, "seq", split_axis=0, concat_axis=0, tiled=True)
-    paired_recv = lax.all_to_all(paired_send, "seq", split_axis=0, concat_axis=0, tiled=True)
+    paired_send = paired_send.reshape(seq_count, tok_rows * 2, head_size)
+    recv = lax.all_to_all(
+        jnp.concatenate([qd_send, paired_send], axis=1), "seq", split_axis=0, concat_axis=0, tiled=True
+    )
+    qd_recv = recv[:, : part_rows * 2].reshape(seq_count, part_rows, 2, head_size)
+    paired_recv = recv[:, part_rows * 2 :].reshape(seq_count, tok_rows, 2, head_size)
     queries = qd_recv[:, :, 0].reshape(seq_count * part_rows, head_size)
     dcontext_heads = qd_recv[:, :, 1].reshape(seq_count * part_rows, head_size)
     keys = paired_recv[:, :, 0].reshape(frame_total, head_size)
@@ -139,19 +142,27 @@
     split_grads = jnp.stack([dkeys, dvalues], axis=1).reshape(seq_count, groups, part_rows, 2, head_size)
     own_half = lax.dynamic_index_in_dim(split_grads, group_index, 1, keepdims=False)
     other_half = lax.dynamic_index_in_dim(split_grads, 1 - group_index, 1, keepdims=False)
-    partner_half = from_partner(other_half, "seq", 0)
-    paired_rows = (own_half + partner_half).astype(jnp.bfloat16)
+    partner_half = from_partner(other_half.astype(jnp.bfloat16), "seq", 0)
+    paired_rows = (own_half + partner_half.astype(jnp.float32)).astype(jnp.bfloat16)
     dtrio = jnp.concatenate([dquery.reshape(seq_count, part_rows, 1, head_size), paired_rows], axis=2)
     returned_grads = lax.all_to_all(dtrio, "seq", split_axis=0, concat_axis=0, tiled=True)
     dqkv = returned_grads.reshape(H, groups, part_rows, 3, head_size)
     dqkv = dqkv.transpose(1, 2, 3, 0, 4).reshape(tok_rows, 3 * width)
     qkv_share = lax.psum_scatter(
-        jnp.dot(normed.T, dqkv, preferred_element_type=jnp.float32),
+        jnp.dot(normed.T, dqkv, preferred_element_type=jnp.float32).astype(jnp.bfloat16),
         "seq",
         scatter_dimension=0,
         tiled=True,
+    ).astype(jnp.float32)
+    batch_count = lax.axis_size("batch")
+    shares = jnp.concatenate([qkv_share, out_share], axis=1)
+    share_rows = shares.shape[0] // batch_count
+    pieces = lax.all_to_all(
+        shares.reshape(batch_count, share_rows, shares.shape[1]), "batch", split_axis=0, concat_axis=0, tiled=True
     )
-    grad_qkv, grad_out = lax.psum((qkv_share, out_share), "batch")
+    summed = lax.all_gather(jnp.sum(pieces, axis=0), "batch", axis=0, tiled=True)
+    grad_qkv = summed[:, : qkv_share.shape[1]]
+    grad_out = summed[:, qkv_share.shape[1] :]
     dnormed = jnp.dot(dqkv, w_qkv.T, preferred_element_type=jnp.float32)
     unused, pull = jax.vjp(layer_norm, inputs)
     grad_input = (cotangent[0].astype(jnp.float32) + pull(dnormed)[0]).astype(jnp.bfloat16)

time: 365 us -> 366 us (level)
  waiting for transfers between devices: 229 us -> 207 us
  blocking collectives: 29.7 us -> 51.4 us
  other arithmetic: 8.16 us -> 13.3 us
  local copies, waits for them, and re-layouts: 18.7 us -> 23.2 us
  starting transfers between devices: 13.1 us -> 9.06 us
    reduce_scatter x1, waiting for transfers between devices: 0.02 us -> 80.3 us  [per_device(): lax.psum_scatter(jnp.dot(context.T, grad_rows, preferred_element_type=jnp...]
    psum x1 -> x0, waiting for transfers between devices: 59.9 us -> none  [per_device(): grad_qkv, grad_out = lax.psum((qkv_share, out_share), 'batch')]
    ppermute x1, waiting for transfers between devices: 46.2 us -> 16.2 us  [from_partner(): lax.ppermute(array, axis, [(i, i ^ 1 << stride) for i in range(lax.axis_s...]
    reduce_scatter x1, waiting for transfers between devices: 94.2 us -> 66.8 us  [per_device(): lax.psum_scatter(jnp.dot(normed.T, dqkv, preferred_element_type=jnp.float...]
    all_to_all x0 -> x1, blocking collectives: none -> 21.5 us  [per_device(): lax.all_to_all(shares.reshape(batch_count, share_rows, shares.shape[1]),...]
    all_gather x0 -> x1, waiting for transfers between devices: none -> 12.4 us  [per_device(): lax.all_gather(jnp.sum(pieces, axis=0), 'batch', axis=0, tiled=True)]
    slice x0 -> x6, local copies, waits for them, and re-layouts: none -> 8.37 us  [the longest x1 2.07 us: per_device(): grad_qkv = summed[:, :qkv_share.shape[1]]]
    convert_element_type x1 -> x3, other arithmetic: 0.27 us -> 5.22 us  [the longest x1 2.37 us: per_device(): partner_half = from_partner(other_half.astype(jnp.bfloat16), 'seq', 0)]
  transfers between devices with their start and end apart: 6 -> 5, of which waited for: 5 -> 5; matrix products, arithmetic and copies ran while one was open for 8% -> 4% of each run, Pallas kernels for 0% -> 0%
where the time goes in v3:
time: 366 us; the launch traced here: 365 us
  waiting for transfers between devices  207 us (57%)
  blocking collectives  51.4 us (14%)
  Pallas kernels  24.8 us (7%)
  local copies, waits for them, and re-layouts  23.2 us (6%)
  matrix products  21.5 us (6%)
  between operations  14.7 us (4%)
  other arithmetic  13.3 us (4%)
  starting transfers between devices  9.06 us (2%)
    reduce_scatter x1, waiting for transfers between devices, per_device(): lax.psum_scatter(jnp.dot(context.T, grad_rows, preferred_element_type=jnp...  80.3 us
    reduce_scatter x1, waiting for transfers between devices, per_device(): lax.psum_scatter(jnp.dot(normed.T, dqkv, preferred_element_type=jnp.float...  66.8 us
    all_to_all x1, waiting for transfers between devices, per_device(): lax.all_to_all(jnp.concatenate([qd_send, paired_send], axis=1), 'seq', sp...  31 us
    pallas_call x1, Pallas kernels, attn_pass(): pl.pallas_call(kernel, grid=grid, in_specs=[pl.BlockSpec((block, hd), lam...  24.8 us
    all_to_all x1, blocking collectives, per_device(): lax.all_to_all(shares.reshape(batch_count, share_rows, shares.shape[1]),...  21.5 us
    all_to_all x1, blocking collectives, per_device(): lax.all_to_all(dtrio, 'seq', split_axis=0, concat_axis=0, tiled=True)  18.6 us
    ppermute x1, waiting for transfers between devices, from_partner(): lax.ppermute(array, axis, [(i, i ^ 1 << stride) for i in range(lax.axis_s...  16.2 us
    all_gather x1, waiting for transfers between devices, per_device(): lax.all_gather(jnp.sum(pieces, axis=0), 'batch', axis=0, tiled=True)  12.4 us
  transfers between devices with their start and end apart: 5, of which 5 were waited for; matrix products, arithmetic and copies ran while one was open for 4% of the time, Pallas kernels for 0%

profile of v3, /device:TPU:1, one launch (start us, length us, event | category | flops | bytes accessed | tf_op | source)
XLA Modules:
  0.0 364.7 jit_solution(12765440771401003046)
XLA Ops:
  7.2 0.0 copy-start
  7.2 1.3 convert_reduce_fusion
  8.5 1.2 fusion.19
  9.7 4.4 %fusion.4 = bf16[24,8,24,128]{3,1,2,0:T(8,128)(2,1)S(1)} fusion(bf16[1024,3072]{1,0:T(8,128)(2,1)} %param.7, bf16[1,192,1024]{2,1,0:T(8,128)(2,1)} %param.5, f32[192]{0:T(256)S(1)} %fusion.43, f32[192]{0:T(256)S(1)} %broadcast_multiply_fusion), kind=kOutput, calls=%fused_computation.13 | convolution fusion | flops 1209335808 | bytes 7865856 | tf_op jit(solution)/shard_map/dot_general | solution.py:96
  14.2 0.2 copy.49
  14.4 0.0 copy-start.3
  14.4 1.0 slice_bitcast_fusion
  16.1 0.9 fusion.8
  17.0 0.1 copy.50
  17.1 0.0 copy-start.5
  17.1 0.1 maximum_bitcast_fusion.1
  17.1 0.8 copy.30
  18.0 0.2 copy-done.5
  18.2 0.6 copy.31
  18.8 1.2 broadcast_in_dim.32
  20.0 1.6 pad_maximum_fusion
  21.6 8.5 %all-to-all-start = ((bf16[16,576,128]{2,1,0:T(8,128)(2,1)}), bf16[16,576,128]{2,1,0:T(8,128)(2,1)}, u32[]{:S(2)}, u32[]{:S(2)}) async-start(bf16[16,576,128]{2,1,0:T(8,128)(2,1)} %pad_maximum_fusion), calls=%async_computation | async-start | bytes 4718592 | tf_op jit(solution)/shard_map/all_to_all | solution.py:113
  30.1 0.2 reduce-scatter.3.cloned.1.call-start
  30.3 0.6 compare_select_fusion.bias_ref
  30.9 31.0 %all-to-all-done = bf16[16,576,128]{2,1,0:T(8,128)(2,1)} async-done(((bf16[16,576,128]{2,1,0:T(8,128)(2,1)}), bf16[16,576,128]{2,1,0:T(8,128)(2,1)}, u32[]{:S(2)}, u32[]{:S(2)}) %all-to-all-start) | async-done | bytes 2359328 | tf_op jit(solution)/shard_map/all_to_all | solution.py:113
  61.9 1.5 slice.45
  63.5 1.0 copy.46
  64.5 0.3 fusion.45
  64.8 1.1 copy.36
  65.9 1.1 copy.37
  66.9 1.2 slice.42
  68.1 0.5 copy.45
  68.6 0.1 fusion.46
  68.8 0.8 copy.34
  69.6 0.8 copy.33
  70.5 24.8 %shard_map.84 = (bf16[1536,128]{1,0:T(8,128)(2,1)}, bf16[1536,128]{1,0:T(8,128)(2,1)}, f32[3072,128]{1,0:T(8,128)}, f32[3072,128]{1,0:T(8,128)}) custom-call(bf16[1536,128]{1,0:T(8,128)(2,1)} %bitcast.128, bf16[1536,128]{1,0:T(8,128)(2,1)} %bitcast.127, bf16[3072,128]{1,0:T(8,128)(2,1)} %bitcast.125, bf16[3072,128]{1,0:T(8,128)(2,1)} %bitcast.126, ...), custom_call_target="tpu_custom_call" | custom-call | tf_op jit(solution)/shard_map/pallas_call | solution.py:56
  95.3 2.4 fusion.24
  97.7 0.3 collective-permute-start
  98.0 16.2 %collective-permute-done = bf16[16,96,2,128]{3,1,2,0:T(8,128)(2,1)} collective-permute-done((bf16[16,96,2,128]{3,1,2,0:T(8,128)(2,1)}, bf16[16,96,2,128]{3,1,2,0:T(8,128)(2,1)}, u32[]{:S(2)}, u32[]{:S(2)}) %collective-permute-start) | collective-permute-done | bytes 786464 | tf_op jit(solution)/shard_map/ppermute | solution.py:13
  114.2 1.8 fusion.3
  116.0 0.1 pad_maximum_fusion.1
  116.2 18.6 %all_to_all.20 = bf16[16,96,3,128]{3,1,2,0:T(8,128)(2,1)S(1)} all-to-all(bf16[16,96,3,128]{3,1,2,0:T(8,128)(2,1)S(1)} %pad_maximum_fusion.1), channel_id=1, replica_groups=mesh['batch'=8,'seq'=16] {'seq'}, dimensions={0} | all-to-all | bytes 2359296 | tf_op jit(solution)/shard_map/all_to_all | solution.py:148
  134.8 1.8 copy.42
  136.5 3.0 reshape.132
  139.6 5.9 %convolution_convert_fusion = bf16[1024,3072]{1,0:T(8,128)(2,1)} fusion(bf16[192,3072]{1,0:T(8,128)(2,1)} %reshape.132, bf16[1,192,1024]{2,1,0:T(8,128)(2,1)S(1)} %copy-done.1, f32[192]{0:T(256)S(1)} %fusion.43, f32[192]{0:T(256)S(1)} %broadcast_multiply_fusion), kind=kOutput, calls=%fused_computation | convolution fusion | flops 1211891712 | bytes 7865856 | tf_op jit(solution)/shard_map/dot_general | solution.py:152
  145.4 0.0 reduce-scatter.3.cloned.1.call-update
  145.5 0.0 reduce-scatter.5.cloned.1.call-start
  145.5 0.9 copy-done.8
  146.4 11.3 %all_to_all.21 = bf16[16,96,128]{2,1,0:T(8,128)(2,1)S(1)} all-to-all(bf16[16,96,128]{2,1,0:T(8,128)(2,1)S(1)} %bitcast.135), channel_id=1, replica_groups=mesh['batch'=8,'seq'=16] {'seq'}, dimensions={0} | all-to-all | bytes 786432 | tf_op jit(solution)/shard_map/all_to_all | solution.py:127
  157.7 0.3 copy.38
  158.0 0.0 copy-start.6
  158.0 0.7 copy-done.6
  158.7 2.8 fusion.29
  161.6 0.0 reduce-scatter.5.cloned.1.call-update
  161.6 0.0 all-gather.2.cloned.1.call-start
  161.6 66.8 %reduce-scatter.3.cloned.1.call-done = bf16[64,3072]{1,0:T(8,128)(2,1)} async-done(((bf16[1024,3072]{1,0:T(8,128)(2,1)}), bf16[64,3072]{1,0:T(8,128)(2,1)}) %reduce-scatter.3.cloned.1.call-update) | async-done | bytes 393232 | tf_op jit(solution)/shard_map/reduce_scatter | solution.py:151
  228.5 1.0 convert_element_type.88
  229.5 80.3 %reduce-scatter.5.cloned.1.call-done = f32[64,1024]{1,0:T(8,128)} async-done(((f32[1024,1024]{1,0:T(8,128)}), f32[64,1024]{1,0:T(8,128)}) %reduce-scatter.5.cloned.1.call-update) | async-done | bytes 262160 | tf_op jit(solution)/shard_map/reduce_scatter | solution.py:135
  309.8 1.0 maximum_bitcast_fusion
  310.8 21.5 %all_to_all.22 = f32[8,8,4096]{2,1,0:T(8,128)S(1)} all-to-all(f32[8,8,4096]{2,1,0:T(8,128)S(1)} %maximum_bitcast_fusion), channel_id=1, replica_groups=mesh['batch'=8,'seq'=16] {'batch'}, dimensions={0} | all-to-all | bytes 2097152 | tf_op jit(solution)/shard_map/all_to_all | solution.py:160
  332.3 0.7 reduce_sum.50
  333.0 0.0 all-gather.2.cloned.1.call-update
  333.0 2.4 fusion.7
  335.5 5.1 %fusion.21 = (f32[192]{0:T(256)S(1)}, f32[192,1024]{1,0:T(8,128)S(1)}) fusion(bf16[1,192,1024]{2,1,0:T(8,128)(2,1)S(1)} %copy-done.1, f32[192]{0:T(256)S(1)} %broadcast_multiply_fusion, bf16[192,3072]{1,0:T(8,128)(2,1)S(1)} %copy-done.2, bf16[1024,3072]{1,0:T(8,128)(2,1)} %param.7), kind=kOutput, calls=%fused_computation.40 | convolution fusion | flops 1208745728 | bytes 8652288 | tf_op jit(solution)/shard_map/dot_general | solution.py:166
  340.6 0.4 fusion.44
  341.0 1.1 fusion.31
  342.1 12.4 %all-gather.2.cloned.1.call-done = f32[64,4096]{1,0:T(8,128)} async-done(((f32[8,4096]{1,0:T(8,128)}), f32[64,4096]{1,0:T(8,128)}) %all-gather.2.cloned.1.call-update) | async-done | bytes 1048592 | tf_op jit(solution)/shard_map/all_gather | solution.py:163
  354.5 2.1 slice.48
  356.5 1.7 slice.49
  (17 shorter events, 0.1 us)
Async XLA Ops:
  7.2 8.9 %copy-start = (bf16[1024,1024]{1,0:T(8,128)(2,1)S(1)}, bf16[1024,1024]{1,0:T(8,128)(2,1)}, u32[]{:S(2)}) copy-start(bf16[1024,1024]{1,0:T(8,128)(2,1)} %param.8) | copy-start | bytes 6291460
  14.4 1.7 copy-start.3
  17.1 1.1 copy-start.5
  21.6 40.4 %all-to-all-start = ((bf16[16,576,128]{2,1,0:T(8,128)(2,1)}), bf16[16,576,128]{2,1,0:T(8,128)(2,1)}, u32[]{:S(2)}, u32[]{:S(2)}) async-start(bf16[16,576,128]{2,1,0:T(8,128)(2,1)} %pad_maximum_fusion), calls=%async_computation | async-start | bytes 4718592 | tf_op jit(solution)/shard_map/all_to_all | solution.py:113
  30.1 198.4 %reduce-scatter.3.cloned.1.call-start = ((), (), s32[]{:S(2)}) async-start(), calls=%async_computation.6 | async-start | bytes 6684672 | tf_op jit(solution)/shard_map/reduce_scatter | solution.py:151
  97.7 16.5 %collective-permute-start = (bf16[16,96,2,128]{3,1,2,0:T(8,128)(2,1)}, bf16[16,96,2,128]{3,1,2,0:T(8,128)(2,1)}, u32[]{:S(2)}, u32[]{:S(2)}) collective-permute-start(bf16[16,96,2,128]{3,1,2,0:T(8,128)(2,1)} %fusion.24), channel_id=1, source_target_pairs={{0,1},{1,0},{2,3},{3,2},{4,5},{5,4},{6,7},{7,6},{8,9},{9,8},{10,11... | collective-permute-start | bytes 2359304 | tf_op jit(solution)/shard_map/ppermute | solution.py:13
  98.0 18.1 %copy-start.7 = (bf16[1536,128]{1,0:T(8,128)(2,1)S(1)}, bf16[1536,128]{1,0:T(8,128)(2,1)}, u32[]{:S(2)}) copy-start(bf16[1536,128]{1,0:T(8,128)(2,1)} %get-tuple-element.9) | copy-start | bytes 1179652
  136.5 3.1 copy-start.1
  145.4 1.0 copy-start.8
  145.5 164.3 %reduce-scatter.5.cloned.1.call-start = ((), (), s32[]{:S(2)}) async-start(), calls=%async_computation.7 | async-start | bytes 4456448 | tf_op jit(solution)/shard_map/reduce_scatter | solution.py:135
  158.0 0.7 copy-start.6
  161.6 192.9 %all-gather.2.cloned.1.call-start = ((), (), s32[]{:S(2)}) async-start(), calls=%async_computation.8 | async-start | bytes 1179648 | tf_op jit(solution)/shard_map/all_gather | solution.py:163
  333.0 2.4 copy-start.2
  335.5 5.5 %copy-start.4 = (bf16[1,192,1024]{2,1,0:T(8,128)(2,1)S(1)}, bf16[1,192,1024]{2,1,0:T(8,128)(2,1)}, u32[]{:S(2)}) copy-start(bf16[1,192,1024]{2,1,0:T(8,128)(2,1)} %param.9) | copy-start | bytes 1179652
Sparse Core Ops, SparseCore 0:
  145.6 82.8 reduce-scatter.2
  231.8 77.9 reduce-scatter.4
  333.1 21.2 all-gather.1

commit v4 on v3

--- a/solution.py
+++ b/solution.py
@@ -124,45 +124,43 @@
 
     context_h, dquery, dkeys, dvalues = attn_pass(queries, keys, values, dcontext_heads, bias, scale)
 
-    context_back = lax.all_to_all(
-        context_h.reshape(seq_count, part_rows, head_size), "seq", split_axis=0, concat_axis=0, tiled=True
-    )
-    context = (
-        context_back.reshape(H, groups, part_rows, head_size).transpose(1, 2, 0, 3).reshape(tok_rows, width)
-    )
-    branch = jnp.dot(context, w_out, preferred_element_type=jnp.float32)
-    output = (inputs + valid[:, None] * branch).astype(jnp.bfloat16)
-    out_share = lax.psum_scatter(
-        jnp.dot(context.T, grad_rows, preferred_element_type=jnp.float32),
-        "seq",
-        scatter_dimension=0,
-        tiled=True,
-    )
-
     split_grads = jnp.stack([dkeys, dvalues], axis=1).reshape(seq_count, groups, part_rows, 2, head_size)
     own_half = lax.dynamic_index_in_dim(split_grads, group_index, 1, keepdims=False)
     other_half = lax.dynamic_index_in_dim(split_grads, 1 - group_index, 1, keepdims=False)
     partner_half = from_partner(other_half.astype(jnp.bfloat16), "seq", 0)
     paired_rows = (own_half + partner_half.astype(jnp.float32)).astype(jnp.bfloat16)
-    dtrio = jnp.concatenate([dquery.reshape(seq_count, part_rows, 1, head_size), paired_rows], axis=2)
-    returned_grads = lax.all_to_all(dtrio, "seq", split_axis=0, concat_axis=0, tiled=True)
-    dqkv = returned_grads.reshape(H, groups, part_rows, 3, head_size)
-    dqkv = dqkv.transpose(1, 2, 3, 0, 4).reshape(tok_rows, 3 * width)
-    qkv_share = lax.psum_scatter(
-        jnp.dot(normed.T, dqkv, preferred_element_type=jnp.float32).astype(jnp.bfloat16),
-        "seq",
-        scatter_dimension=0,
-        tiled=True,
+    back = jnp.concatenate(
+        [
+            context_h.reshape(seq_count, part_rows, 1, head_size),
+            dquery.reshape(seq_count, part_rows, 1, head_size),
+            paired_rows,
+        ],
+        axis=2,
+    )
+    returned = lax.all_to_all(back, "seq", split_axis=0, concat_axis=0, tiled=True)
+    returned = returned.reshape(H, groups, part_rows, 4, head_size).transpose(1, 2, 3, 0, 4)
+    context = returned[:, :, 0].reshape(tok_rows, width)
+    dqkv = returned[:, :, 1:].reshape(tok_rows, 3 * width)
+    branch = jnp.dot(context, w_out, preferred_element_type=jnp.float32)
+    output = (inputs + valid[:, None] * branch).astype(jnp.bfloat16)
+    partials = jnp.concatenate(
+        [
+            jnp.dot(normed.T, dqkv, preferred_element_type=jnp.float32),
+            jnp.dot(context.T, grad_rows, preferred_element_type=jnp.float32),
+        ],
+        axis=1,
+    )
+    shares = lax.psum_scatter(
+        partials.astype(jnp.bfloat16), "seq", scatter_dimension=0, tiled=True
     ).astype(jnp.float32)
     batch_count = lax.axis_size("batch")
-    shares = jnp.concatenate([qkv_share, out_share], axis=1)
     share_rows = shares.shape[0] // batch_count
     pieces = lax.all_to_all(
         shares.reshape(batch_count, share_rows, shares.shape[1]), "batch", split_axis=0, concat_axis=0, tiled=True
     )
     summed = lax.all_gather(jnp.sum(pieces, axis=0), "batch", axis=0, tiled=True)
-    grad_qkv = summed[:, : qkv_share.shape[1]]
-    grad_out = summed[:, qkv_share.shape[1] :]
+    grad_qkv = summed[:, : 3 * width]
+    grad_out = summed[:, 3 * width :]
     dnormed = jnp.dot(dqkv, w_qkv.T, preferred_element_type=jnp.float32)
     unused, pull = jax.vjp(layer_norm, inputs)
     grad_input = (cotangent[0].astype(jnp.float32) + pull(dnormed)[0]).astype(jnp.bfloat16)

time: 366 us -> 301 us (0.82)
  waiting for transfers between devices: 207 us -> 147 us
  blocking collectives: 51.4 us -> 44 us
  other arithmetic: 13.3 us -> 19.7 us
    reduce_scatter x2 -> x1, waiting for transfers between devices: 147 us -> 86.6 us  [per_device(): lax.psum_scatter(partials.astype(jnp.bfloat16), 'seq', scatter_dimension=...]
    concatenate x1 -> x2, other arithmetic: 0.1 us -> 7.71 us  [the longest x1 7.57 us: per_device(): jnp.concatenate([jnp.dot(normed.T, dqkv, preferred_element_type=jnp.float...]
    all_to_all x2 -> x1, blocking collectives: 29.9 us -> 22.8 us  [per_device(): lax.all_to_all(back, 'seq', split_axis=0, concat_axis=0, tiled=True)]
  transfers between devices with their start and end apart: 5 -> 4, of which waited for: 5 -> 4; matrix products, arithmetic and copies ran while one was open for 4% -> 3% of each run, Pallas kernels for 0% -> 0%
where the time goes in v4:
time: 301 us
  waiting for transfers between devices  147 us (49%)
  blocking collectives  44 us (15%)
  Pallas kernels  24.8 us (8%)
  local copies, waits for them, and re-layouts  21.3 us (7%)
  matrix products  19.9 us (7%)
  other arithmetic  19.7 us (7%)
  between operations  15 us (5%)
  starting transfers between devices  9.02 us (3%)
    reduce_scatter x1, waiting for transfers between devices, per_device(): lax.psum_scatter(partials.astype(jnp.bfloat16), 'seq', scatter_dimension=...  86.6 us
    all_to_all x1, waiting for transfers between devices, per_device(): lax.all_to_all(jnp.concatenate([qd_send, paired_send], axis=1), 'seq', sp...  31 us
    pallas_call x1, Pallas kernels, attn_pass(): pl.pallas_call(kernel, grid=grid, in_specs=[pl.BlockSpec((block, hd), lam...  24.8 us
    all_to_all x1, blocking collectives, per_device(): lax.all_to_all(back, 'seq', split_axis=0, concat_axis=0, tiled=True)  22.8 us
    all_to_all x1, blocking collectives, per_device(): lax.all_to_all(shares.reshape(batch_count, share_rows, shares.shape[1]),...  21.2 us
    ppermute x1, waiting for transfers between devices, from_partner(): lax.ppermute(array, axis, [(i, i ^ 1 << stride) for i in range(lax.axis_s...  16.1 us
    all_gather x1, waiting for transfers between devices, per_device(): lax.all_gather(jnp.sum(pieces, axis=0), 'batch', axis=0, tiled=True)  13.3 us
    all_to_all x1, starting transfers between devices, per_device(): lax.all_to_all(jnp.concatenate([qd_send, paired_send], axis=1), 'seq', sp...  8.46 us
  transfers between devices with their start and end apart: 4, of which 4 were waited for; matrix products, arithmetic and copies ran while one was open for 3% of the time, Pallas kernels for 0%

profile of v4, /device:TPU:1, one launch (start us, length us, event | category | flops | bytes accessed | tf_op | source)
XLA Modules:
  0.0 300.8 jit_solution(3736412868956418259)
XLA Ops:
  7.2 0.0 copy-start
  7.2 1.3 convert_reduce_fusion
  8.5 1.2 fusion.19
  9.7 4.4 %fusion.4 = bf16[24,8,24,128]{3,1,2,0:T(8,128)(2,1)S(1)} fusion(bf16[1024,3072]{1,0:T(8,128)(2,1)} %param.7, bf16[1,192,1024]{2,1,0:T(8,128)(2,1)} %param.5, f32[192]{0:T(256)S(1)} %fusion.42, f32[192]{0:T(256)S(1)} %broadcast_multiply_fusion), kind=kOutput, calls=%fused_computation.16 | convolution fusion | flops 1209335808 | bytes 7865856 | tf_op jit(solution)/shard_map/dot_general | solution.py:96
  14.2 0.2 copy.56
  14.4 0.0 copy-start.3
  14.4 0.8 slice.48
  15.1 0.1 slice_bitcast_fusion
  16.0 0.9 fusion.8
  16.8 0.0 copy-start.5
  16.9 0.1 copy.57
  16.9 0.6 copy.35
  17.5 0.3 copy-done.5
  17.8 0.1 maximum_bitcast_fusion
  17.9 0.8 copy.34
  18.7 1.2 broadcast_in_dim.32
  20.0 1.6 pad_maximum_fusion.1
  21.5 8.5 %all-to-all-start = ((bf16[16,576,128]{2,1,0:T(8,128)(2,1)}), bf16[16,576,128]{2,1,0:T(8,128)(2,1)}, u32[]{:S(2)}, u32[]{:S(2)}) async-start(bf16[16,576,128]{2,1,0:T(8,128)(2,1)} %pad_maximum_fusion.1), calls=%async_computation | async-start | bytes 4718592 | tf_op jit(solution)/shard_map/all_to_all | solution.py:113
  30.0 0.2 reduce-scatter.2.cloned.1.call-start
  30.2 0.6 compare_select_fusion.bias_ref
  30.9 31.0 %all-to-all-done = bf16[16,576,128]{2,1,0:T(8,128)(2,1)} async-done(((bf16[16,576,128]{2,1,0:T(8,128)(2,1)}), bf16[16,576,128]{2,1,0:T(8,128)(2,1)}, u32[]{:S(2)}, u32[]{:S(2)}) %all-to-all-start) | async-done | bytes 2359328 | tf_op jit(solution)/shard_map/all_to_all | solution.py:113
  61.9 1.5 slice.53
  63.4 1.0 copy.53
  64.4 1.2 slice.50
  65.6 0.5 copy.52
  66.1 0.1 fusion.45
  66.3 0.8 copy.38
  67.1 0.3 fusion.44
  67.4 1.1 copy.41
  68.5 0.8 copy.37
  69.3 1.1 copy.40
  70.4 24.8 %shard_map.84 = (bf16[1536,128]{1,0:T(8,128)(2,1)}, bf16[1536,128]{1,0:T(8,128)(2,1)}, f32[3072,128]{1,0:T(8,128)}, f32[3072,128]{1,0:T(8,128)}) custom-call(bf16[1536,128]{1,0:T(8,128)(2,1)} %bitcast.130, bf16[1536,128]{1,0:T(8,128)(2,1)} %bitcast.129, bf16[3072,128]{1,0:T(8,128)(2,1)} %bitcast.128, bf16[3072,128]{1,0:T(8,128)(2,1)} %bitcast.127, ...), custom_call_target="tpu_custom_call" | custom-call | tf_op jit(solution)/shard_map/pallas_call | solution.py:56
  95.2 2.4 fusion.24
  97.6 0.3 collective-permute-start
  97.9 16.1 %collective-permute-done = bf16[16,96,2,128]{3,1,2,0:T(8,128)(2,1)S(1)} collective-permute-done((bf16[16,96,2,128]{3,1,2,0:T(8,128)(2,1)}, bf16[16,96,2,128]{3,1,2,0:T(8,128)(2,1)S(1)}, u32[]{:S(2)}, u32[]{:S(2)}) %collective-permute-start) | collective-permute-done | bytes 786464 | tf_op jit(solution)/shard_map/ppermute | solution.py:13
  114.0 1.6 fusion.3
  115.6 0.1 pad_maximum_fusion.2
  115.8 22.8 %all_to_all.15 = bf16[16,96,4,128]{3,1,2,0:T(8,128)(2,1)S(1)} all-to-all(bf16[16,96,4,128]{3,1,2,0:T(8,128)(2,1)S(1)} %pad_maximum_fusion.2), channel_id=1, replica_groups=mesh['batch'=8,'seq'=16] {'seq'}, dimensions={0} | all-to-all | bytes 3145728 | tf_op jit(solution)/shard_map/all_to_all | solution.py:140
  138.6 0.8 slice.56
  139.4 0.1 slice.57
  139.5 0.8 copy.47
  140.2 1.4 reshape.127
  141.6 1.3 copy.46
  142.8 0.0 copy-start.6
  142.9 0.7 copy-done.6
  143.6 3.1 %convolution_convert_fusion.2 = bf16[1024,1024]{1,0:T(8,128)(2,1)} fusion(bf16[1,192,1024]{2,1,0:T(8,128)(2,1)} %param.9, f32[192]{0:T(256)S(1)} %compare_convert_fusion, bf16[24,8,8,128]{3,2,1,0:T(8,128)(2,1)S(1)} %bitcast.133), kind=kOutput, calls=%fused_computation.8 | convolution fusion | flops 404291584 | bytes 2884352 | tf_op jit(solution)/shard_map/dot_general | solution.py:149
  146.7 4.6 %convolution_convert_fusion = bf16[1024,3072]{1,0:T(8,128)(2,1)} fusion(bf16[192,3072]{1,0:T(8,128)(2,1)S(1)} %copy-done.2, bf16[1,192,1024]{2,1,0:T(8,128)(2,1)S(1)} %copy-done.1, f32[192]{0:T(256)S(1)} %fusion.42, f32[192]{0:T(256)S(1)} %broadcast_multiply_fusion), kind=kOutput, calls=%fused_computation.1 | convolution fusion | flops 1211891712 | bytes 7865856 | tf_op jit(solution)/shard_map/dot_general | solution.py:148
  151.4 7.6 %pad_maximum_fusion = bf16[1024,4096]{1,0:T(8,128)(2,1)} fusion(bf16[1024,1024]{1,0:T(8,128)(2,1)} %convolution_convert_fusion.2, bf16[1024,3072]{1,0:T(8,128)(2,1)} %convolution_convert_fusion), kind=kLoop, calls=%fused_computation | loop fusion | flops 16777216 | bytes 16777216 | tf_op jit(solution)/shard_map/concatenate | solution.py:146
  158.9 0.0 reduce-scatter.2.cloned.1.call-update
  159.0 0.0 all-gather.2.cloned.1.call-start
  159.0 86.6 %reduce-scatter.2.cloned.1.call-done = bf16[64,4096]{1,0:T(8,128)(2,1)} async-done(((bf16[1024,4096]{1,0:T(8,128)(2,1)}), bf16[64,4096]{1,0:T(8,128)(2,1)}) %reduce-scatter.2.cloned.1.call-update) | async-done | bytes 524304 | tf_op jit(solution)/shard_map/reduce_scatter | solution.py:153
  245.6 1.1 bitcast_convert_fusion
  246.7 21.2 %all_to_all.16 = f32[8,8,4096]{2,1,0:T(8,128)S(1)} all-to-all(f32[8,8,4096]{2,1,0:T(8,128)S(1)} %bitcast_convert_fusion), channel_id=1, replica_groups=mesh['batch'=8,'seq'=16] {'batch'}, dimensions={0} | all-to-all | bytes 2097152 | tf_op jit(solution)/shard_map/all_to_all | solution.py:158
  267.9 0.7 reduce_sum.50
  268.6 0.0 all-gather.2.cloned.1.call-update
  268.6 0.0 copy-start.7
  268.6 5.5 %fusion.21 = (f32[192]{0:T(256)S(1)}, f32[192,1024]{1,0:T(8,128)S(1)}) fusion(bf16[1,192,1024]{2,1,0:T(8,128)(2,1)S(1)} %copy-done.1, f32[192]{0:T(256)S(1)} %broadcast_multiply_fusion, bf16[192,3072]{1,0:T(8,128)(2,1)} %reshape.127, bf16[1024,3072]{1,0:T(8,128)(2,1)} %param.7), kind=kOutput, calls=%fused_computation.41 | convolution fusion | flops 1208745728 | bytes 8652288 | tf_op jit(solution)/shard_map/dot_general | solution.py:164
  274.1 0.4 fusion.43
  274.5 0.0 copy-start.4
  274.5 1.3 fusion.7
  275.9 1.1 fusion.30
  276.9 13.3 %all-gather.2.cloned.1.call-done = f32[64,4096]{1,0:T(8,128)} async-done(((f32[8,4096]{1,0:T(8,128)}), f32[64,4096]{1,0:T(8,128)}) %all-gather.2.cloned.1.call-update) | async-done | bytes 1048592 | tf_op jit(solution)/shard_map/all_gather | solution.py:161
  290.2 1.7 slice.59
  291.9 2.1 slice.58
  (17 shorter events, 0.1 us)
Async XLA Ops:
  7.2 8.8 %copy-start = (bf16[1024,1024]{1,0:T(8,128)(2,1)S(1)}, bf16[1024,1024]{1,0:T(8,128)(2,1)}, u32[]{:S(2)}) copy-start(bf16[1024,1024]{1,0:T(8,128)(2,1)} %param.8) | copy-start | bytes 6291460
  14.4 1.6 copy-start.3
  16.8 1.0 copy-start.5
  21.5 40.3 %all-to-all-start = ((bf16[16,576,128]{2,1,0:T(8,128)(2,1)}), bf16[16,576,128]{2,1,0:T(8,128)(2,1)}, u32[]{:S(2)}, u32[]{:S(2)}) async-start(bf16[16,576,128]{2,1,0:T(8,128)(2,1)} %pad_maximum_fusion.1), calls=%async_computation | async-start | bytes 4718592 | tf_op jit(solution)/shard_map/all_to_all | solution.py:113
  30.0 215.6 %reduce-scatter.2.cloned.1.call-start = ((), (), s32[]{:S(2)}) async-start(), calls=%async_computation.4 | async-start | bytes 8912896 | tf_op jit(solution)/shard_map/reduce_scatter | solution.py:153
  97.6 16.4 %collective-permute-start = (bf16[16,96,2,128]{3,1,2,0:T(8,128)(2,1)}, bf16[16,96,2,128]{3,1,2,0:T(8,128)(2,1)S(1)}, u32[]{:S(2)}, u32[]{:S(2)}) collective-permute-start(bf16[16,96,2,128]{3,1,2,0:T(8,128)(2,1)} %fusion.24), channel_id=1, source_target_pairs={{0,1},{1,0},{2,3},{3,2},{4,5},{5,4},{6,7},{7,6},{8,9},{9,8},{10,11... | collective-permute-start | bytes 2359304 | tf_op jit(solution)/shard_map/ppermute | solution.py:13
  97.9 17.7 %copy-start.8 = (bf16[1536,128]{1,0:T(8,128)(2,1)S(1)}, bf16[1536,128]{1,0:T(8,128)(2,1)}, u32[]{:S(2)}) copy-start(bf16[1536,128]{1,0:T(8,128)(2,1)} %get-tuple-element.8) | copy-start | bytes 1179652
  97.9 17.7 %copy-start.9 = (bf16[1536,128]{1,0:T(8,128)(2,1)S(1)}, bf16[1536,128]{1,0:T(8,128)(2,1)}, u32[]{:S(2)}) copy-start(bf16[1536,128]{1,0:T(8,128)(2,1)} %get-tuple-element.9) | copy-start | bytes 1179652
  142.8 0.7 copy-start.6
  142.8 3.9 %copy-start.1 = (bf16[1,192,1024]{2,1,0:T(8,128)(2,1)S(1)}, bf16[1,192,1024]{2,1,0:T(8,128)(2,1)}, u32[]{:S(2)}) copy-start(bf16[1,192,1024]{2,1,0:T(8,128)(2,1)} %param.5) | copy-start | bytes 1179652
  142.9 3.9 %copy-start.2 = (bf16[192,3072]{1,0:T(8,128)(2,1)S(1)}, bf16[192,3072]{1,0:T(8,128)(2,1)}, u32[]{:S(2)}) copy-start(bf16[192,3072]{1,0:T(8,128)(2,1)} %reshape.127) | copy-start | bytes 3538948
  159.0 131.3 %all-gather.2.cloned.1.call-start = ((), (), s32[]{:S(2)}) async-start(), calls=%async_computation.5 | async-start | bytes 1179648 | tf_op jit(solution)/shard_map/all_gather | solution.py:161
  268.6 5.9 %copy-start.7 = (bf16[2,96,1,8,128]{4,3,1,0,2:T(8,128)(2,1)S(1)}, bf16[2,96,1,8,128]{4,3,1,0,2:T(8,128)(2,1)}, u32[]{:S(2)}) copy-start(bf16[2,96,1,8,128]{4,3,1,0,2:T(8,128)(2,1)} %copy-done.6) | copy-start | bytes 1179652
  274.5 1.4 copy-start.4
Sparse Core Ops, SparseCore 0:
  159.1 86.4 reduce-scatter.1
  268.7 21.4 all-gather.1

commit v5 on v4

--- a/solution.py
+++ b/solution.py
@@ -113,6 +113,10 @@
     recv = lax.all_to_all(
         jnp.concatenate([qd_send, paired_send], axis=1), "seq", split_axis=0, concat_axis=0, tiled=True
     )
+    normed_send = jnp.broadcast_to(normed.reshape(1, groups, part_rows, width), (H, groups, part_rows, width))
+    normed_recv = lax.all_to_all(
+        normed_send.reshape(seq_count, part_rows, width), "seq", split_axis=0, concat_axis=0, tiled=True
+    ).reshape(seq_count * part_rows, width)
     qd_recv = recv[:, : part_rows * 2].reshape(seq_count, part_rows, 2, head_size)
     paired_recv = recv[:, part_rows * 2 :].reshape(seq_count, tok_rows, 2, head_size)
     queries = qd_recv[:, :, 0].reshape(seq_count * part_rows, head_size)
@@ -143,16 +147,23 @@
     dqkv = returned[:, :, 1:].reshape(tok_rows, 3 * width)
     branch = jnp.dot(context, w_out, preferred_element_type=jnp.float32)
     output = (inputs + valid[:, None] * branch).astype(jnp.bfloat16)
-    partials = jnp.concatenate(
-        [
-            jnp.dot(normed.T, dqkv, preferred_element_type=jnp.float32),
-            jnp.dot(context.T, grad_rows, preferred_element_type=jnp.float32),
-        ],
-        axis=1,
+    dqkv_head = jnp.concatenate([dquery.reshape(seq_count, part_rows, 1, head_size), paired_rows], axis=2)
+    qkv_part = jnp.dot(
+        normed_recv.T, dqkv_head.reshape(seq_count * part_rows, 3 * head_size), preferred_element_type=jnp.float32
     )
-    shares = lax.psum_scatter(
-        partials.astype(jnp.bfloat16), "seq", scatter_dimension=0, tiled=True
+    out_part = jnp.dot(context.T, grad_rows, preferred_element_type=jnp.float32)
+    share_rows = width // seq_count
+    parts = jnp.concatenate([qkv_part, out_part], axis=1).astype(jnp.bfloat16)
+    gathered = lax.all_to_all(
+        parts.reshape(seq_count, share_rows, parts.shape[1]), "seq", split_axis=0, concat_axis=0, tiled=True
     ).astype(jnp.float32)
+    qkv_rows = (
+        jnp.sum(gathered[:, :, : 3 * head_size].reshape(H, groups, share_rows, 3, head_size), axis=1)
+        .transpose(1, 2, 0, 3)
+        .reshape(share_rows, 3 * width)
+    )
+    out_rows = jnp.sum(gathered[:, :, 3 * head_size :], axis=0)
+    shares = jnp.concatenate([qkv_rows, out_rows], axis=1)
     batch_count = lax.axis_size("batch")
     share_rows = shares.shape[0] // batch_count
     pieces = lax.all_to_all(

time: 301 us -> 269 us (0.89)
  waiting for transfers between devices: 147 us -> 54.6 us
  local copies, waits for them, and re-layouts: 21.3 us -> 50.6 us
  blocking collectives: 44 us -> 61.7 us
  starting transfers between devices: 9.02 us -> 23.4 us
    reduce_scatter x1 -> x0, waiting for transfers between devices: 86.6 us -> none  [per_device(): lax.psum_scatter(partials.astype(jnp.bfloat16), 'seq', scatter_dimension=...]
    all_to_all x1, blocking collectives: 22.8 us -> 38 us  [per_device(): lax.all_to_all(parts.reshape(seq_count, share_rows, parts.shape[1]), 'seq...]
    all_to_all x0 -> x2, starting transfers between devices: none -> 13.4 us  [the longest x1 8.79 us: per_device(): lax.all_to_all(back, 'seq', split_axis=0, concat_axis=0, tiled=True)]
    reshape x0 -> x3, local copies, waits for them, and re-layouts: none -> 9.97 us  [the longest x1 3.95 us: per_device(): dqkv_head.reshape(seq_count * part_rows, 3 * head_size)]
    all_gather x1, waiting for transfers between devices: 13.3 us -> 6.38 us  [per_device(): lax.all_gather(jnp.sum(pieces, axis=0), 'batch', axis=0, tiled=True)]
    dot_general x0 -> x2, local copies, waits for them, and re-layouts: none -> 5.84 us  [the longest x1 4.65 us: per_device(): jnp.dot(normed_recv.T, dqkv_head.reshape(seq_count * part_rows, 3 * head_...]
    concatenate x1 -> x3, other arithmetic: 7.57 us -> 2.5 us  [the longest x1 2.12 us: per_device(): jnp.concatenate([dquery.reshape(seq_count, part_rows, 1, head_size), pair...]
    concatenate x0 -> x2, local copies, waits for them, and re-layouts: none -> 4 us  [the longest x1 2.75 us: per_device(): jnp.concatenate([dquery.reshape(seq_count, part_rows, 1, head_size), pair...]
  transfers between devices with their start and end apart: 4 -> 5, of which waited for: 4 -> 4; matrix products, arithmetic and copies ran while one was open for 3% -> 17% of each run, Pallas kernels for 0% -> 9%
where the time goes in v5:
time: 269 us; the launch traced here: 267 us
  blocking collectives  61.7 us (23%)
  waiting for transfers between devices  54.6 us (20%)
  local copies, waits for them, and re-layouts  50.6 us (19%)
  Pallas kernels  24.8 us (9%)
  starting transfers between devices  23.4 us (9%)
  other arithmetic  19.3 us (7%)
  matrix products  17.9 us (7%)
  between operations  15.1 us (6%)
    all_to_all x1, blocking collectives, per_device(): lax.all_to_all(parts.reshape(seq_count, share_rows, parts.shape[1]), 'seq...  38 us
    all_to_all x1, waiting for transfers between devices, per_device(): lax.all_to_all(jnp.concatenate([qd_send, paired_send], axis=1), 'seq', sp...  31.5 us
    pallas_call x1, Pallas kernels, attn_pass(): pl.pallas_call(kernel, grid=grid, in_specs=[pl.BlockSpec((block, hd), lam...  24.8 us
    all_to_all x1, blocking collectives, per_device(): lax.all_to_all(shares.reshape(batch_count, share_rows, shares.shape[1]),...  23.8 us
    ppermute x1, waiting for transfers between devices, from_partner(): lax.ppermute(array, axis, [(i, i ^ 1 << stride) for i in range(lax.axis_s...  15.3 us
    all_to_all x1, starting transfers between devices, per_device(): lax.all_to_all(back, 'seq', split_axis=0, concat_axis=0, tiled=True)  8.79 us
    all_to_all x1, starting transfers between devices, per_device(): lax.all_to_all(jnp.concatenate([qd_send, paired_send], axis=1), 'seq', sp...  8.59 us
    all_gather x1, waiting for transfers between devices, per_device(): lax.all_gather(jnp.sum(pieces, axis=0), 'batch', axis=0, tiled=True)  6.38 us
  transfers between devices with their start and end apart: 5, of which 4 were waited for; matrix products, arithmetic and copies ran while one was open for 17% of the time, Pallas kernels for 9%

profile of v5, /device:TPU:1, one launch (start us, length us, event | category | flops | bytes accessed | tf_op | source)
XLA Modules:
  0.0 267.4 jit_solution(164816544742148194)
XLA Ops:
  7.2 1.3 convert_reduce_fusion
  8.5 1.2 multiply_reduce_fusion.1
  9.7 4.4 %fusion.4 = bf16[24,8,24,128]{3,1,2,0:T(8,128)(2,1)S(1)} fusion(bf16[1024,3072]{1,0:T(8,128)(2,1)} %param.7, bf16[1,192,1024]{2,1,0:T(8,128)(2,1)} %param.5, f32[192]{0:T(256)S(1)} %fusion.25, f32[192]{0:T(256)S(1)} %broadcast_multiply_fusion), kind=kOutput, calls=%fused_computation.17 | convolution fusion | flops 1209335808 | bytes 7865856 | tf_op jit(solution)/shard_map/dot_general | solution.py:96
  14.4 0.8 slice.56
  16.0 0.9 fusion.8
  16.9 0.6 copy.47
  17.5 0.3 copy-done.10
  17.9 0.8 copy.46
  18.7 1.2 broadcast_in_dim.20
  20.0 1.6 pad_maximum_fusion.1
  21.5 8.6 %all-to-all-start = ((bf16[16,576,128]{2,1,0:T(8,128)(2,1)}), bf16[16,576,128]{2,1,0:T(8,128)(2,1)}, u32[]{:S(2)}, u32[]{:S(2)}) async-start(bf16[16,576,128]{2,1,0:T(8,128)(2,1)} %pad_maximum_fusion.1), calls=%async_computation | async-start | bytes 4718592 | tf_op jit(solution)/shard_map/all_to_all | solution.py:113
  30.5 31.5 %all-to-all-done = bf16[16,576,128]{2,1,0:T(8,128)(2,1)} async-done(((bf16[16,576,128]{2,1,0:T(8,128)(2,1)}), bf16[16,576,128]{2,1,0:T(8,128)(2,1)}, u32[]{:S(2)}, u32[]{:S(2)}) %all-to-all-start) | async-done | bytes 2359328 | tf_op jit(solution)/shard_map/all_to_all | solution.py:113
  62.0 2.1 broadcast_in_dim.44
  64.1 4.7 %all-to-all-start.2 = ((bf16[16,96,1024]{2,1,0:T(8,128)(2,1)}), bf16[16,96,1024]{2,1,0:T(8,128)(2,1)}, u32[]{:S(2)}, u32[]{:S(2)}) async-start(bf16[16,96,1024]{2,1,0:T(8,128)(2,1)} %bitcast.121), calls=%async_computation.2 | async-start | bytes 6291456 | tf_op jit(solution)/shard_map/all_to_all | solution.py:117
  68.8 0.6 compare_select_fusion.bias_ref
  69.4 1.5 slice.61
  70.9 1.0 copy.70
  71.9 1.2 slice.58
  73.1 0.5 copy.69
  73.8 0.8 copy.50
  74.6 0.3 fusion.27
  74.9 1.1 copy.53
  76.0 0.8 copy.49
  76.9 1.1 copy.52
  77.9 24.8 %shard_map.84 = (bf16[1536,128]{1,0:T(8,128)(2,1)}, bf16[1536,128]{1,0:T(8,128)(2,1)}, f32[3072,128]{1,0:T(8,128)}, f32[3072,128]{1,0:T(8,128)}) custom-call(bf16[1536,128]{1,0:T(8,128)(2,1)} %bitcast.145, bf16[1536,128]{1,0:T(8,128)(2,1)} %bitcast.144, bf16[3072,128]{1,0:T(8,128)(2,1)} %bitcast.138, bf16[3072,128]{1,0:T(8,128)(2,1)} %bitcast.137, ...), custom_call_target="tpu_custom_call" | custom-call | tf_op jit(solution)/shard_map/pallas_call | solution.py:56
  102.7 1.5 fusion.14
  104.2 1.1 collective-permute-start
  105.3 15.3 %collective-permute-done = bf16[16,96,2,128]{3,1,2,0:T(8,128)(2,1)} collective-permute-done((bf16[16,96,2,128]{3,1,2,0:T(8,128)(2,1)S(1)}, bf16[16,96,2,128]{3,1,2,0:T(8,128)(2,1)}, u32[]{:S(2)}, u32[]{:S(2)}) %collective-permute-start) | collective-permute-done | bytes 786464 | tf_op jit(solution)/shard_map/ppermute | solution.py:13
  120.6 1.8 fusion.3
  122.5 1.3 pad_maximum_fusion.2
  123.8 8.8 %all-to-all-start.1 = ((bf16[16,96,4,128]{3,1,2,0:T(8,128)(2,1)}), bf16[16,96,4,128]{3,1,2,0:T(8,128)(2,1)}, u32[]{:S(2)}, u32[]{:S(2)}) async-start(bf16[16,96,4,128]{3,1,2,0:T(8,128)(2,1)} %pad_maximum_fusion.2), calls=%async_computation.1 | async-start | bytes 3145728 | tf_op jit(solution)/shard_map/all_to_all | solution.py:144
  132.6 0.3 all-gather.2.cloned.1.call-start
  132.9 4.6 %copy.59 = bf16[1024,1536]{1,0:T(8,128)(2,1)} copy(bf16[1024,1536]{0,1:T(8,128)(2,1)} %bitcast.29) | data formatting | bytes 6291456 | tf_op jit(solution)/shard_map/dot_general | solution.py:151
  137.5 2.1 pad_maximum_fusion.3
  139.6 2.7 %copy.61 = bf16[16,96,3,128]{1,0,3,2:T(8,128)(2,1)} copy(bf16[16,96,3,128]{3,1,2,0:T(8,128)(2,1)} %pad_maximum_fusion.3) | data formatting | bytes 2359296 | tf_op jit(solution)/shard_map/concatenate | solution.py:150
  142.4 4.0 %reshape.174 = bf16[1536,384,1]{0,1,2:T(8,128)(2,1)} reshape(bf16[16,96,3,128]{1,0,3,2:T(8,128)(2,1)} %copy.61) | data formatting | bytes 2359296 | tf_op jit(solution)/shard_map/reshape | solution.py:152
  146.3 4.9 %convolution_convert_fusion.2 = bf16[16,64,384]{2,1,0:T(8,128)(2,1)} fusion(bf16[16,64,1536]{2,1,0:T(8,128)(2,1)} %bitcast.135, bf16[1536,384,1]{0,1,2:T(8,128)(2,1)} %reshape.174), kind=kOutput, calls=%fused_computation.18 | convolution fusion | flops 1208352768 | bytes 5111808 | tf_op jit(solution)/shard_map/dot_general | solution.py:151
  151.2 1.4 all-to-all-done.1
  152.7 2.4 copy.90
  155.1 1.2 copy-done.3
  156.3 0.9 copy.91
  157.2 1.2 copy.63
  158.4 0.8 convolution_convert_fusion.1
  159.2 0.3 copy-done.11
  159.5 0.3 pad_maximum_fusion
  159.9 38.0 %all_to_all.25 = bf16[16,64,1408]{2,1,0:T(8,128)(2,1)S(1)} all-to-all(bf16[16,64,1408]{2,1,0:T(8,128)(2,1)S(1)} %pad_maximum_fusion), channel_id=1, replica_groups=mesh['batch'=8,'seq'=16] {'seq'}, dimensions={0} | all-to-all | bytes 5767168 | tf_op jit(solution)/shard_map/all_to_all | solution.py:157
  197.8 1.6 copy-done.1
  199.4 1.3 slice.66
  200.7 3.6 %reshape.167 = f32[8,2,64,3,128]{4,3,2,1,0:T(4,128)} reshape(f32[16,64,384]{2,1,0:T(8,128)} %slice.66) | data formatting | bytes 3145728 | tf_op jit(solution)/shard_map/reshape | solution.py:161
  204.3 2.4 reduce_sum.69
  206.7 1.3 copy.64
  208.1 1.3 concatenate.28
  209.3 2.4 convert_element_type.99
  212.0 23.8 %all_to_all.26 = f32[8,8,4096]{2,1,0:T(8,128)S(1)} all-to-all(f32[8,8,4096]{2,1,0:T(8,128)S(1)} %pad_maximum_fusion.4), channel_id=1, replica_groups=mesh['batch'=8,'seq'=16] {'batch'}, dimensions={0} | all-to-all | bytes 2097152 | tf_op jit(solution)/shard_map/all_to_all | solution.py:169
  235.8 0.7 reduce_sum.71
  236.5 2.5 slice.65
  239.0 3.0 %reshape.163 = bf16[192,3072]{1,0:T(8,128)(2,1)} reshape(bf16[2,96,3,8,128]{4,3,2,1,0:T(8,128)(2,1)} %slice.65) | data formatting | bytes 2359296 | tf_op jit(solution)/shard_map/reshape | solution.py:147
  242.0 5.6 %multiply_reduce_fusion = (f32[192]{0:T(256)S(1)}, f32[192,1024]{1,0:T(8,128)S(1)}) fusion(bf16[1,192,1024]{2,1,0:T(8,128)(2,1)S(1)} %copy-done.2, f32[192]{0:T(256)S(1)} %broadcast_multiply_fusion, bf16[192,3072]{1,0:T(8,128)(2,1)} %reshape.163, bf16[1024,3072]{1,0:T(8,128)(2,1)} %param.7), kind=kOutput, calls=%fused_computation.40 | convolution fusion | flops 1208745728 | bytes 8652288 | tf_op jit(solution)/shard_map/dot_general | solution.py:175
  247.7 0.4 fusion.26
  248.0 1.3 fusion.7
  249.4 1.1 fusion.17
  250.5 6.4 %all-gather.2.cloned.1.call-done = f32[64,4096]{1,0:T(8,128)} async-done(((f32[8,4096]{1,0:T(8,128)}), f32[64,4096]{1,0:T(8,128)}) %all-gather.2.cloned.1.call-update) | async-done | bytes 1048592 | tf_op jit(solution)/shard_map/all_gather | solution.py:172
  256.8 1.7 slice.69
  258.5 2.1 slice.68
  (40 shorter events, 1.4 us)
Async XLA Ops:
  7.2 8.8 %copy-start = (bf16[1024,1024]{1,0:T(8,128)(2,1)S(1)}, bf16[1024,1024]{1,0:T(8,128)(2,1)}, u32[]{:S(2)}) copy-start(bf16[1024,1024]{1,0:T(8,128)(2,1)} %param.8) | copy-start | bytes 6291460
  14.4 1.6 copy-start.4
  16.8 1.0 copy-start.10
  21.5 8.8 %copy-start.2 = (bf16[1,192,1024]{2,1,0:T(8,128)(2,1)S(1)}, bf16[1,192,1024]{2,1,0:T(8,128)(2,1)}, u32[]{:S(2)}) copy-start(bf16[1,192,1024]{2,1,0:T(8,128)(2,1)} %param.5) | copy-start | bytes 1179652
  21.5 40.5 %all-to-all-start = ((bf16[16,576,128]{2,1,0:T(8,128)(2,1)}), bf16[16,576,128]{2,1,0:T(8,128)(2,1)}, u32[]{:S(2)}, u32[]{:S(2)}) async-start(bf16[16,576,128]{2,1,0:T(8,128)(2,1)} %pad_maximum_fusion.1), calls=%async_computation | async-start | bytes 4718592 | tf_op jit(solution)/shard_map/all_to_all | solution.py:113
  64.1 59.7 %all-to-all-start.2 = ((bf16[16,96,1024]{2,1,0:T(8,128)(2,1)}), bf16[16,96,1024]{2,1,0:T(8,128)(2,1)}, u32[]{:S(2)}, u32[]{:S(2)}) async-start(bf16[16,96,1024]{2,1,0:T(8,128)(2,1)} %bitcast.121), calls=%async_computation.2 | async-start | bytes 6291456 | tf_op jit(solution)/shard_map/all_to_all | solution.py:117
  104.2 16.4 %collective-permute-start = (bf16[16,96,2,128]{3,1,2,0:T(8,128)(2,1)S(1)}, bf16[16,96,2,128]{3,1,2,0:T(8,128)(2,1)}, u32[]{:S(2)}, u32[]{:S(2)}) collective-permute-start(bf16[16,96,2,128]{3,1,2,0:T(8,128)(2,1)S(1)} %fusion.14), channel_id=1, source_target_pairs={{0,1},{1,0},{2,3},{3,2},{4,5},{5,4},{6,7},{7,6},{8,9},{9,8},{10,11... | collective-permute-start | bytes 2359304 | tf_op jit(solution)/shard_map/ppermute | solution.py:13
  105.3 17.2 %copy-start.7 = (bf16[1536,128]{1,0:T(8,128)(2,1)S(1)}, bf16[1536,128]{1,0:T(8,128)(2,1)}, u32[]{:S(2)}) copy-start(bf16[1536,128]{1,0:T(8,128)(2,1)} %get-tuple-element.9) | copy-start | bytes 1179652
  105.3 17.2 %copy-start.12 = (bf16[1536,128]{1,0:T(8,128)(2,1)S(1)}, bf16[1536,128]{1,0:T(8,128)(2,1)}, u32[]{:S(2)}) copy-start(bf16[1536,128]{1,0:T(8,128)(2,1)} %get-tuple-element.8) | copy-start | bytes 1179652
  123.8 28.9 %all-to-all-start.1 = ((bf16[16,96,4,128]{3,1,2,0:T(8,128)(2,1)}), bf16[16,96,4,128]{3,1,2,0:T(8,128)(2,1)}, u32[]{:S(2)}, u32[]{:S(2)}) async-start(bf16[16,96,4,128]{3,1,2,0:T(8,128)(2,1)} %pad_maximum_fusion.2), calls=%async_computation.1 | async-start | bytes 3145728 | tf_op jit(solution)/shard_map/all_to_all | solution.py:144
  132.6 124.2 %all-gather.2.cloned.1.call-start = ((), (), s32[]{:S(2)}) async-start(), calls=%async_computation.5 | async-start | bytes 1179648 | tf_op jit(solution)/shard_map/all_gather | solution.py:172
  155.1 1.2 copy-start.3
  155.1 3.3 %copy-start.5 = (bf16[1,192,1024]{2,1,0:T(8,128)(2,1)S(1)}, bf16[1,192,1024]{2,1,0:T(8,128)(2,1)}, u32[]{:S(2)}) copy-start(bf16[1,192,1024]{2,1,0:T(8,128)(2,1)} %param.9) | copy-start | bytes 1179652
  156.3 0.9 copy-start.8
  158.4 1.1 copy-start.11
  197.8 1.6 copy-start.1
  242.0 6.0 %copy-start.9 = (bf16[2,96,1,8,128]{4,3,2,1,0:T(8,128)(2,1)S(1)}, bf16[2,96,1,8,128]{4,3,2,1,0:T(8,128)(2,1)}, u32[]{:S(2)}) copy-start(bf16[2,96,1,8,128]{4,3,2,1,0:T(8,128)(2,1)} %copy-done.8) | copy-start | bytes 1179652
  248.0 1.4 copy-start.6
Sparse Core Ops, SparseCore 0:
  236.6 20.1 all-gather.1

commit v6 on v5

v6 whole, which is shorter than its diff:
```python
import jax
import jax.numpy as jnp
from jax import lax
from jax.sharding import PartitionSpec as P
from jax.experimental import pallas as pl
from jax.experimental.pallas import tpu as pltpu
import functools

H = 8


def from_partner(array, axis, stride):
    return lax.ppermute(array, axis, [(i, i ^ 1 << stride) for i in range(lax.axis_size(axis))])


def layer_norm(values):
    mean = jnp.mean(values, axis=-1, keepdims=True)
    centred = values - mean
    var = jnp.mean(centred * centred, axis=-1, keepdims=True)
    return centred * lax.rsqrt(var + 1e-05)


def _attn_kernel(q_ref, do_ref, k_ref, v_ref, bias_ref, ctx_ref, dq_ref, dk_ref, dv_ref, *, scale):
    i = pl.program_id(0)

    @pl.when(i == 0)
    def _():
        dk_ref[...] = jnp.zeros_like(dk_ref)
        dv_ref[...] = jnp.zeros_like(dv_ref)

    nb, rows, hd = q_ref.shape
    ns, kr, _ = k_ref.shape
    q = q_ref[...].reshape(nb * rows, hd)
    do = do_ref[...].reshape(nb * rows, hd)
    k = k_ref[...].reshape(ns * kr, hd)
    v = v_ref[...].reshape(ns * kr, hd)
    nt = (((1,), (1,)), ((), ()))
    tn = (((0,), (0,)), ((), ()))
    s = lax.dot_general(q, k, nt, preferred_element_type=jnp.float32) * scale + bias_ref[...]
    m = jnp.max(s, axis=1, keepdims=True)
    e = jnp.exp(s - m)
    p = e / jnp.sum(e, axis=1, keepdims=True)
    p16 = p.astype(jnp.bfloat16)
    ctx = jnp.dot(p16, v, preferred_element_type=jnp.float32)
    ctx_ref[...] = ctx.reshape(nb, rows, hd).astype(ctx_ref.dtype)
    dp = lax.dot_general(do, v, nt, preferred_element_type=jnp.float32)
    delta = jnp.sum(p * dp, axis=1, keepdims=True)
    ds = (p * (dp - delta)).astype(jnp.bfloat16)
    dq = jnp.dot(ds, k, preferred_element_type=jnp.float32) * scale
    dq_ref[...] = dq.reshape(nb, rows, hd).astype(dq_ref.dtype)
    dk_ref[...] += lax.dot_general(ds, q, tn, preferred_element_type=jnp.float32) * scale
    dv_ref[...] += lax.dot_general(p16, do, tn, preferred_element_type=jnp.float32)


def attn_pass(recv, part_rows, bias, scale, block_sources=2):
    sources, _, hd = recv.shape
    key_rows = 2 * part_rows
    nq = sources * part_rows
    nk = sources * key_rows
    kernel = functools.partial(_attn_kernel, scale=scale)
    return pl.pallas_call(
        kernel,
        grid=(sources // block_sources,),
        in_specs=[
            pl.BlockSpec((block_sources, part_rows, hd), lambda i: (i, 0, 0)),
            pl.BlockSpec((block_sources, part_rows, hd), lambda i: (i, 1, 0)),
            pl.BlockSpec((sources, key_rows, hd), lambda i: (0, 1, 0)),
            pl.BlockSpec((sources, key_rows, hd), lambda i: (0, 2, 0)),
            pl.BlockSpec((1, nk), lambda i: (0, 0)),
        ],
        out_specs=[
            pl.BlockSpec((block_sources, part_rows, hd), lambda i: (i, 0, 0)),
            pl.BlockSpec((block_sources, part_rows, hd), lambda i: (i, 0, 0)),
            pl.BlockSpec((nk, hd), lambda i: (0, 0)),
            pl.BlockSpec((nk, hd), lambda i: (0, 0)),
        ],
        out_shape=[
            jax.ShapeDtypeStruct((sources, part_rows, hd), jnp.bfloat16),
            jax.ShapeDtypeStruct((sources, part_rows, hd), jnp.bfloat16),
            jax.ShapeDtypeStruct((nk, hd), jnp.float32),
            jax.ShapeDtypeStruct((nk, hd), jnp.float32),
        ],
        compiler_params=pltpu.CompilerParams(dimension_semantics=("arbitrary",)),
    )(recv, recv, recv, recv, bias.reshape(1, nk))


def per_device(frames, lengths, w_qkv, w_out, cotangent):
    width = w_out.shape[0]
    head_size = width // H
    scale = float(head_size) ** (-0.5)
    tok_rows = frames.shape[1]
    seq_count = lax.axis_size("seq")
    groups = seq_count // H
    part_rows = tok_rows // groups
    frame_total = tok_rows * seq_count
    group_index = lax.axis_index("seq") % groups
    length = lengths[0]
    inputs = frames[0].astype(jnp.float32)
    normed = layer_norm(inputs).astype(jnp.bfloat16)
    qkv = jnp.dot(normed, w_qkv, preferred_element_type=jnp.float32).astype(jnp.bfloat16)
    qkv_local = qkv.reshape(tok_rows, 3, H, head_size)
    offset = lax.axis_index("seq") * tok_rows
    own_pos = offset + jnp.arange(tok_rows, dtype=jnp.int32)
    valid = (own_pos < length).astype(jnp.float32)
    grad_rows = (cotangent[0].astype(jnp.float32) * valid[:, None]).astype(jnp.bfloat16)
    dcontext = jnp.dot(grad_rows, w_out.T, preferred_element_type=jnp.float32).astype(jnp.bfloat16)

    def by_half(rows_heads):
        return rows_heads.reshape(groups, part_rows, H, head_size).transpose(2, 0, 1, 3).reshape(
            seq_count, part_rows, head_size
        )

    def to_both(rows_heads):
        both = jnp.broadcast_to(rows_heads.transpose(1, 0, 2)[:, None], (H, groups, tok_rows, head_size))
        return both.reshape(seq_count, tok_rows, head_size)

    send = jnp.concatenate(
        [
            by_half(qkv_local[:, 0]),
            by_half(dcontext.reshape(tok_rows, H, head_size)),
            to_both(qkv_local[:, 1]),
            to_both(qkv_local[:, 2]),
        ],
        axis=1,
    )
    recv = lax.all_to_all(send, "seq", split_axis=0, concat_axis=0, tiled=True)
    normed_send = jnp.broadcast_to(normed.reshape(1, groups, part_rows, width), (H, groups, part_rows, width))
    normed_recv = lax.all_to_all(
        normed_send.reshape(seq_count, part_rows, width), "seq", split_axis=0, concat_axis=0, tiled=True
    )
    position = jnp.arange(frame_total, dtype=jnp.int32)
    bias = jnp.where(position < length, 0.0, -1000000000.0).astype(jnp.float32)

    context_h, dquery, dkeys, dvalues = attn_pass(recv, part_rows, bias, scale)

    split_grads = jnp.stack([dkeys, dvalues], axis=1).reshape(seq_count, groups, part_rows, 2, head_size)
    own_half = lax.dynamic_index_in_dim(split_grads, group_index, 1, keepdims=False)
    other_half = lax.dynamic_index_in_dim(split_grads, 1 - group_index, 1, keepdims=False)
    partner_half = from_partner(other_half.astype(jnp.bfloat16), "seq", 0)
    paired_rows = (own_half + partner_half.astype(jnp.float32)).astype(jnp.bfloat16)
    back = jnp.concatenate(
        [
            context_h.reshape(seq_count, part_rows, 1, head_size),
            dquery.reshape(seq_count, part_rows, 1, head_size),
            paired_rows,
        ],
        axis=2,
    )
    returned = lax.all_to_all(back, "seq", split_axis=0, concat_axis=0, tiled=True)
    returned = returned.reshape(H, groups, part_rows, 4, head_size).transpose(1, 2, 3, 0, 4)
    context = returned[:, :, 0].reshape(tok_rows, width)
    dqkv = returned[:, :, 1:].reshape(tok_rows, 3 * width)
    branch = jnp.dot(context, w_out, preferred_element_type=jnp.float32)
    output = (inputs + valid[:, None] * branch).astype(jnp.bfloat16)
    over_frames = (((0, 1), (0, 1)), ((), ()))
    qkv_part = jnp.stack(
        [
            lax.dot_general(normed_recv, piece, over_frames, preferred_element_type=jnp.float32)
            for piece in (dquery, paired_rows[:, :, 0], paired_rows[:, :, 1])
        ],
        axis=1,
    ).reshape(width, 3 * head_size)
    out_part = jnp.dot(context.T, grad_rows, preferred_element_type=jnp.float32)
    share_rows = width // seq_count
    parts = jnp.concatenate([qkv_part, out_part], axis=1).astype(jnp.bfloat16)
    gathered = lax.all_to_all(
        parts.reshape(seq_count, share_rows, parts.shape[1]), "seq", split_axis=0, concat_axis=0, tiled=True
    )
    qkv_rows = (
        jnp.sum(gathered[:, :, : 3 * head_size].astype(jnp.float32).reshape(H, groups, share_rows, 3 * head_size), axis=1)
        .reshape(H, share_rows, 3, head_size)
        .transpose(1, 2, 0, 3)
        .reshape(share_rows, 3 * width)
    )
    out_rows = jnp.sum(gathered[:, :, 3 * head_size :].astype(jnp.float32), axis=0)
    batch_count = lax.axis_size("batch")
    piece_rows = share_rows // batch_count
    shares = jnp.concatenate([qkv_rows, out_rows], axis=1).astype(jnp.bfloat16)
    pieces = lax.all_to_all(
        shares.reshape(batch_count, piece_rows, shares.shape[1]), "batch", split_axis=0, concat_axis=0, tiled=True
    )
    summed = jnp.sum(pieces.astype(jnp.float32), axis=0)
    grad_qkv, grad_out = lax.all_gather(
        (summed[:, : 3 * width], summed[:, 3 * width :]), "batch", axis=0, tiled=True
    )
    dnormed = jnp.dot(dqkv, w_qkv.T, preferred_element_type=jnp.float32)
    unused, pull = jax.vjp(layer_norm, inputs)
    grad_input = (cotangent[0].astype(jnp.float32) + pull(dnormed)[0]).astype(jnp.bfloat16)
    return (output[None], grad_input[None], grad_qkv, grad_out)


def solution(mesh):
    return jax.shard_map(
        per_device,
        mesh=mesh,
        in_specs=(P("batch", "seq", None), P("batch"), P(), P(), P("batch", "seq", None)),
        out_specs=(
            P("batch", "seq", None),
            P("batch", "seq", None),
            P("seq", None),
            P("seq", None),
        ),
        check_vma=False,
    )
```

time: 269 us -> 254 us (0.944)
  waiting for transfers between devices: 54.6 us -> 91.9 us
  blocking collectives: 61.7 us -> 27 us
  local copies, waits for them, and re-layouts: 50.6 us -> 25.3 us
  starting transfers between devices: 23.4 us -> 38.8 us
  between operations: 15.1 us -> 1.66 us
  matrix products: 17.9 us -> 21.7 us
  Pallas kernels: 24.8 us -> 28.1 us
    all_to_all x2 -> x0, blocking collectives: 61.7 us -> none  [the longest x1 38 us: per_device(): lax.all_to_all(parts.reshape(seq_count, share_rows, parts.shape[1]), 'seq...]
    all_gather x0 -> x2, blocking collectives: none -> 27 us  [per_device(): lax.all_gather((summed[:, :3 * width], summed[:, 3 * width:]), 'batch', a...]
    all_to_all x1 -> x3, waiting for transfers between devices: 31.5 us -> 58.4 us  [the longest x1 31.5 us: per_device(): recv = lax.all_to_all(send, 'seq', split_axis=0, concat_axis=0, tiled=True)]
    all_to_all x1 -> x3, starting transfers between devices: 8.59 us -> 23.9 us  [the longest x1 10.8 us: per_device(): lax.all_to_all(shares.reshape(batch_count, piece_rows, shares.shape[1]),...]
    slice x11 -> x2, local copies, waits for them, and re-layouts: 12 us -> 0.01 us  [the longest x1 0.01 us: per_device(): summed[:, :3 * width]]
    all_to_all x1, waiting for transfers between devices: 1.43 us -> 11.2 us  [per_device(): lax.all_to_all(back, 'seq', split_axis=0, concat_axis=0, tiled=True)]
    ppermute x1, waiting for transfers between devices: 15.3 us -> 22.4 us  [from_partner(): lax.ppermute(array, axis, [(i, i ^ 1 << stride) for i in range(lax.axis_s...]
    all_gather x1 -> x0, waiting for transfers between devices: 6.38 us -> none  [per_device(): lax.all_gather(jnp.sum(pieces, axis=0), 'batch', axis=0, tiled=True)]
  transfers between devices with their start and end apart: 5 -> 6, of which waited for: 4 -> 5; matrix products, arithmetic and copies ran while one was open for 17% -> 13% of each run, Pallas kernels for 9% -> 11%
where the time goes in v6:
time: 254 us; the launch traced here: 252 us
  waiting for transfers between devices  91.9 us (36%)
  starting transfers between devices  38.8 us (15%)
  Pallas kernels  28.1 us (11%)
  blocking collectives  27 us (11%)
  local copies, waits for them, and re-layouts  25.3 us (10%)
  matrix products  21.7 us (9%)
  other arithmetic  17.9 us (7%)
    all_to_all x1, waiting for transfers between devices, per_device(): recv = lax.all_to_all(send, 'seq', split_axis=0, concat_axis=0, tiled=True)  31.5 us
    pallas_call x1, Pallas kernels, attn_pass(): pl.pallas_call(kernel, grid=(sources // block_sources,), in_specs=[pl.Blo...  28.1 us
    all_gather x2, blocking collectives, per_device(): lax.all_gather((summed[:, :3 * width], summed[:, 3 * width:]), 'batch', a...  27 us
    ppermute x1, waiting for transfers between devices, from_partner(): lax.ppermute(array, axis, [(i, i ^ 1 << stride) for i in range(lax.axis_s...  22.4 us
    all_to_all x1, waiting for transfers between devices, per_device(): lax.all_to_all(parts.reshape(seq_count, share_rows, parts.shape[1]), 'seq...  19.7 us
    all_to_all x1, waiting for transfers between devices, per_device(): lax.all_to_all(back, 'seq', split_axis=0, concat_axis=0, tiled=True)  11.2 us
    all_to_all x1, starting transfers between devices, per_device(): lax.all_to_all(shares.reshape(batch_count, piece_rows, shares.shape[1]),...  10.8 us
    all_to_all x1, starting transfers between devices, per_device(): lax.all_to_all(back, 'seq', split_axis=0, concat_axis=0, tiled=True)  9.22 us
  transfers between devices with their start and end apart: 6, of which 5 were waited for; matrix products, arithmetic and copies ran while one was open for 13% of the time, Pallas kernels for 11%

profile of v6, /device:TPU:1, one launch (start us, length us, event | category | flops | bytes accessed | tf_op | source)
XLA Modules:
  0.0 252.5 jit_solution(8552047102157223005)
XLA Ops:
  0.6 1.3 convert_reduce_fusion.1
  1.9 1.2 multiply_reduce_fusion.1
  3.2 4.4 %fusion.7 = bf16[24,8,24,128]{3,1,2,0:T(8,128)(2,1)S(1)} fusion(bf16[1024,3072]{1,0:T(8,128)(2,1)} %param.7, bf16[1,192,1024]{2,1,0:T(8,128)(2,1)} %param.5, f32[192]{0:T(256)S(1)} %fusion.34, f32[192]{0:T(256)S(1)} %broadcast_multiply_fusion), kind=kOutput, calls=%fused_computation.18 | convolution fusion | flops 1209335808 | bytes 7865856 | tf_op jit(solution)/shard_map/dot_general | solution.py:100
  7.6 0.2 copy.39
  7.8 0.2 fusion.36
  8.1 0.1 copy.27
  8.1 0.8 copy.28
  9.7 0.9 fusion.11
  10.6 0.1 copy.40
  10.7 0.1 broadcast_in_dim.22
  10.8 0.1 broadcast_in_dim.23
  11.0 1.6 pad_maximum_fusion.1
  12.6 8.6 %all-to-all-start = ((bf16[16,576,128]{2,1,0:T(8,128)(2,1)}), bf16[16,576,128]{2,1,0:T(8,128)(2,1)}, u32[]{:S(2)}, u32[]{:S(2)}) async-start(bf16[16,576,128]{2,1,0:T(8,128)(2,1)} %pad_maximum_fusion.1), calls=%async_computation | async-start | bytes 4718592 | tf_op jit(solution)/shard_map/all_to_all | solution.py:126
  21.2 0.1 rsqrt.16
  21.3 0.1 div.27
  21.4 0.2 multiply_convert_fusion
  21.6 31.5 %all-to-all-done.q_ref.do_ref.k_ref.v_ref = bf16[16,576,128]{2,1,0:T(8,128)(2,1)} async-done(((bf16[16,576,128]{2,1,0:T(8,128)(2,1)}), bf16[16,576,128]{2,1,0:T(8,128)(2,1)}, u32[]{:S(2)}, u32[]{:S(2)}) %all-to-all-start) | async-done | bytes 2359328 | tf_op jit(solution)/shard_map/all_to_all | solution.py:126
  53.1 2.1 broadcast_in_dim.51
  55.2 4.5 %all-to-all-start.2 = ((bf16[16,96,1024]{2,1,0:T(8,128)(2,1)}), bf16[16,96,1024]{2,1,0:T(8,128)(2,1)}, u32[]{:S(2)}, u32[]{:S(2)}) async-start(bf16[16,96,1024]{2,1,0:T(8,128)(2,1)} %bitcast.152), calls=%async_computation.2 | async-start | bytes 6291456 | tf_op jit(solution)/shard_map/all_to_all | solution.py:128
  59.7 0.6 compare_select_fusion.bias_ref
  60.3 28.1 %shard_map.84 = (bf16[16,96,128]{2,1,0:T(8,128)(2,1)}, bf16[16,96,128]{2,1,0:T(8,128)(2,1)}, f32[3072,128]{1,0:T(8,128)}, f32[3072,128]{1,0:T(8,128)}) custom-call(bf16[16,576,128]{2,1,0:T(8,128)(2,1)} %all-to-all-done.q_ref.do_ref.k_ref.v_ref, bf16[16,576,128]{2,1,0:T(8,128)(2,1)} %all-to-all-done.q_ref.do_ref.k_ref.v_ref, ...), custom_call_target="tpu_custom_call" | custom-call | tf_op jit(solution)/shard_map/pallas_call | solution.py:61
  88.4 1.5 fusion.23
  89.9 1.3 collective-permute-start
  91.1 22.4 %collective-permute-done = bf16[16,96,2,128]{3,1,0,2:T(8,128)(2,1)} collective-permute-done((bf16[16,96,2,128]{3,1,0,2:T(8,128)(2,1)S(1)}, bf16[16,96,2,128]{3,1,0,2:T(8,128)(2,1)}, u32[]{:S(2)}, u32[]{:S(2)}) %collective-permute-start) | collective-permute-done | bytes 786464 | tf_op jit(solution)/shard_map/ppermute | solution.py:13
  113.6 1.8 fusion.6
  115.4 0.2 pad_maximum_fusion.2
  115.5 1.3 copy.31
  116.8 9.2 %all-to-all-start.1 = ((bf16[16,96,4,128]{3,1,2,0:T(8,128)(2,1)}), bf16[16,96,4,128]{3,1,2,0:T(8,128)(2,1)}, u32[]{:S(2)}, u32[]{:S(2)}) async-start(bf16[16,96,4,128]{3,1,2,0:T(8,128)(2,1)} %copy.31), calls=%async_computation.1 | async-start | bytes 3145728 | tf_op jit(solution)/shard_map/all_to_all | solution.py:149
  126.1 3.0 %fusion.17 = bf16[1024,1,128]{2,0,1:T(8,128)(2,1)S(1)} fusion(bf16[16,96,1024]{2,1,0:T(8,128)(2,1)} %all-to-all-done.2, bf16[16,96,128]{2,1,0:T(8,128)(2,1)} %get-tuple-element.9), kind=kOutput, calls=%fused_computation.34 | convolution fusion | flops 402784256 | bytes 3801088 | tf_op jit(solution)/shard_map/dot_general | solution.py:158
  129.1 2.9 %fusion.15 = bf16[1024,1,128]{2,0,1:T(8,128)(2,1)S(1)} fusion(bf16[16,96,1024]{2,1,0:T(8,128)(2,1)} %all-to-all-done.2, bf16[16,96,2,128]{3,1,0,2:T(8,128)(2,1)S(1)} %fusion.6), kind=kOutput, calls=%fused_computation.32 | convolution fusion | flops 402784256 | bytes 3801088 | tf_op jit(solution)/shard_map/dot_general | solution.py:158
  132.0 2.9 %fusion.16 = bf16[1024,1,128]{2,0,1:T(8,128)(2,1)S(1)} fusion(bf16[16,96,1024]{2,1,0:T(8,128)(2,1)} %all-to-all-done.2, bf16[16,96,2,128]{3,1,0,2:T(8,128)(2,1)S(1)} %fusion.6), kind=kOutput, calls=%fused_computation.33 | convolution fusion | flops 402784256 | bytes 3801088 | tf_op jit(solution)/shard_map/dot_general | solution.py:158
  134.9 0.1 pad_maximum_fusion.3
  135.0 0.7 copy.33
  135.7 1.4 concatenate.25
  137.1 11.2 %all-to-all-done.1 = bf16[16,96,4,128]{3,1,2,0:T(8,128)(2,1)} async-done(((bf16[16,96,4,128]{3,1,2,0:T(8,128)(2,1)}), bf16[16,96,4,128]{3,1,2,0:T(8,128)(2,1)}, u32[]{:S(2)}, u32[]{:S(2)}) %all-to-all-start.1) | async-done | bytes 1572896 | tf_op jit(solution)/shard_map/all_to_all | solution.py:149
  148.3 2.5 copy.48
  150.8 1.2 copy-done.2
  152.0 0.9 copy.49
  152.9 1.2 copy.34
  154.1 0.8 convolution_convert_fusion.1
  154.9 0.3 copy-done.6
  155.2 1.9 pad_maximum_fusion
  157.2 4.5 %all-to-all-start.3 = ((bf16[16,64,1408]{2,1,0:T(8,128)(2,1)}), bf16[16,64,1408]{2,1,0:T(8,128)(2,1)}, u32[]{:S(2)}, u32[]{:S(2)}) async-start(bf16[16,64,1408]{2,1,0:T(8,128)(2,1)} %pad_maximum_fusion), calls=%async_computation.3 | async-start | bytes 5767168 | tf_op jit(solution)/shard_map/all_to_all | solution.py:166
  161.6 2.5 %slice.48 = bf16[2,96,3,8,128]{4,3,2,1,0:T(8,128)(2,1)} slice(bf16[2,96,4,8,128]{4,3,2,1,0:T(8,128)(2,1)} %bitcast.159), slice={[0:2], [0:96], [1:4], [0:8], [0:128]} | slice | bytes 2359296 | tf_op jit(solution)/shard_map/slice | solution.py:152
  164.2 3.0 %reshape.164 = bf16[192,3072]{1,0:T(8,128)(2,1)} reshape(bf16[2,96,3,8,128]{4,3,2,1,0:T(8,128)(2,1)} %slice.48) | data formatting | bytes 2359296 | tf_op jit(solution)/shard_map/reshape | solution.py:152
  167.2 5.5 %multiply_reduce_fusion = (f32[192]{0:T(256)S(1)}, f32[192,1024]{1,0:T(8,128)S(1)}) fusion(bf16[1,192,1024]{2,1,0:T(8,128)(2,1)S(1)} %copy-done.1, f32[192]{0:T(256)S(1)} %broadcast_multiply_fusion, bf16[192,3072]{1,0:T(8,128)(2,1)} %reshape.164, bf16[1024,3072]{1,0:T(8,128)(2,1)} %param.7), kind=kOutput, calls=%fused_computation.48 | convolution fusion | flops 1208745728 | bytes 8652288 | tf_op jit(solution)/shard_map/dot_general | solution.py:186
  172.7 0.9 copy-done.5
  173.5 0.3 fusion.35
  173.9 1.3 fusion.10
  175.2 19.7 %all-to-all-done.3 = bf16[16,64,1408]{2,1,0:T(8,128)(2,1)} async-done(((bf16[16,64,1408]{2,1,0:T(8,128)(2,1)}), bf16[16,64,1408]{2,1,0:T(8,128)(2,1)}, u32[]{:S(2)}, u32[]{:S(2)}) %all-to-all-start.3) | async-done | bytes 2883616 | tf_op jit(solution)/shard_map/all_to_all | solution.py:166
  195.0 2.1 bitcast_reduce_fusion
  197.1 1.4 reshape.168
  198.5 1.2 copy.35
  199.7 1.2 concatenate.27
  200.8 1.9 slice_reduce_fusion
  202.8 0.8 pad_maximum_fusion.4
  203.6 10.8 %all-to-all-start.4 = ((bf16[8,8,4096]{2,1,0:T(8,128)(2,1)}), bf16[8,8,4096]{2,1,0:T(8,128)(2,1)S(1)}, u32[]{:S(2)}, u32[]{:S(2)}) async-start(bf16[8,8,4096]{2,1,0:T(8,128)(2,1)} %pad_maximum_fusion.4), calls=%async_computation.4 | async-start | bytes 1048576 | tf_op jit(solution)/shard_map/all_to_all | solution.py:179
  214.4 2.2 fusion.26
  216.6 7.2 %all-to-all-done.4 = bf16[8,8,4096]{2,1,0:T(8,128)(2,1)S(1)} async-done(((bf16[8,8,4096]{2,1,0:T(8,128)(2,1)}), bf16[8,8,4096]{2,1,0:T(8,128)(2,1)S(1)}, u32[]{:S(2)}, u32[]{:S(2)}) %all-to-all-start.4) | async-done | bytes 524320 | tf_op jit(solution)/shard_map/all_to_all | solution.py:179
  223.8 0.1 convert_reduce_fusion
  223.9 14.2 %all_gather.6 = f32[64,3072]{1,0:T(8,128)S(1)} all-gather(f32[8,3072]{1,0:T(8,128)S(1)} %slice.53), channel_id=1, replica_groups=mesh['batch'=8,'seq'=16] {'batch'}, dimensions={0}, use_global_device_ids=true | all-gather | bytes 884736 | tf_op jit(solution)/shard_map/all_gather | solution.py:183
  238.1 12.8 %all_gather.7 = f32[64,1024]{1,0:T(8,128)S(1)} all-gather(f32[8,1024]{1,0:T(8,128)S(1)} %slice.54), channel_id=1, replica_groups=mesh['batch'=8,'seq'=16] {'batch'}, dimensions={0}, use_global_device_ids=true | all-gather | bytes 294912 | tf_op jit(solution)/shard_map/all_gather | solution.py:183
  250.9 0.9 copy.53
  251.8 0.7 copy.54
  (32 shorter events, 0.3 us)
Async XLA Ops:
  0.6 9.0 %copy-start = (bf16[1024,1024]{1,0:T(8,128)(2,1)S(1)}, bf16[1024,1024]{1,0:T(8,128)(2,1)}, u32[]{:S(2)}) copy-start(bf16[1024,1024]{1,0:T(8,128)(2,1)} %param.8) | copy-start | bytes 6291460
  7.8 1.8 copy-start.3
  9.7 1.2 copy-start.9
  12.6 8.8 %copy-start.1 = (bf16[1,192,1024]{2,1,0:T(8,128)(2,1)S(1)}, bf16[1,192,1024]{2,1,0:T(8,128)(2,1)}, u32[]{:S(2)}) copy-start(bf16[1,192,1024]{2,1,0:T(8,128)(2,1)} %param.5) | copy-start | bytes 1179652
  12.6 40.5 %all-to-all-start = ((bf16[16,576,128]{2,1,0:T(8,128)(2,1)}), bf16[16,576,128]{2,1,0:T(8,128)(2,1)}, u32[]{:S(2)}, u32[]{:S(2)}) async-start(bf16[16,576,128]{2,1,0:T(8,128)(2,1)} %pad_maximum_fusion.1), calls=%async_computation | async-start | bytes 4718592 | tf_op jit(solution)/shard_map/all_to_all | solution.py:126
  55.2 61.7 %all-to-all-start.2 = ((bf16[16,96,1024]{2,1,0:T(8,128)(2,1)}), bf16[16,96,1024]{2,1,0:T(8,128)(2,1)}, u32[]{:S(2)}, u32[]{:S(2)}) async-start(bf16[16,96,1024]{2,1,0:T(8,128)(2,1)} %bitcast.152), calls=%async_computation.2 | async-start | bytes 6291456 | tf_op jit(solution)/shard_map/all_to_all | solution.py:128
  89.9 23.7 %collective-permute-start = (bf16[16,96,2,128]{3,1,0,2:T(8,128)(2,1)S(1)}, bf16[16,96,2,128]{3,1,0,2:T(8,128)(2,1)}, u32[]{:S(2)}, u32[]{:S(2)}) collective-permute-start(bf16[16,96,2,128]{3,1,0,2:T(8,128)(2,1)S(1)} %fusion.23), channel_id=1, source_target_pairs={{0,1},{1,0},{2,3},{3,2},{4,5},{5,4},{6,7},{7,6},{8,9},{9,8},{10,11... | collective-permute-start | bytes 2359304 | tf_op jit(solution)/shard_map/ppermute | solution.py:13
  91.1 24.2 %copy-start.10 = (bf16[16,96,128]{2,1,0:T(8,128)(2,1)S(1)}, bf16[16,96,128]{2,1,0:T(8,128)(2,1)}, u32[]{:S(2)}) copy-start(bf16[16,96,128]{2,1,0:T(8,128)(2,1)} %get-tuple-element.9) | copy-start | bytes 1179652
  91.1 24.2 %copy-start.11 = (bf16[16,96,128]{2,1,0:T(8,128)(2,1)S(1)}, bf16[16,96,128]{2,1,0:T(8,128)(2,1)}, u32[]{:S(2)}) copy-start(bf16[16,96,128]{2,1,0:T(8,128)(2,1)} %get-tuple-element.8) | copy-start | bytes 1179652
  116.8 31.4 %all-to-all-start.1 = ((bf16[16,96,4,128]{3,1,2,0:T(8,128)(2,1)}), bf16[16,96,4,128]{3,1,2,0:T(8,128)(2,1)}, u32[]{:S(2)}, u32[]{:S(2)}) async-start(bf16[16,96,4,128]{3,1,2,0:T(8,128)(2,1)} %copy.31), calls=%async_computation.1 | async-start | bytes 3145728 | tf_op jit(solution)/shard_map/all_to_all | solution.py:149
  148.3 5.8 %copy-start.4 = (bf16[1,192,1024]{2,1,0:T(8,128)(2,1)S(1)}, bf16[1,192,1024]{2,1,0:T(8,128)(2,1)}, u32[]{:S(2)}) copy-start(bf16[1,192,1024]{2,1,0:T(8,128)(2,1)} %param.9) | copy-start | bytes 1179652
  150.8 1.2 copy-start.2
  152.0 0.9 copy-start.7
  154.1 1.1 copy-start.6
  157.2 37.8 %all-to-all-start.3 = ((bf16[16,64,1408]{2,1,0:T(8,128)(2,1)}), bf16[16,64,1408]{2,1,0:T(8,128)(2,1)}, u32[]{:S(2)}, u32[]{:S(2)}) async-start(bf16[16,64,1408]{2,1,0:T(8,128)(2,1)} %pad_maximum_fusion), calls=%async_computation.3 | async-start | bytes 5767168 | tf_op jit(solution)/shard_map/all_to_all | solution.py:166
  167.2 6.7 %copy-start.8 = (bf16[2,96,1,8,128]{4,3,2,1,0:T(8,128)(2,1)S(1)}, bf16[2,96,1,8,128]{4,3,2,1,0:T(8,128)(2,1)}, u32[]{:S(2)}) copy-start(bf16[2,96,1,8,128]{4,3,2,1,0:T(8,128)(2,1)} %copy-done.7) | copy-start | bytes 1179652
  172.7 0.9 copy-start.5
  203.6 20.2 %all-to-all-start.4 = ((bf16[8,8,4096]{2,1,0:T(8,128)(2,1)}), bf16[8,8,4096]{2,1,0:T(8,128)(2,1)S(1)}, u32[]{:S(2)}, u32[]{:S(2)}) async-start(bf16[8,8,4096]{2,1,0:T(8,128)(2,1)} %pad_maximum_fusion.4), calls=%async_computation.4 | async-start | bytes 1048576 | tf_op jit(solution)/shard_map/all_to_all | solution.py:179

commit v7 on v6

--- a/solution.py
+++ b/solution.py
@@ -52,7 +52,7 @@
     dv_ref[...] += lax.dot_general(p16, do, tn, preferred_element_type=jnp.float32)
 
 
-def attn_pass(recv, part_rows, bias, scale, block_sources=2):
+def attn_pass(recv, part_rows, bias, scale, block_sources=4):
     sources, _, hd = recv.shape
     key_rows = 2 * part_rows
     nq = sources * part_rows
@@ -180,9 +180,9 @@
         shares.reshape(batch_count, piece_rows, shares.shape[1]), "batch", split_axis=0, concat_axis=0, tiled=True
     )
     summed = jnp.sum(pieces.astype(jnp.float32), axis=0)
-    grad_qkv, grad_out = lax.all_gather(
-        (summed[:, : 3 * width], summed[:, 3 * width :]), "batch", axis=0, tiled=True
-    )
+    summed = lax.all_gather(summed, "batch", axis=0, tiled=True)
+    grad_qkv = summed[:, : 3 * width]
+    grad_out = summed[:, 3 * width :]
     dnormed = jnp.dot(dqkv, w_qkv.T, preferred_element_type=jnp.float32)
     unused, pull = jax.vjp(layer_norm, inputs)
     grad_input = (cotangent[0].astype(jnp.float32) + pull(dnormed)[0]).astype(jnp.bfloat16)

time: 254 us -> 255 us (level)
  blocking collectives: 27 us -> 55.2 us
  starting transfers between devices: 38.8 us -> 21.8 us
  waiting for transfers between devices: 91.9 us -> 75 us
  between operations: 1.66 us -> 15 us
  Pallas kernels: 28.1 us -> 22.9 us
  other arithmetic: 17.9 us -> 13.8 us
  local copies, waits for them, and re-layouts: 25.3 us -> 28.1 us
    all_to_all x0 -> x2, blocking collectives: none -> 55.2 us  [the longest x1 37.3 us: per_device(): lax.all_to_all(parts.reshape(seq_count, share_rows, parts.shape[1]), 'seq...]
    all_gather x2 -> x0, blocking collectives: 27 us -> none  [per_device(): lax.all_gather((summed[:, :3 * width], summed[:, 3 * width:]), 'batch', a...]
    all_to_all x2 -> x0, waiting for transfers between devices: 26.9 us -> none  [the longest x1 19.7 us: per_device(): lax.all_to_all(parts.reshape(seq_count, share_rows, parts.shape[1]), 'seq...]
    all_to_all x2 -> x0, starting transfers between devices: 15.3 us -> none  [the longest x1 10.8 us: per_device(): lax.all_to_all(shares.reshape(batch_count, piece_rows, shares.shape[1]),...]
    all_gather x0 -> x1, waiting for transfers between devices: none -> 6.39 us  [per_device(): summed = lax.all_gather(summed, 'batch', axis=0, tiled=True)]
    pallas_call x1, Pallas kernels: 28.1 us -> 22.9 us  [attn_pass(): pl.pallas_call(kernel, grid=(sources // block_sources,), in_specs=[pl.Blo...]
    ppermute x1, waiting for transfers between devices: 22.4 us -> 27.7 us  [from_partner(): lax.ppermute(array, axis, [(i, i ^ 1 << stride) for i in range(lax.axis_s...]
    slice x2, local copies, waits for them, and re-layouts: 0.01 us -> 3.74 us  [the longest x1 2.07 us: per_device(): grad_qkv = summed[:, :3 * width]]
  transfers between devices with their start and end apart: 6 -> 5, of which waited for: 5 -> 4; matrix products, arithmetic and copies ran while one was open for 13% -> 12% of each run, Pallas kernels for 11% -> 9%
where the time goes in v7:
time: 255 us; the launch traced here: 254 us
  waiting for transfers between devices  75 us (29%)
  blocking collectives  55.2 us (22%)
  local copies, waits for them, and re-layouts  28.1 us (11%)
  Pallas kernels  22.9 us (9%)
  matrix products  21.8 us (9%)
  starting transfers between devices  21.8 us (9%)
  between operations  15 us (6%)
  other arithmetic  13.8 us (5%)
    all_to_all x1, blocking collectives, per_device(): lax.all_to_all(parts.reshape(seq_count, share_rows, parts.shape[1]), 'seq...  37.3 us
    all_to_all x1, waiting for transfers between devices, per_device(): recv = lax.all_to_all(send, 'seq', split_axis=0, concat_axis=0, tiled=True)  31.5 us
    ppermute x1, waiting for transfers between devices, from_partner(): lax.ppermute(array, axis, [(i, i ^ 1 << stride) for i in range(lax.axis_s...  27.7 us
    pallas_call x1, Pallas kernels, attn_pass(): pl.pallas_call(kernel, grid=(sources // block_sources,), in_specs=[pl.Blo...  22.9 us
    all_to_all x1, blocking collectives, per_device(): lax.all_to_all(shares.reshape(batch_count, piece_rows, shares.shape[1]),...  17.9 us
    all_to_all x1, waiting for transfers between devices, per_device(): lax.all_to_all(back, 'seq', split_axis=0, concat_axis=0, tiled=True)  9.49 us
    dot_general x3, matrix products, per_device(): lax.dot_general(normed_recv, piece, over_frames, preferred_element_type=j...  8.8 us
    all_to_all x1, starting transfers between devices, per_device(): recv = lax.all_to_all(send, 'seq', split_axis=0, concat_axis=0, tiled=True)  8.59 us
  transfers between devices with their start and end apart: 5, of which 4 were waited for; matrix products, arithmetic and copies ran while one was open for 12% of the time, Pallas kernels for 9%

profile of v7, /device:TPU:1, one launch (start us, length us, event | category | flops | bytes accessed | tf_op | source)
XLA Modules:
  0.0 253.7 jit_solution(15656929852218397544)
XLA Ops:
  7.2 1.3 convert_reduce_fusion.1
  8.5 1.2 multiply_reduce_fusion.1
  9.7 4.4 %fusion.7 = bf16[24,8,24,128]{3,1,2,0:T(8,128)(2,1)S(1)} fusion(bf16[1024,3072]{1,0:T(8,128)(2,1)} %param.7, bf16[1,192,1024]{2,1,0:T(8,128)(2,1)} %param.5, f32[192]{0:T(256)S(1)} %fusion.34, f32[192]{0:T(256)S(1)} %broadcast_multiply_fusion), kind=kOutput, calls=%fused_computation.18 | convolution fusion | flops 1209335808 | bytes 7865856 | tf_op jit(solution)/shard_map/dot_general | solution.py:100
  14.2 0.2 copy.39
  14.4 0.2 fusion.36
  14.6 0.1 copy.27
  14.6 0.8 copy.28
  15.5 0.1 copy.25
  16.2 0.9 fusion.11
  17.1 0.1 copy.40
  17.2 0.1 copy.26
  17.2 0.1 broadcast_in_dim.22
  17.4 0.1 broadcast_in_dim.23
  17.5 1.6 pad_maximum_fusion.1
  19.1 8.6 %all-to-all-start = ((bf16[16,576,128]{2,1,0:T(8,128)(2,1)}), bf16[16,576,128]{2,1,0:T(8,128)(2,1)}, u32[]{:S(2)}, u32[]{:S(2)}) async-start(bf16[16,576,128]{2,1,0:T(8,128)(2,1)} %pad_maximum_fusion.1), calls=%async_computation | async-start | bytes 4718592 | tf_op jit(solution)/shard_map/all_to_all | solution.py:126
  27.7 0.1 rsqrt.16
  27.8 0.1 div.27
  27.9 0.2 multiply_convert_fusion
  28.1 31.5 %all-to-all-done.q_ref.do_ref.k_ref.v_ref = bf16[16,576,128]{2,1,0:T(8,128)(2,1)} async-done(((bf16[16,576,128]{2,1,0:T(8,128)(2,1)}), bf16[16,576,128]{2,1,0:T(8,128)(2,1)}, u32[]{:S(2)}, u32[]{:S(2)}) %all-to-all-start) | async-done | bytes 2359328 | tf_op jit(solution)/shard_map/all_to_all | solution.py:126
  59.6 2.1 broadcast_in_dim.51
  61.7 4.5 %all-to-all-start.2 = ((bf16[16,96,1024]{2,1,0:T(8,128)(2,1)}), bf16[16,96,1024]{2,1,0:T(8,128)(2,1)}, u32[]{:S(2)}, u32[]{:S(2)}) async-start(bf16[16,96,1024]{2,1,0:T(8,128)(2,1)} %bitcast.152), calls=%async_computation.2 | async-start | bytes 6291456 | tf_op jit(solution)/shard_map/all_to_all | solution.py:128
  66.2 0.6 compare_select_fusion.bias_ref
  66.8 22.9 %shard_map.84 = (bf16[16,96,128]{2,1,0:T(8,128)(2,1)}, bf16[16,96,128]{2,1,0:T(8,128)(2,1)}, f32[3072,128]{1,0:T(8,128)}, f32[3072,128]{1,0:T(8,128)}) custom-call(bf16[16,576,128]{2,1,0:T(8,128)(2,1)} %all-to-all-done.q_ref.do_ref.k_ref.v_ref, bf16[16,576,128]{2,1,0:T(8,128)(2,1)} %all-to-all-done.q_ref.do_ref.k_ref.v_ref, ...), custom_call_target="tpu_custom_call" | custom-call | tf_op jit(solution)/shard_map/pallas_call | solution.py:61
  89.7 1.5 fusion.23
  91.2 1.3 collective-permute-start
  92.4 27.7 %collective-permute-done = bf16[16,96,2,128]{3,1,0,2:T(8,128)(2,1)} collective-permute-done((bf16[16,96,2,128]{3,1,0,2:T(8,128)(2,1)S(1)}, bf16[16,96,2,128]{3,1,0,2:T(8,128)(2,1)}, u32[]{:S(2)}, u32[]{:S(2)}) %collective-permute-start) | collective-permute-done | bytes 786464 | tf_op jit(solution)/shard_map/ppermute | solution.py:13
  120.1 1.8 fusion.6
  121.9 0.2 pad_maximum_fusion.2
  122.1 1.3 copy.31
  123.4 7.3 %all-to-all-start.1 = ((bf16[16,96,4,128]{3,1,2,0:T(8,128)(2,1)}), bf16[16,96,4,128]{3,1,2,0:T(8,128)(2,1)}, u32[]{:S(2)}, u32[]{:S(2)}) async-start(bf16[16,96,4,128]{3,1,2,0:T(8,128)(2,1)} %copy.31), calls=%async_computation.1 | async-start | bytes 3145728 | tf_op jit(solution)/shard_map/all_to_all | solution.py:149
  130.7 0.2 all-gather.2.cloned.1.call-start
  130.9 3.0 %fusion.17 = bf16[1024,1,128]{2,0,1:T(8,128)(2,1)S(1)} fusion(bf16[16,96,1024]{2,1,0:T(8,128)(2,1)} %all-to-all-done.2, bf16[16,96,128]{2,1,0:T(8,128)(2,1)} %get-tuple-element.9), kind=kOutput, calls=%fused_computation.34 | convolution fusion | flops 402784256 | bytes 3801088 | tf_op jit(solution)/shard_map/dot_general | solution.py:158
  133.9 2.9 %fusion.15 = bf16[1024,1,128]{2,0,1:T(8,128)(2,1)S(1)} fusion(bf16[16,96,1024]{2,1,0:T(8,128)(2,1)} %all-to-all-done.2, bf16[16,96,2,128]{3,1,0,2:T(8,128)(2,1)S(1)} %fusion.6), kind=kOutput, calls=%fused_computation.32 | convolution fusion | flops 402784256 | bytes 3801088 | tf_op jit(solution)/shard_map/dot_general | solution.py:158
  136.8 2.9 %fusion.16 = bf16[1024,1,128]{2,0,1:T(8,128)(2,1)S(1)} fusion(bf16[16,96,1024]{2,1,0:T(8,128)(2,1)} %all-to-all-done.2, bf16[16,96,2,128]{3,1,0,2:T(8,128)(2,1)S(1)} %fusion.6), kind=kOutput, calls=%fused_computation.33 | convolution fusion | flops 402784256 | bytes 3801088 | tf_op jit(solution)/shard_map/dot_general | solution.py:158
  139.7 0.1 pad_maximum_fusion.3
  139.8 0.7 copy.33
  140.5 1.4 concatenate.25
  141.9 9.5 %all-to-all-done.1 = bf16[16,96,4,128]{3,1,2,0:T(8,128)(2,1)} async-done(((bf16[16,96,4,128]{3,1,2,0:T(8,128)(2,1)}), bf16[16,96,4,128]{3,1,2,0:T(8,128)(2,1)}, u32[]{:S(2)}, u32[]{:S(2)}) %all-to-all-start.1) | async-done | bytes 1572896 | tf_op jit(solution)/shard_map/all_to_all | solution.py:149
  151.4 2.5 copy.48
  153.9 1.1 copy-done.3
  155.1 0.1 slice.47
  155.1 0.9 copy.49
  156.0 1.2 copy.34
  157.2 0.8 convolution_convert_fusion.1
  158.0 0.3 copy-done.6
  158.3 0.3 pad_maximum_fusion
  158.7 37.3 %all_to_all.25 = bf16[16,64,1408]{2,1,0:T(8,128)(2,1)S(1)} all-to-all(bf16[16,64,1408]{2,1,0:T(8,128)(2,1)S(1)} %pad_maximum_fusion), channel_id=1, replica_groups=mesh['batch'=8,'seq'=16] {'seq'}, dimensions={0} | all-to-all | bytes 5767168 | tf_op jit(solution)/shard_map/all_to_all | solution.py:166
  196.0 1.6 copy-done.1
  197.6 0.9 bitcast_reduce_fusion
  198.5 1.4 reshape.168
  199.9 1.2 copy.35
  201.1 1.2 concatenate.27
  202.2 1.9 slice_reduce_fusion
  204.2 17.9 %all_to_all.26 = bf16[8,8,4096]{2,1,0:T(8,128)(2,1)S(1)} all-to-all(bf16[8,8,4096]{2,1,0:T(8,128)(2,1)S(1)} %pad_maximum_fusion.4), channel_id=1, replica_groups=mesh['batch'=8,'seq'=16] {'batch'}, dimensions={0} | all-to-all | bytes 1048576 | tf_op jit(solution)/shard_map/all_to_all | solution.py:179
  222.1 0.7 convert_reduce_fusion
  222.9 2.5 slice.48
  225.4 3.0 %reshape.164 = bf16[192,3072]{1,0:T(8,128)(2,1)} reshape(bf16[2,96,3,8,128]{4,3,2,1,0:T(8,128)(2,1)} %slice.48) | data formatting | bytes 2359296 | tf_op jit(solution)/shard_map/reshape | solution.py:152
  228.3 5.6 %multiply_reduce_fusion = (f32[192]{0:T(256)S(1)}, f32[192,1024]{1,0:T(8,128)S(1)}) fusion(bf16[1,192,1024]{2,1,0:T(8,128)(2,1)S(1)} %copy-done.2, f32[192]{0:T(256)S(1)} %broadcast_multiply_fusion, bf16[192,3072]{1,0:T(8,128)(2,1)} %reshape.164, bf16[1024,3072]{1,0:T(8,128)(2,1)} %param.7), kind=kOutput, calls=%fused_computation.48 | convolution fusion | flops 1208745728 | bytes 8652288 | tf_op jit(solution)/shard_map/dot_general | solution.py:186
  234.0 0.4 fusion.35
  234.4 1.3 fusion.10
  235.7 1.1 fusion.26
  236.8 6.4 %all-gather.2.cloned.1.call-done = f32[64,4096]{1,0:T(8,128)} async-done(((f32[8,4096]{1,0:T(8,128)}), f32[64,4096]{1,0:T(8,128)}) %all-gather.2.cloned.1.call-update) | async-done | bytes 1048592 | tf_op jit(solution)/shard_map/all_gather | solution.py:183
  243.2 2.1 slice.53
  245.2 1.7 slice.54
  (29 shorter events, 0.1 us)
Async XLA Ops:
  7.2 9.0 %copy-start = (bf16[1024,1024]{1,0:T(8,128)(2,1)S(1)}, bf16[1024,1024]{1,0:T(8,128)(2,1)}, u32[]{:S(2)}) copy-start(bf16[1024,1024]{1,0:T(8,128)(2,1)} %param.8) | copy-start | bytes 6291460
  14.4 1.8 copy-start.4
  16.2 1.2 copy-start.9
  19.1 8.8 %copy-start.2 = (bf16[1,192,1024]{2,1,0:T(8,128)(2,1)S(1)}, bf16[1,192,1024]{2,1,0:T(8,128)(2,1)}, u32[]{:S(2)}) copy-start(bf16[1,192,1024]{2,1,0:T(8,128)(2,1)} %param.5) | copy-start | bytes 1179652
  19.1 40.5 %all-to-all-start = ((bf16[16,576,128]{2,1,0:T(8,128)(2,1)}), bf16[16,576,128]{2,1,0:T(8,128)(2,1)}, u32[]{:S(2)}, u32[]{:S(2)}) async-start(bf16[16,576,128]{2,1,0:T(8,128)(2,1)} %pad_maximum_fusion.1), calls=%async_computation | async-start | bytes 4718592 | tf_op jit(solution)/shard_map/all_to_all | solution.py:126
  61.7 61.7 %all-to-all-start.2 = ((bf16[16,96,1024]{2,1,0:T(8,128)(2,1)}), bf16[16,96,1024]{2,1,0:T(8,128)(2,1)}, u32[]{:S(2)}, u32[]{:S(2)}) async-start(bf16[16,96,1024]{2,1,0:T(8,128)(2,1)} %bitcast.152), calls=%async_computation.2 | async-start | bytes 6291456 | tf_op jit(solution)/shard_map/all_to_all | solution.py:128
  91.2 28.9 %collective-permute-start = (bf16[16,96,2,128]{3,1,0,2:T(8,128)(2,1)S(1)}, bf16[16,96,2,128]{3,1,0,2:T(8,128)(2,1)}, u32[]{:S(2)}, u32[]{:S(2)}) collective-permute-start(bf16[16,96,2,128]{3,1,0,2:T(8,128)(2,1)S(1)} %fusion.23), channel_id=1, source_target_pairs={{0,1},{1,0},{2,3},{3,2},{4,5},{5,4},{6,7},{7,6},{8,9},{9,8},{10,11... | collective-permute-start | bytes 2359304 | tf_op jit(solution)/shard_map/ppermute | solution.py:13
  92.4 29.5 %copy-start.10 = (bf16[16,96,128]{2,1,0:T(8,128)(2,1)S(1)}, bf16[16,96,128]{2,1,0:T(8,128)(2,1)}, u32[]{:S(2)}) copy-start(bf16[16,96,128]{2,1,0:T(8,128)(2,1)} %get-tuple-element.9) | copy-start | bytes 1179652
  92.4 29.5 %copy-start.11 = (bf16[16,96,128]{2,1,0:T(8,128)(2,1)S(1)}, bf16[16,96,128]{2,1,0:T(8,128)(2,1)}, u32[]{:S(2)}) copy-start(bf16[16,96,128]{2,1,0:T(8,128)(2,1)} %get-tuple-element.8) | copy-start | bytes 1179652
  123.4 28.1 %all-to-all-start.1 = ((bf16[16,96,4,128]{3,1,2,0:T(8,128)(2,1)}), bf16[16,96,4,128]{3,1,2,0:T(8,128)(2,1)}, u32[]{:S(2)}, u32[]{:S(2)}) async-start(bf16[16,96,4,128]{3,1,2,0:T(8,128)(2,1)} %copy.31), calls=%async_computation.1 | async-start | bytes 3145728 | tf_op jit(solution)/shard_map/all_to_all | solution.py:149
  130.7 112.5 %all-gather.2.cloned.1.call-start = ((), (), s32[]{:S(2)}) async-start(), calls=%async_computation.5 | async-start | bytes 1179648 | tf_op jit(solution)/shard_map/all_gather | solution.py:183
  151.4 5.8 %copy-start.5 = (bf16[1,192,1024]{2,1,0:T(8,128)(2,1)S(1)}, bf16[1,192,1024]{2,1,0:T(8,128)(2,1)}, u32[]{:S(2)}) copy-start(bf16[1,192,1024]{2,1,0:T(8,128)(2,1)} %param.9) | copy-start | bytes 1179652
  153.9 1.2 copy-start.3
  155.1 0.9 copy-start.7
  157.2 1.1 copy-start.6
  196.0 1.6 copy-start.1
  228.3 6.0 %copy-start.8 = (bf16[2,96,1,8,128]{4,3,2,1,0:T(8,128)(2,1)S(1)}, bf16[2,96,1,8,128]{4,3,2,1,0:T(8,128)(2,1)}, u32[]{:S(2)}) copy-start(bf16[2,96,1,8,128]{4,3,2,1,0:T(8,128)(2,1)} %copy-done.7) | copy-start | bytes 1179652
Sparse Core Ops, SparseCore 0:
  223.0 20.1 all-gather.1

commit v8 on v7

--- a/solution.py
+++ b/solution.py
@@ -153,12 +153,8 @@
     branch = jnp.dot(context, w_out, preferred_element_type=jnp.float32)
     output = (inputs + valid[:, None] * branch).astype(jnp.bfloat16)
     over_frames = (((0, 1), (0, 1)), ((), ()))
-    qkv_part = jnp.stack(
-        [
-            lax.dot_general(normed_recv, piece, over_frames, preferred_element_type=jnp.float32)
-            for piece in (dquery, paired_rows[:, :, 0], paired_rows[:, :, 1])
-        ],
-        axis=1,
+    qkv_part = lax.dot_general(
+        normed_recv, back[:, :, 1:], over_frames, preferred_element_type=jnp.float32
     ).reshape(width, 3 * head_size)
     out_part = jnp.dot(context.T, grad_rows, preferred_element_type=jnp.float32)
     share_rows = width // seq_count

time: 255 us -> 255 us (level)
  waiting for transfers between devices: 75 us -> 80.2 us
  matrix products: 21.8 us -> 16.8 us
    all_to_all x1, waiting for transfers between devices: 9.49 us -> 14.6 us  [per_device(): lax.all_to_all(back, 'seq', split_axis=0, concat_axis=0, tiled=True)]
    dot_general x3 -> x1, matrix products: 8.8 us -> 3.76 us  [per_device(): lax.dot_general(normed_recv, back[:, :, 1:], over_frames, preferred_eleme...]
  transfers between devices with their start and end apart: 5 -> 5, of which waited for: 4 -> 4; matrix products, arithmetic and copies ran while one was open for 12% -> 10% of each run, Pallas kernels for 9% -> 9%
where the time goes in v8:
time: 255 us; the launch traced here: 254 us
  waiting for transfers between devices  80.2 us (31%)
  blocking collectives  55.2 us (22%)
  local copies, waits for them, and re-layouts  28.8 us (11%)
  Pallas kernels  22.9 us (9%)
  starting transfers between devices  21.8 us (9%)
  matrix products  16.8 us (7%)
  between operations  15 us (6%)
  other arithmetic  13.8 us (5%)
    all_to_all x1, blocking collectives, per_device(): lax.all_to_all(parts.reshape(seq_count, share_rows, parts.shape[1]), 'seq...  37.3 us
    all_to_all x1, waiting for transfers between devices, per_device(): recv = lax.all_to_all(send, 'seq', split_axis=0, concat_axis=0, tiled=True)  31.5 us
    ppermute x1, waiting for transfers between devices, from_partner(): lax.ppermute(array, axis, [(i, i ^ 1 << stride) for i in range(lax.axis_s...  27.7 us
    pallas_call x1, Pallas kernels, attn_pass(): pl.pallas_call(kernel, grid=(sources // block_sources,), in_specs=[pl.Blo...  22.9 us
    all_to_all x1, blocking collectives, per_device(): lax.all_to_all(shares.reshape(batch_count, piece_rows, shares.shape[1]),...  17.9 us
    all_to_all x1, waiting for transfers between devices, per_device(): lax.all_to_all(back, 'seq', split_axis=0, concat_axis=0, tiled=True)  14.6 us
    all_to_all x1, starting transfers between devices, per_device(): recv = lax.all_to_all(send, 'seq', split_axis=0, concat_axis=0, tiled=True)  8.6 us
    all_to_all x1, starting transfers between devices, per_device(): lax.all_to_all(back, 'seq', split_axis=0, concat_axis=0, tiled=True)  7.29 us
  transfers between devices with their start and end apart: 5, of which 4 were waited for; matrix products, arithmetic and copies ran while one was open for 10% of the time, Pallas kernels for 9%

profile of v8, /device:TPU:1, one launch (start us, length us, event | category | flops | bytes accessed | tf_op | source)
XLA Modules:
  0.0 254.4 jit_solution(14324225402843750132)
XLA Ops:
  7.2 0.0 copy-start
  7.2 1.3 convert_reduce_fusion.1
  8.5 1.2 multiply_reduce_fusion.1
  9.7 4.4 %fusion.11 = bf16[24,8,24,128]{3,1,2,0:T(8,128)(2,1)S(1)} fusion(bf16[1024,3072]{1,0:T(8,128)(2,1)} %param.7, bf16[1,192,1024]{2,1,0:T(8,128)(2,1)} %param.5, f32[192]{0:T(256)S(1)} %fusion.35, f32[192]{0:T(256)S(1)} %broadcast_multiply_fusion), kind=kOutput, calls=%fused_computation.21 | convolution fusion | flops 1209335808 | bytes 7865856 | tf_op jit(solution)/shard_map/dot_general | solution.py:100
  14.2 0.2 copy.40
  14.4 0.2 fusion.38
  14.6 0.1 copy.27
  14.6 0.8 copy.28
  15.5 0.1 copy.25
  16.2 0.9 fusion.15
  17.1 0.1 copy.41
  17.2 0.1 copy.26
  17.2 0.1 broadcast_in_dim.22
  17.4 0.7 copy-done.9
  18.1 0.1 broadcast_in_dim.23
  18.2 1.6 pad_maximum_fusion.1
  19.8 8.6 %all-to-all-start = ((bf16[16,576,128]{2,1,0:T(8,128)(2,1)}), bf16[16,576,128]{2,1,0:T(8,128)(2,1)}, u32[]{:S(2)}, u32[]{:S(2)}) async-start(bf16[16,576,128]{2,1,0:T(8,128)(2,1)} %pad_maximum_fusion.1), calls=%async_computation | async-start | bytes 4718592 | tf_op jit(solution)/shard_map/all_to_all | solution.py:126
  28.4 0.1 rsqrt.16
  28.5 0.1 div.27
  28.6 0.2 multiply_convert_fusion
  28.8 31.5 %all-to-all-done.q_ref.do_ref.k_ref.v_ref = bf16[16,576,128]{2,1,0:T(8,128)(2,1)} async-done(((bf16[16,576,128]{2,1,0:T(8,128)(2,1)}), bf16[16,576,128]{2,1,0:T(8,128)(2,1)}, u32[]{:S(2)}, u32[]{:S(2)}) %all-to-all-start) | async-done | bytes 2359328 | tf_op jit(solution)/shard_map/all_to_all | solution.py:126
  60.3 2.1 broadcast_in_dim.51
  62.4 4.5 %all-to-all-start.2 = ((bf16[16,96,1024]{2,1,0:T(8,128)(2,1)}), bf16[16,96,1024]{2,1,0:T(8,128)(2,1)}, u32[]{:S(2)}, u32[]{:S(2)}) async-start(bf16[16,96,1024]{2,1,0:T(8,128)(2,1)} %bitcast.126), calls=%async_computation.2 | async-start | bytes 6291456 | tf_op jit(solution)/shard_map/all_to_all | solution.py:128
  66.9 0.6 compare_select_fusion.bias_ref
  67.5 22.9 %shard_map.84 = (bf16[16,96,128]{2,1,0:T(8,128)(2,1)}, bf16[16,96,128]{2,1,0:T(8,128)(2,1)}, f32[3072,128]{1,0:T(8,128)}, f32[3072,128]{1,0:T(8,128)}) custom-call(bf16[16,576,128]{2,1,0:T(8,128)(2,1)} %all-to-all-done.q_ref.do_ref.k_ref.v_ref, bf16[16,576,128]{2,1,0:T(8,128)(2,1)} %all-to-all-done.q_ref.do_ref.k_ref.v_ref, ...), custom_call_target="tpu_custom_call" | custom-call | tf_op jit(solution)/shard_map/pallas_call | solution.py:61
  90.4 1.5 fusion.24
  91.9 1.3 collective-permute-start
  93.1 27.7 %collective-permute-done = bf16[16,96,2,128]{3,1,0,2:T(8,128)(2,1)} collective-permute-done((bf16[16,96,2,128]{3,1,0,2:T(8,128)(2,1)S(1)}, bf16[16,96,2,128]{3,1,0,2:T(8,128)(2,1)}, u32[]{:S(2)}, u32[]{:S(2)}) %collective-permute-start) | collective-permute-done | bytes 786464 | tf_op jit(solution)/shard_map/ppermute | solution.py:13
  120.8 1.8 fusion.8
  122.6 0.2 pad_maximum_fusion.2
  122.8 1.3 copy.31
  124.1 7.3 %all-to-all-start.1 = ((bf16[16,96,4,128]{3,1,2,0:T(8,128)(2,1)}), bf16[16,96,4,128]{3,1,2,0:T(8,128)(2,1)}, u32[]{:S(2)}, u32[]{:S(2)}) async-start(bf16[16,96,4,128]{3,1,2,0:T(8,128)(2,1)} %copy.31), calls=%async_computation.1 | async-start | bytes 3145728 | tf_op jit(solution)/shard_map/all_to_all | solution.py:149
  131.4 0.2 all-gather.2.cloned.1.call-start
  131.6 3.8 %bitcast_convert_fusion = bf16[1024,3,128]{2,0,1:T(8,128)(2,1)S(1)} fusion(bf16[16,96,1024]{2,1,0:T(8,128)(2,1)} %all-to-all-done.2, bf16[16,96,2,128]{3,1,0,2:T(8,128)(2,1)S(1)} %fusion.8, bf16[16,96,1,128]{3,1,0,2:T(8,128)(2,1)} %bitcast.146), kind=kOutput, calls=%fused_computation.19 | convolution fusion | flops 1210712064 | bytes 5111808 | tf_op jit(solution)/shard_map/dot_general | solution.py:156
  135.4 0.7 copy.33
  136.1 1.4 concatenate.29
  137.5 14.6 %all-to-all-done.1 = bf16[16,96,4,128]{3,1,2,0:T(8,128)(2,1)} async-done(((bf16[16,96,4,128]{3,1,2,0:T(8,128)(2,1)}), bf16[16,96,4,128]{3,1,2,0:T(8,128)(2,1)}, u32[]{:S(2)}, u32[]{:S(2)}) %all-to-all-start.1) | async-done | bytes 1572896 | tf_op jit(solution)/shard_map/all_to_all | solution.py:149
  152.2 2.5 copy.49
  154.6 1.1 copy-done.3
  155.8 0.1 slice.41
  155.8 0.9 copy.50
  156.7 1.2 copy.34
  157.9 0.8 convolution_convert_fusion.1
  158.7 0.3 copy-done.6
  159.1 0.3 pad_maximum_fusion
  159.4 37.3 %all_to_all.25 = bf16[16,64,1408]{2,1,0:T(8,128)(2,1)S(1)} all-to-all(bf16[16,64,1408]{2,1,0:T(8,128)(2,1)S(1)} %pad_maximum_fusion), channel_id=1, replica_groups=mesh['batch'=8,'seq'=16] {'seq'}, dimensions={0} | all-to-all | bytes 5767168 | tf_op jit(solution)/shard_map/all_to_all | solution.py:162
  196.7 1.6 copy-done.1
  198.3 0.9 bitcast_reduce_fusion
  199.2 1.4 reshape.168
  200.6 1.2 copy.35
  201.8 1.2 concatenate.31
  202.9 1.9 slice_reduce_fusion
  204.9 17.9 %all_to_all.26 = bf16[8,8,4096]{2,1,0:T(8,128)(2,1)S(1)} all-to-all(bf16[8,8,4096]{2,1,0:T(8,128)(2,1)S(1)} %pad_maximum_fusion.3), channel_id=1, replica_groups=mesh['batch'=8,'seq'=16] {'batch'}, dimensions={0} | all-to-all | bytes 1048576 | tf_op jit(solution)/shard_map/all_to_all | solution.py:175
  222.8 0.7 convert_reduce_fusion
  223.5 0.0 all-gather.2.cloned.1.call-update
  223.5 2.5 slice.42
  226.0 3.0 %reshape.164 = bf16[192,3072]{1,0:T(8,128)(2,1)} reshape(bf16[2,96,3,8,128]{4,3,2,1,0:T(8,128)(2,1)} %slice.42) | data formatting | bytes 2359296 | tf_op jit(solution)/shard_map/reshape | solution.py:152
  229.0 5.6 %multiply_reduce_fusion = (f32[192]{0:T(256)S(1)}, f32[192,1024]{1,0:T(8,128)S(1)}) fusion(bf16[1,192,1024]{2,1,0:T(8,128)(2,1)S(1)} %copy-done.2, f32[192]{0:T(256)S(1)} %broadcast_multiply_fusion, bf16[192,3072]{1,0:T(8,128)(2,1)} %reshape.164, bf16[1024,3072]{1,0:T(8,128)(2,1)} %param.7), kind=kOutput, calls=%fused_computation.44 | convolution fusion | flops 1208745728 | bytes 8652288 | tf_op jit(solution)/shard_map/dot_general | solution.py:182
  234.7 0.4 fusion.37
  235.0 1.3 fusion.14
  236.4 1.1 fusion.27
  237.4 6.4 %all-gather.2.cloned.1.call-done = f32[64,4096]{1,0:T(8,128)} async-done(((f32[8,4096]{1,0:T(8,128)}), f32[64,4096]{1,0:T(8,128)}) %all-gather.2.cloned.1.call-update) | async-done | bytes 1048592 | tf_op jit(solution)/shard_map/all_gather | solution.py:179
  243.8 2.1 slice.45
  245.9 1.7 slice.46
  (26 shorter events, 0.1 us)
Async XLA Ops:
  7.2 9.0 %copy-start = (bf16[1024,1024]{1,0:T(8,128)(2,1)S(1)}, bf16[1024,1024]{1,0:T(8,128)(2,1)}, u32[]{:S(2)}) copy-start(bf16[1024,1024]{1,0:T(8,128)(2,1)} %param.8) | copy-start | bytes 6291460
  14.4 1.8 copy-start.4
  17.1 1.0 copy-start.9
  19.8 8.8 %copy-start.2 = (bf16[1,192,1024]{2,1,0:T(8,128)(2,1)S(1)}, bf16[1,192,1024]{2,1,0:T(8,128)(2,1)}, u32[]{:S(2)}) copy-start(bf16[1,192,1024]{2,1,0:T(8,128)(2,1)} %param.5) | copy-start | bytes 1179652
  19.8 40.5 %all-to-all-start = ((bf16[16,576,128]{2,1,0:T(8,128)(2,1)}), bf16[16,576,128]{2,1,0:T(8,128)(2,1)}, u32[]{:S(2)}, u32[]{:S(2)}) async-start(bf16[16,576,128]{2,1,0:T(8,128)(2,1)} %pad_maximum_fusion.1), calls=%async_computation | async-start | bytes 4718592 | tf_op jit(solution)/shard_map/all_to_all | solution.py:126
  62.4 61.7 %all-to-all-start.2 = ((bf16[16,96,1024]{2,1,0:T(8,128)(2,1)}), bf16[16,96,1024]{2,1,0:T(8,128)(2,1)}, u32[]{:S(2)}, u32[]{:S(2)}) async-start(bf16[16,96,1024]{2,1,0:T(8,128)(2,1)} %bitcast.126), calls=%async_computation.2 | async-start | bytes 6291456 | tf_op jit(solution)/shard_map/all_to_all | solution.py:128
  91.9 28.9 %collective-permute-start = (bf16[16,96,2,128]{3,1,0,2:T(8,128)(2,1)S(1)}, bf16[16,96,2,128]{3,1,0,2:T(8,128)(2,1)}, u32[]{:S(2)}, u32[]{:S(2)}) collective-permute-start(bf16[16,96,2,128]{3,1,0,2:T(8,128)(2,1)S(1)} %fusion.24), channel_id=1, source_target_pairs={{0,1},{1,0},{2,3},{3,2},{4,5},{5,4},{6,7},{7,6},{8,9},{9,8},{10,11... | collective-permute-start | bytes 2359304 | tf_op jit(solution)/shard_map/ppermute | solution.py:13
  93.1 29.5 %copy-start.10 = (bf16[16,96,128]{2,1,0:T(8,128)(2,1)S(1)}, bf16[16,96,128]{2,1,0:T(8,128)(2,1)}, u32[]{:S(2)}) copy-start(bf16[16,96,128]{2,1,0:T(8,128)(2,1)} %get-tuple-element.9) | copy-start | bytes 1179652
  93.1 29.5 %copy-start.11 = (bf16[16,96,128]{2,1,0:T(8,128)(2,1)S(1)}, bf16[16,96,128]{2,1,0:T(8,128)(2,1)}, u32[]{:S(2)}) copy-start(bf16[16,96,128]{2,1,0:T(8,128)(2,1)} %get-tuple-element.8) | copy-start | bytes 1179652
  124.1 28.1 %all-to-all-start.1 = ((bf16[16,96,4,128]{3,1,2,0:T(8,128)(2,1)}), bf16[16,96,4,128]{3,1,2,0:T(8,128)(2,1)}, u32[]{:S(2)}, u32[]{:S(2)}) async-start(bf16[16,96,4,128]{3,1,2,0:T(8,128)(2,1)} %copy.31), calls=%async_computation.1 | async-start | bytes 3145728 | tf_op jit(solution)/shard_map/all_to_all | solution.py:149
  131.4 112.5 %all-gather.2.cloned.1.call-start = ((), (), s32[]{:S(2)}) async-start(), calls=%async_computation.5 | async-start | bytes 1179648 | tf_op jit(solution)/shard_map/all_gather | solution.py:179
  152.1 5.8 %copy-start.5 = (bf16[1,192,1024]{2,1,0:T(8,128)(2,1)S(1)}, bf16[1,192,1024]{2,1,0:T(8,128)(2,1)}, u32[]{:S(2)}) copy-start(bf16[1,192,1024]{2,1,0:T(8,128)(2,1)} %param.9) | copy-start | bytes 1179652
  154.6 1.2 copy-start.3
  155.8 0.9 copy-start.7
  157.9 1.1 copy-start.6
  196.7 1.6 copy-start.1
  229.0 6.0 %copy-start.8 = (bf16[2,96,1,8,128]{4,3,2,1,0:T(8,128)(2,1)S(1)}, bf16[2,96,1,8,128]{4,3,2,1,0:T(8,128)(2,1)}, u32[]{:S(2)}) copy-start(bf16[2,96,1,8,128]{4,3,2,1,0:T(8,128)(2,1)} %copy-done.7) | copy-start | bytes 1179652
Sparse Core Ops, SparseCore 0:
  223.7 20.1 all-gather.1

commit v9 on v8

--- a/solution.py
+++ b/solution.py
@@ -133,50 +133,49 @@
 
     context_h, dquery, dkeys, dvalues = attn_pass(recv, part_rows, bias, scale)
 
+    batch_count = lax.axis_size("batch")
+    share_rows = width // seq_count
+    piece_rows = share_rows // batch_count
+    context_back = lax.all_to_all(context_h, "seq", split_axis=0, concat_axis=0, tiled=True)
+    context = context_back.reshape(H, groups, part_rows, head_size).transpose(1, 2, 0, 3).reshape(tok_rows, width)
+    branch = jnp.dot(context, w_out, preferred_element_type=jnp.float32)
+    output = (inputs + valid[:, None] * branch).astype(jnp.bfloat16)
+    out_part = jnp.dot(context.T, grad_rows, preferred_element_type=jnp.float32).astype(jnp.bfloat16)
+    out_part = out_part.reshape(seq_count, batch_count, piece_rows, width).transpose(1, 0, 2, 3)
+    out_batch = lax.psum_scatter(out_part.reshape(width, width), "batch", scatter_dimension=0, tiled=True)
+
     split_grads = jnp.stack([dkeys, dvalues], axis=1).reshape(seq_count, groups, part_rows, 2, head_size)
     own_half = lax.dynamic_index_in_dim(split_grads, group_index, 1, keepdims=False)
     other_half = lax.dynamic_index_in_dim(split_grads, 1 - group_index, 1, keepdims=False)
     partner_half = from_partner(other_half.astype(jnp.bfloat16), "seq", 0)
     paired_rows = (own_half + partner_half.astype(jnp.float32)).astype(jnp.bfloat16)
-    back = jnp.concatenate(
-        [
-            context_h.reshape(seq_count, part_rows, 1, head_size),
-            dquery.reshape(seq_count, part_rows, 1, head_size),
-            paired_rows,
-        ],
-        axis=2,
+    back = jnp.concatenate([dquery.reshape(seq_count, part_rows, 1, head_size), paired_rows], axis=2)
+    returned = lax.all_to_all(back, "seq", split_axis=0, concat_axis=0, tiled=True)
+    dqkv = returned.reshape(H, groups, part_rows, 3, head_size).transpose(1, 2, 3, 0, 4).reshape(tok_rows, 3 * width)
+    over_frames = (((0, 1), (0, 1)), ((), ()))
+    qkv_part = lax.dot_general(normed_recv, back, over_frames, preferred_element_type=jnp.float32)
+    qkv_send = qkv_part.astype(jnp.bfloat16).reshape(seq_count, share_rows * 3 * head_size)
+    out_send = out_batch.reshape(seq_count, piece_rows * width)
+    gathered = lax.all_to_all(
+        jnp.concatenate([qkv_send, out_send], axis=1), "seq", split_axis=0, concat_axis=0, tiled=True
     )
-    returned = lax.all_to_all(back, "seq", split_axis=0, concat_axis=0, tiled=True)
-    returned = returned.reshape(H, groups, part_rows, 4, head_size).transpose(1, 2, 3, 0, 4)
-    context = returned[:, :, 0].reshape(tok_rows, width)
-    dqkv = returned[:, :, 1:].reshape(tok_rows, 3 * width)
-    branch = jnp.dot(context, w_out, preferred_element_type=jnp.float32)
-    output = (inputs + valid[:, None] * branch).astype(jnp.bfloat16)
-    over_frames = (((0, 1), (0, 1)), ((), ()))
-    qkv_part = lax.dot_general(
-        normed_recv, back[:, :, 1:], over_frames, preferred_element_type=jnp.float32
-    ).reshape(width, 3 * head_size)
-    out_part = jnp.dot(context.T, grad_rows, preferred_element_type=jnp.float32)
-    share_rows = width // seq_count
-    parts = jnp.concatenate([qkv_part, out_part], axis=1).astype(jnp.bfloat16)
-    gathered = lax.all_to_all(
-        parts.reshape(seq_count, share_rows, parts.shape[1]), "seq", split_axis=0, concat_axis=0, tiled=True
-    )
+    qkv_split = share_rows * 3 * head_size
     qkv_rows = (
-        jnp.sum(gathered[:, :, : 3 * head_size].astype(jnp.float32).reshape(H, groups, share_rows, 3 * head_size), axis=1)
+        jnp.sum(gathered[:, :qkv_split].astype(jnp.float32).reshape(H, groups, share_rows, 3 * head_size), axis=1)
         .reshape(H, share_rows, 3, head_size)
         .transpose(1, 2, 0, 3)
         .reshape(share_rows, 3 * width)
     )
-    out_rows = jnp.sum(gathered[:, :, 3 * head_size :].astype(jnp.float32), axis=0)
-    batch_count = lax.axis_size("batch")
-    piece_rows = share_rows // batch_count
-    shares = jnp.concatenate([qkv_rows, out_rows], axis=1).astype(jnp.bfloat16)
+    out_rows = jnp.sum(gathered[:, qkv_split:].astype(jnp.float32).reshape(seq_count, piece_rows, width), axis=0)
     pieces = lax.all_to_all(
-        shares.reshape(batch_count, piece_rows, shares.shape[1]), "batch", split_axis=0, concat_axis=0, tiled=True
+        qkv_rows.astype(jnp.bfloat16).reshape(batch_count, piece_rows, 3 * width),
+        "batch",
+        split_axis=0,
+        concat_axis=0,
+        tiled=True,
     )
-    summed = jnp.sum(pieces.astype(jnp.float32), axis=0)
-    summed = lax.all_gather(summed, "batch", axis=0, tiled=True)
+    qkv_sum = jnp.sum(pieces.astype(jnp.float32), axis=0)
+    summed = lax.all_gather(jnp.concatenate([qkv_sum, out_rows], axis=1), "batch", axis=0, tiled=True)
     grad_qkv = summed[:, : 3 * width]
     grad_out = summed[:, 3 * width :]
     dnormed = jnp.dot(dqkv, w_qkv.T, preferred_element_type=jnp.float32)

time: 255 us -> 275 us (1.078)
  blocking collectives: 55.2 us -> 36 us
  waiting for transfers between devices: 80.2 us -> 94.8 us
  local copies, waits for them, and re-layouts: 28.8 us -> 40.4 us
  other arithmetic: 13.8 us -> 18.9 us
  starting transfers between devices: 21.8 us -> 26.4 us
    all_to_all x2, blocking collectives: 55.2 us -> 36 us  [the longest x1 24.5 us: per_device(): lax.all_to_all(jnp.concatenate([qkv_send, out_send], axis=1), 'seq', spli...]
    ppermute x1, waiting for transfers between devices: 27.7 us -> 46.7 us  [from_partner(): lax.ppermute(array, axis, [(i, i ^ 1 << stride) for i in range(lax.axis_s...]
    unnamed x27 -> x20, local copies, waits for them, and re-layouts: 4.91 us -> 12.5 us
    all_to_all x0 -> x1, starting transfers between devices: none -> 7.52 us  [per_device(): lax.all_to_all(qkv_rows.astype(jnp.bfloat16).reshape(batch_count, piece_r...]
    convert_element_type x0 -> x4, local copies, waits for them, and re-layouts: none -> 6.87 us  [the longest x3 6.19 us: per_device(): qkv_rows.astype(jnp.bfloat16).reshape(batch_count, piece_rows, 3 * width)]
    all_gather x1, waiting for transfers between devices: 6.4 us -> 0.01 us  [per_device(): lax.all_gather(jnp.concatenate([qkv_sum, out_rows], axis=1), 'batch', axi...]
    all_to_all x0 -> x1, waiting for transfers between devices: none -> 5.34 us  [per_device(): lax.all_to_all(qkv_rows.astype(jnp.bfloat16).reshape(batch_count, piece_r...]
    reshape x3 -> x6, local copies, waits for them, and re-layouts: 6.85 us -> 11.1 us  [the longest x2 6.07 us: per_device(): returned.reshape(H, groups, part_rows, 3, head_size)]
  transfers between devices with their start and end apart: 5 -> 7, of which waited for: 4 -> 4; matrix products, arithmetic and copies ran while one was open for 10% -> 12% of each run, Pallas kernels for 9% -> 0%
where the time goes in v9:
time: 275 us; the launch traced here: 272 us
  waiting for transfers between devices  94.8 us (34%)
  local copies, waits for them, and re-layouts  40.4 us (15%)
  blocking collectives  36 us (13%)
  starting transfers between devices  26.4 us (10%)
  Pallas kernels  22.9 us (8%)
  other arithmetic  18.9 us (7%)
  matrix products  17.7 us (6%)
  between operations  15 us (5%)
    ppermute x1, waiting for transfers between devices, from_partner(): lax.ppermute(array, axis, [(i, i ^ 1 << stride) for i in range(lax.axis_s...  46.7 us
    all_to_all x1, waiting for transfers between devices, per_device(): recv = lax.all_to_all(send, 'seq', split_axis=0, concat_axis=0, tiled=True)  31.2 us
    all_to_all x1, blocking collectives, per_device(): lax.all_to_all(jnp.concatenate([qkv_send, out_send], axis=1), 'seq', spli...  24.5 us
    pallas_call x1, Pallas kernels, attn_pass(): pl.pallas_call(kernel, grid=(sources // block_sources,), in_specs=[pl.Blo...  22.9 us
    unnamed x20, local copies, waits for them, and re-layouts  12.5 us
    all_to_all x1, blocking collectives, per_device(): lax.all_to_all(context_h, 'seq', split_axis=0, concat_axis=0, tiled=True)  11.5 us
    all_to_all x1, waiting for transfers between devices, per_device(): lax.all_to_all(back, 'seq', split_axis=0, concat_axis=0, tiled=True)  11.5 us
    all_to_all x1, starting transfers between devices, per_device(): recv = lax.all_to_all(send, 'seq', split_axis=0, concat_axis=0, tiled=True)  8.47 us
  transfers between devices with their start and end apart: 7, of which 4 were waited for; matrix products, arithmetic and copies ran while one was open for 12% of the time, Pallas kernels for 0%

profile of v9, /device:TPU:1, one launch (start us, length us, event | category | flops | bytes accessed | tf_op | source)
XLA Modules:
  0.0 272.1 jit_solution(17784690179662982210)
XLA Ops:
  7.2 1.3 convert_reduce_fusion.1
  8.5 1.2 multiply_reduce_fusion.1
  9.7 4.4 %fusion.11 = bf16[24,8,24,128]{3,1,2,0:T(8,128)(2,1)S(1)} fusion(bf16[1024,3072]{1,0:T(8,128)(2,1)} %param.7, bf16[1,192,1024]{2,1,0:T(8,128)(2,1)} %param.5, f32[192]{0:T(256)S(1)} %fusion.34, f32[192]{0:T(256)S(1)} %broadcast_multiply_fusion), kind=kOutput, calls=%fused_computation.17 | convolution fusion | flops 1209335808 | bytes 7865856 | tf_op jit(solution)/shard_map/dot_general | solution.py:100
  14.2 0.2 copy.57
  14.4 0.2 fusion.36
  14.6 0.8 copy.42
  16.2 0.9 fusion.15
  17.2 0.1 broadcast_in_dim.22
  17.4 0.7 copy-done.5
  18.1 0.1 broadcast_in_dim.23
  18.2 1.6 pad_maximum_fusion
  19.8 8.5 %all-to-all-start = ((bf16[16,576,128]{2,1,0:T(8,128)(2,1)}), bf16[16,576,128]{2,1,0:T(8,128)(2,1)}, u32[]{:S(2)}, u32[]{:S(2)}) async-start(bf16[16,576,128]{2,1,0:T(8,128)(2,1)} %pad_maximum_fusion), calls=%async_computation | async-start | bytes 4718592 | tf_op jit(solution)/shard_map/all_to_all | solution.py:126
  28.3 0.6 compare_select_fusion.bias_ref
  28.9 31.2 %all-to-all-done.q_ref.do_ref.k_ref.v_ref = bf16[16,576,128]{2,1,0:T(8,128)(2,1)} async-done(((bf16[16,576,128]{2,1,0:T(8,128)(2,1)}), bf16[16,576,128]{2,1,0:T(8,128)(2,1)}, u32[]{:S(2)}, u32[]{:S(2)}) %all-to-all-start) | async-done | bytes 2359328 | tf_op jit(solution)/shard_map/all_to_all | solution.py:126
  60.2 22.9 %shard_map.84 = (bf16[16,96,128]{2,1,0:T(8,128)(2,1)}, bf16[16,96,128]{2,1,0:T(8,128)(2,1)}, f32[3072,128]{1,0:T(8,128)}, f32[3072,128]{1,0:T(8,128)}) custom-call(bf16[16,576,128]{2,1,0:T(8,128)(2,1)} %all-to-all-done.q_ref.do_ref.k_ref.v_ref, bf16[16,576,128]{2,1,0:T(8,128)(2,1)} %all-to-all-done.q_ref.do_ref.k_ref.v_ref, ...), custom_call_target="tpu_custom_call" | custom-call | tf_op jit(solution)/shard_map/pallas_call | solution.py:61
  83.0 11.5 %all_to_all.37 = bf16[16,96,128]{2,1,0:T(8,128)(2,1)S(1)} all-to-all(bf16[16,96,128]{2,1,0:T(8,128)(2,1)} %get-tuple-element.8), channel_id=1, replica_groups=mesh['batch'=8,'seq'=16] {'seq'}, dimensions={0} | all-to-all | bytes 786432 | tf_op jit(solution)/shard_map/all_to_all | solution.py:139
  94.5 0.3 copy.43
  94.8 0.8 convolution_convert_fusion.1
  95.6 1.5 copy.49
  97.2 0.1 rsqrt.16
  97.3 0.1 div.27
  97.3 0.8 copy-done.1
  98.1 0.2 multiply_convert_fusion
  98.4 2.1 broadcast_in_dim.51
  100.5 4.5 %all-to-all-start.3 = ((bf16[16,96,1024]{2,1,0:T(8,128)(2,1)}), bf16[16,96,1024]{2,1,0:T(8,128)(2,1)}, u32[]{:S(2)}, u32[]{:S(2)}) async-start(bf16[16,96,1024]{2,1,0:T(8,128)(2,1)} %bitcast.130), calls=%async_computation.3 | async-start | bytes 6291456 | tf_op jit(solution)/shard_map/all_to_all | solution.py:128
  105.0 1.5 fusion.21
  106.5 1.4 collective-permute-start
  107.9 46.7 %collective-permute-done = bf16[16,96,2,128]{3,1,0,2:T(8,128)(2,1)} collective-permute-done((bf16[16,96,2,128]{3,1,0,2:T(8,128)(2,1)S(1)}, bf16[16,96,2,128]{3,1,0,2:T(8,128)(2,1)}, u32[]{:S(2)}, u32[]{:S(2)}) %collective-permute-start) | collective-permute-done | bytes 786464 | tf_op jit(solution)/shard_map/ppermute | solution.py:13
  154.6 1.8 fusion.8
  156.4 0.9 copy-done.4
  157.3 3.8 %bitcast_convert_fusion = bf16[1024,3,128]{2,0,1:T(8,128)(2,1)S(1)} fusion(bf16[16,96,1024]{2,1,0:T(8,128)(2,1)} %all-to-all-done.3, bf16[16,96,2,128]{3,1,0,2:T(8,128)(2,1)S(1)} %fusion.8, bf16[16,96,1,128]{3,1,0,2:T(8,128)(2,1)} %bitcast.153), kind=kOutput, calls=%fused_computation.16 | convolution fusion | flops 1210712064 | bytes 5111808 | tf_op jit(solution)/shard_map/dot_general | solution.py:156
  161.1 0.7 copy.48
  161.7 1.5 reshape.174
  163.3 1.8 reshape.177
  165.0 1.3 maximum_bitcast_fusion
  166.3 0.5 broadcast.105
  166.8 2.1 reduce.3
  168.9 2.6 reshape.184
  171.6 24.5 %all_to_all.38 = bf16[16,2,16384]{2,1,0:T(2,128)(2,1)S(1)} all-to-all(bf16[16,2,16384]{2,1,0:T(2,128)(2,1)} %reshape.184), channel_id=1, replica_groups=mesh['batch'=8,'seq'=16] {'seq'}, dimensions={0} | all-to-all | bytes 2097152 | tf_op jit(solution)/shard_map/all_to_all | solution.py:159
  196.1 3.5 %reshape.185 = bf16[16,1,32768]{2,1,0:T(2,128)(2,1)} reshape(bf16[16,2,16384]{2,1,0:T(2,128)(2,1)S(1)} %all_to_all.38) | data formatting | bytes 2097152
  199.6 2.7 %copy.72 = bf16[16,1,32768]{2,0,1:T(8,128)(2,1)S(1)} copy(bf16[16,1,32768]{2,1,0:T(2,128)(2,1)} %reshape.185) | data formatting | bytes 2097152
  202.4 1.0 copy.60
  203.4 2.1 reduce.2
  205.5 2.0 convert_element_type.123
  207.5 2.3 copy.51
  209.8 1.9 convert_element_type.125
  211.7 7.5 %all-to-all-start.5 = ((bf16[8,8,3072]{2,1,0:T(8,128)(2,1)}), bf16[8,8,3072]{2,1,0:T(8,128)(2,1)}, u32[]{:S(2)}, u32[]{:S(2)}) async-start(bf16[8,8,3072]{2,1,0:T(8,128)(2,1)} %convert_element_type.125), calls=%async_computation.6 | async-start | bytes 786432 | tf_op jit(solution)/shard_map/all_to_all | solution.py:170
  219.2 1.3 pad_maximum_fusion.1
  220.5 1.1 copy.46
  221.7 5.3 %all-to-all-done.5 = bf16[8,8,3072]{2,1,0:T(8,128)(2,1)} async-done(((bf16[8,8,3072]{2,1,0:T(8,128)(2,1)}), bf16[8,8,3072]{2,1,0:T(8,128)(2,1)}, u32[]{:S(2)}, u32[]{:S(2)}) %all-to-all-start.5) | async-done | bytes 393248 | tf_op jit(solution)/shard_map/all_to_all | solution.py:170
  227.0 4.4 %all-to-all-start.2 = ((bf16[16,96,3,128]{3,1,2,0:T(8,128)(2,1)}), bf16[16,96,3,128]{3,1,2,0:T(8,128)(2,1)}, u32[]{:S(2)}, u32[]{:S(2)}) async-start(bf16[16,96,3,128]{3,1,2,0:T(8,128)(2,1)} %copy.46), calls=%async_computation.2 | async-start | bytes 2359296 | tf_op jit(solution)/shard_map/all_to_all | solution.py:153
  231.4 0.7 convert_reduce_fusion.2
  232.2 0.8 reduce_sum.88
  232.9 1.1 convert_reduce_fusion
  234.0 0.7 pad_maximum_fusion.2
  234.7 2.3 fusion.14
  237.0 11.5 %all-to-all-done.2 = bf16[16,96,3,128]{3,1,2,0:T(8,128)(2,1)} async-done(((bf16[16,96,3,128]{3,1,2,0:T(8,128)(2,1)}), bf16[16,96,3,128]{3,1,2,0:T(8,128)(2,1)}, u32[]{:S(2)}, u32[]{:S(2)}) %all-to-all-start.2) | async-done | bytes 1179680 | tf_op jit(solution)/shard_map/all_to_all | solution.py:153
  248.5 3.1 %copy.71 = bf16[8,2,96,3,128]{4,0,3,2,1:T(8,128)(2,1)} copy(bf16[8,2,96,3,128]{4,2,3,1,0:T(8,128)(2,1)} %bitcast.22) | data formatting | bytes 2359296 | tf_op jit(solution)/shard_map/reshape | solution.py:154
  251.5 3.0 %reshape.172 = bf16[192,3072]{1,0:T(8,128)(2,1)} reshape(bf16[2,96,3,8,128]{4,3,2,1,0:T(8,128)(2,1)} %bitcast.139) | data formatting | bytes 2359296 | tf_op jit(solution)/shard_map/reshape | solution.py:154
  254.5 5.5 %multiply_reduce_fusion = (f32[192]{0:T(256)S(1)}, f32[192,1024]{1,0:T(8,128)S(1)}) fusion(bf16[1,192,1024]{2,1,0:T(8,128)(2,1)S(1)} %copy-done.1, f32[192]{0:T(256)S(1)} %broadcast_multiply_fusion, bf16[192,3072]{1,0:T(8,128)(2,1)} %reshape.172, bf16[1024,3072]{1,0:T(8,128)(2,1)} %param.7), kind=kOutput, calls=%fused_computation.40 | convolution fusion | flops 1208745728 | bytes 8652288 | tf_op jit(solution)/shard_map/dot_general | solution.py:181
  260.1 0.4 fusion.35
  260.5 1.1 fusion.24
  261.6 2.1 slice.33
  263.6 1.7 slice.34
  (28 shorter events, 0.5 us)
Async XLA Ops:
  7.2 9.0 %copy-start = (bf16[1024,1024]{1,0:T(8,128)(2,1)S(1)}, bf16[1024,1024]{1,0:T(8,128)(2,1)}, u32[]{:S(2)}) copy-start(bf16[1024,1024]{1,0:T(8,128)(2,1)} %param.8) | copy-start | bytes 6291460
  14.4 1.8 copy-start.2
  17.1 1.0 copy-start.5
  19.8 40.4 %all-to-all-start = ((bf16[16,576,128]{2,1,0:T(8,128)(2,1)}), bf16[16,576,128]{2,1,0:T(8,128)(2,1)}, u32[]{:S(2)}, u32[]{:S(2)}) async-start(bf16[16,576,128]{2,1,0:T(8,128)(2,1)} %pad_maximum_fusion), calls=%async_computation | async-start | bytes 4718592 | tf_op jit(solution)/shard_map/all_to_all | solution.py:126
  28.3 135.0 %reduce-scatter.2.cloned.1.call-start = ((), (), s32[]{:S(2)}) async-start(), calls=%async_computation.7 | async-start | bytes 2359296 | tf_op jit(solution)/shard_map/reduce_scatter | solution.py:145
  94.8 0.8 copy-start.6
  97.1 1.0 copy-start.1
  100.5 56.0 %all-to-all-start.3 = ((bf16[16,96,1024]{2,1,0:T(8,128)(2,1)}), bf16[16,96,1024]{2,1,0:T(8,128)(2,1)}, u32[]{:S(2)}, u32[]{:S(2)}) async-start(bf16[16,96,1024]{2,1,0:T(8,128)(2,1)} %bitcast.130), calls=%async_computation.3 | async-start | bytes 6291456 | tf_op jit(solution)/shard_map/all_to_all | solution.py:128
  106.5 48.2 %collective-permute-start = (bf16[16,96,2,128]{3,1,0,2:T(8,128)(2,1)S(1)}, bf16[16,96,2,128]{3,1,0,2:T(8,128)(2,1)}, u32[]{:S(2)}, u32[]{:S(2)}) collective-permute-start(bf16[16,96,2,128]{3,1,0,2:T(8,128)(2,1)S(1)} %fusion.21), channel_id=1, source_target_pairs={{0,1},{1,0},{2,3},{3,2},{4,5},{5,4},{6,7},{7,6},{8,9},{9,8},{10,11... | collective-permute-start | bytes 2359304 | tf_op jit(solution)/shard_map/ppermute | solution.py:13
  156.4 0.9 copy-start.4
  211.7 15.3 %all-to-all-start.5 = ((bf16[8,8,3072]{2,1,0:T(8,128)(2,1)}), bf16[8,8,3072]{2,1,0:T(8,128)(2,1)}, u32[]{:S(2)}, u32[]{:S(2)}) async-start(bf16[8,8,3072]{2,1,0:T(8,128)(2,1)} %convert_element_type.125), calls=%async_computation.6 | async-start | bytes 786432 | tf_op jit(solution)/shard_map/all_to_all | solution.py:170
  227.0 21.5 %all-to-all-start.2 = ((bf16[16,96,3,128]{3,1,2,0:T(8,128)(2,1)}), bf16[16,96,3,128]{3,1,2,0:T(8,128)(2,1)}, u32[]{:S(2)}, u32[]{:S(2)}) async-start(bf16[16,96,3,128]{3,1,2,0:T(8,128)(2,1)} %copy.46), calls=%async_computation.2 | async-start | bytes 2359296 | tf_op jit(solution)/shard_map/all_to_all | solution.py:153
  231.4 30.2 %all-gather.2.cloned.1.call-start = ((), (), s32[]{:S(2)}) async-start(), calls=%async_computation.8 | async-start | bytes 1179648 | tf_op jit(solution)/shard_map/all_gather | solution.py:178
  254.5 5.9 %copy-start.3 = (bf16[1,192,1024]{2,1,0:T(8,128)(2,1)S(1)}, bf16[1,192,1024]{2,1,0:T(8,128)(2,1)}, u32[]{:S(2)}) copy-start(bf16[1,192,1024]{2,1,0:T(8,128)(2,1)} %param.9) | copy-start | bytes 1179652
Sparse Core Ops, SparseCore 0:
  97.3 33.1 reduce-scatter.1
  234.8 23.7 all-gather.1

commit v10 on v8

--- a/solution.py
+++ b/solution.py
@@ -55,7 +55,6 @@
 def attn_pass(recv, part_rows, bias, scale, block_sources=4):
     sources, _, hd = recv.shape
     key_rows = 2 * part_rows
-    nq = sources * part_rows
     nk = sources * key_rows
     kernel = functools.partial(_attn_kernel, scale=scale)
     return pl.pallas_call(
@@ -84,7 +83,7 @@
     )(recv, recv, recv, recv, bias.reshape(1, nk))
 
 
-def per_device(frames, lengths, w_qkv, w_out, cotangent):
+def device_body(frames, lengths, w_qkv, w_out, cotangent):
     width = w_out.shape[0]
     head_size = width // H
     scale = float(head_size) ** (-0.5)
@@ -180,14 +179,14 @@
     grad_qkv = summed[:, : 3 * width]
     grad_out = summed[:, 3 * width :]
     dnormed = jnp.dot(dqkv, w_qkv.T, preferred_element_type=jnp.float32)
-    unused, pull = jax.vjp(layer_norm, inputs)
+    _, pull = jax.vjp(layer_norm, inputs)
     grad_input = (cotangent[0].astype(jnp.float32) + pull(dnormed)[0]).astype(jnp.bfloat16)
     return (output[None], grad_input[None], grad_qkv, grad_out)
 
 
 def solution(mesh):
     return jax.shard_map(
-        per_device,
+        device_body,
         mesh=mesh,
         in_specs=(P("batch", "seq", None), P("batch"), P(), P(), P("batch", "seq", None)),
         out_specs=(

time: 255 us -> 255 us (level)
  no operation moved by 1% of the time
where the time goes in v10:
time: 255 us; the launch traced here: 254 us
  waiting for transfers between devices  80.2 us (31%)
  blocking collectives  55.2 us (22%)
  local copies, waits for them, and re-layouts  28.8 us (11%)
  Pallas kernels  22.9 us (9%)
  starting transfers between devices  21.8 us (9%)
  matrix products  16.8 us (7%)
  between operations  15 us (6%)
  other arithmetic  13.8 us (5%)
    all_to_all x1, blocking collectives, device_body(): lax.all_to_all(parts.reshape(seq_count, share_rows, parts.shape[1]), 'seq...  37.3 us
    all_to_all x1, waiting for transfers between devices, device_body(): recv = lax.all_to_all(send, 'seq', split_axis=0, concat_axis=0, tiled=True)  31.5 us
    ppermute x1, waiting for transfers between devices, from_partner(): lax.ppermute(array, axis, [(i, i ^ 1 << stride) for i in range(lax.axis_s...  27.7 us
    pallas_call x1, Pallas kernels, attn_pass(): pl.pallas_call(kernel, grid=(sources // block_sources,), in_specs=[pl.Blo...  22.9 us
    all_to_all x1, blocking collectives, device_body(): lax.all_to_all(shares.reshape(batch_count, piece_rows, shares.shape[1]),...  17.9 us
    all_to_all x1, waiting for transfers between devices, device_body(): lax.all_to_all(back, 'seq', split_axis=0, concat_axis=0, tiled=True)  14.6 us
    all_to_all x1, starting transfers between devices, device_body(): recv = lax.all_to_all(send, 'seq', split_axis=0, concat_axis=0, tiled=True)  8.6 us
    all_to_all x1, starting transfers between devices, device_body(): lax.all_to_all(back, 'seq', split_axis=0, concat_axis=0, tiled=True)  7.29 us
  transfers between devices with their start and end apart: 5, of which 4 were waited for; matrix products, arithmetic and copies ran while one was open for 10% of the time, Pallas kernels for 9%

profile of v10, /device:TPU:1, one launch (start us, length us, event | category | flops | bytes accessed | tf_op | source)
XLA Modules:
  0.0 254.4 jit_solution(14324225402843750132)
XLA Ops:
  7.2 0.0 copy-start
  7.2 1.3 convert_reduce_fusion.1
  8.5 1.2 multiply_reduce_fusion.1
  9.7 4.4 %fusion.11 = bf16[24,8,24,128]{3,1,2,0:T(8,128)(2,1)S(1)} fusion(bf16[1024,3072]{1,0:T(8,128)(2,1)} %param.7, bf16[1,192,1024]{2,1,0:T(8,128)(2,1)} %param.5, f32[192]{0:T(256)S(1)} %fusion.35, f32[192]{0:T(256)S(1)} %broadcast_multiply_fusion), kind=kOutput, calls=%fused_computation.21 | convolution fusion | flops 1209335808 | bytes 7865856 | tf_op jit(solution)/shard_map/dot_general | solution.py:99
  14.2 0.2 copy.40
  14.4 0.2 fusion.38
  14.6 0.1 copy.27
  14.6 0.8 copy.28
  15.5 0.1 copy.25
  16.2 0.9 fusion.15
  17.1 0.1 copy.41
  17.2 0.1 copy.26
  17.2 0.1 broadcast_in_dim.22
  17.4 0.7 copy-done.9
  18.1 0.1 broadcast_in_dim.23
  18.2 1.6 pad_maximum_fusion.1
  19.8 8.6 %all-to-all-start = ((bf16[16,576,128]{2,1,0:T(8,128)(2,1)}), bf16[16,576,128]{2,1,0:T(8,128)(2,1)}, u32[]{:S(2)}, u32[]{:S(2)}) async-start(bf16[16,576,128]{2,1,0:T(8,128)(2,1)} %pad_maximum_fusion.1), calls=%async_computation | async-start | bytes 4718592 | tf_op jit(solution)/shard_map/all_to_all | solution.py:125
  28.4 0.1 rsqrt.16
  28.5 0.1 div.27
  28.6 0.2 multiply_convert_fusion
  28.8 31.5 %all-to-all-done.q_ref.do_ref.k_ref.v_ref = bf16[16,576,128]{2,1,0:T(8,128)(2,1)} async-done(((bf16[16,576,128]{2,1,0:T(8,128)(2,1)}), bf16[16,576,128]{2,1,0:T(8,128)(2,1)}, u32[]{:S(2)}, u32[]{:S(2)}) %all-to-all-start) | async-done | bytes 2359328 | tf_op jit(solution)/shard_map/all_to_all | solution.py:125
  60.3 2.1 broadcast_in_dim.51
  62.4 4.5 %all-to-all-start.2 = ((bf16[16,96,1024]{2,1,0:T(8,128)(2,1)}), bf16[16,96,1024]{2,1,0:T(8,128)(2,1)}, u32[]{:S(2)}, u32[]{:S(2)}) async-start(bf16[16,96,1024]{2,1,0:T(8,128)(2,1)} %bitcast.126), calls=%async_computation.2 | async-start | bytes 6291456 | tf_op jit(solution)/shard_map/all_to_all | solution.py:127
  66.9 0.6 compare_select_fusion.bias_ref
  67.5 22.9 %shard_map.84 = (bf16[16,96,128]{2,1,0:T(8,128)(2,1)}, bf16[16,96,128]{2,1,0:T(8,128)(2,1)}, f32[3072,128]{1,0:T(8,128)}, f32[3072,128]{1,0:T(8,128)}) custom-call(bf16[16,576,128]{2,1,0:T(8,128)(2,1)} %all-to-all-done.q_ref.do_ref.k_ref.v_ref, bf16[16,576,128]{2,1,0:T(8,128)(2,1)} %all-to-all-done.q_ref.do_ref.k_ref.v_ref, ...), custom_call_target="tpu_custom_call" | custom-call | tf_op jit(solution)/shard_map/pallas_call | solution.py:60
  90.4 1.5 fusion.24
  91.9 1.3 collective-permute-start
  93.1 27.7 %collective-permute-done = bf16[16,96,2,128]{3,1,0,2:T(8,128)(2,1)} collective-permute-done((bf16[16,96,2,128]{3,1,0,2:T(8,128)(2,1)S(1)}, bf16[16,96,2,128]{3,1,0,2:T(8,128)(2,1)}, u32[]{:S(2)}, u32[]{:S(2)}) %collective-permute-start) | collective-permute-done | bytes 786464 | tf_op jit(solution)/shard_map/ppermute | solution.py:13
  120.8 1.8 fusion.8
  122.6 0.2 pad_maximum_fusion.2
  122.8 1.3 copy.31
  124.1 7.3 %all-to-all-start.1 = ((bf16[16,96,4,128]{3,1,2,0:T(8,128)(2,1)}), bf16[16,96,4,128]{3,1,2,0:T(8,128)(2,1)}, u32[]{:S(2)}, u32[]{:S(2)}) async-start(bf16[16,96,4,128]{3,1,2,0:T(8,128)(2,1)} %copy.31), calls=%async_computation.1 | async-start | bytes 3145728 | tf_op jit(solution)/shard_map/all_to_all | solution.py:148
  131.4 0.2 all-gather.2.cloned.1.call-start
  131.6 3.8 %bitcast_convert_fusion = bf16[1024,3,128]{2,0,1:T(8,128)(2,1)S(1)} fusion(bf16[16,96,1024]{2,1,0:T(8,128)(2,1)} %all-to-all-done.2, bf16[16,96,2,128]{3,1,0,2:T(8,128)(2,1)S(1)} %fusion.8, bf16[16,96,1,128]{3,1,0,2:T(8,128)(2,1)} %bitcast.146), kind=kOutput, calls=%fused_computation.19 | convolution fusion | flops 1210712064 | bytes 5111808 | tf_op jit(solution)/shard_map/dot_general | solution.py:155
  135.4 0.7 copy.33
  136.1 1.4 concatenate.29
  137.5 14.6 %all-to-all-done.1 = bf16[16,96,4,128]{3,1,2,0:T(8,128)(2,1)} async-done(((bf16[16,96,4,128]{3,1,2,0:T(8,128)(2,1)}), bf16[16,96,4,128]{3,1,2,0:T(8,128)(2,1)}, u32[]{:S(2)}, u32[]{:S(2)}) %all-to-all-start.1) | async-done | bytes 1572896 | tf_op jit(solution)/shard_map/all_to_all | solution.py:148
  152.2 2.5 copy.49
  154.6 1.1 copy-done.3
  155.8 0.1 slice.41
  155.8 0.9 copy.50
  156.7 1.2 copy.34
  157.9 0.8 convolution_convert_fusion.1
  158.7 0.3 copy-done.6
  159.1 0.3 pad_maximum_fusion
  159.4 37.3 %all_to_all.25 = bf16[16,64,1408]{2,1,0:T(8,128)(2,1)S(1)} all-to-all(bf16[16,64,1408]{2,1,0:T(8,128)(2,1)S(1)} %pad_maximum_fusion), channel_id=1, replica_groups=mesh['batch'=8,'seq'=16] {'seq'}, dimensions={0} | all-to-all | bytes 5767168 | tf_op jit(solution)/shard_map/all_to_all | solution.py:161
  196.7 1.6 copy-done.1
  198.3 0.9 bitcast_reduce_fusion
  199.2 1.4 reshape.168
  200.6 1.2 copy.35
  201.8 1.2 concatenate.31
  202.9 1.9 slice_reduce_fusion
  204.9 17.9 %all_to_all.26 = bf16[8,8,4096]{2,1,0:T(8,128)(2,1)S(1)} all-to-all(bf16[8,8,4096]{2,1,0:T(8,128)(2,1)S(1)} %pad_maximum_fusion.3), channel_id=1, replica_groups=mesh['batch'=8,'seq'=16] {'batch'}, dimensions={0} | all-to-all | bytes 1048576 | tf_op jit(solution)/shard_map/all_to_all | solution.py:174
  222.8 0.7 convert_reduce_fusion
  223.5 0.0 all-gather.2.cloned.1.call-update
  223.5 2.5 slice.42
  226.0 3.0 %reshape.164 = bf16[192,3072]{1,0:T(8,128)(2,1)} reshape(bf16[2,96,3,8,128]{4,3,2,1,0:T(8,128)(2,1)} %slice.42) | data formatting | bytes 2359296 | tf_op jit(solution)/shard_map/reshape | solution.py:151
  229.0 5.6 %multiply_reduce_fusion = (f32[192]{0:T(256)S(1)}, f32[192,1024]{1,0:T(8,128)S(1)}) fusion(bf16[1,192,1024]{2,1,0:T(8,128)(2,1)S(1)} %copy-done.2, f32[192]{0:T(256)S(1)} %broadcast_multiply_fusion, bf16[192,3072]{1,0:T(8,128)(2,1)} %reshape.164, bf16[1024,3072]{1,0:T(8,128)(2,1)} %param.7), kind=kOutput, calls=%fused_computation.44 | convolution fusion | flops 1208745728 | bytes 8652288 | tf_op jit(solution)/shard_map/dot_general | solution.py:181
  234.7 0.4 fusion.37
  235.0 1.3 fusion.14
  236.4 1.1 fusion.27
  237.4 6.4 %all-gather.2.cloned.1.call-done = f32[64,4096]{1,0:T(8,128)} async-done(((f32[8,4096]{1,0:T(8,128)}), f32[64,4096]{1,0:T(8,128)}) %all-gather.2.cloned.1.call-update) | async-done | bytes 1048592 | tf_op jit(solution)/shard_map/all_gather | solution.py:178
  243.8 2.1 slice.45
  245.9 1.7 slice.46
  (26 shorter events, 0.1 us)
Async XLA Ops:
  7.2 9.0 %copy-start = (bf16[1024,1024]{1,0:T(8,128)(2,1)S(1)}, bf16[1024,1024]{1,0:T(8,128)(2,1)}, u32[]{:S(2)}) copy-start(bf16[1024,1024]{1,0:T(8,128)(2,1)} %param.8) | copy-start | bytes 6291460
  14.4 1.8 copy-start.4
  17.1 1.0 copy-start.9
  19.8 8.8 %copy-start.2 = (bf16[1,192,1024]{2,1,0:T(8,128)(2,1)S(1)}, bf16[1,192,1024]{2,1,0:T(8,128)(2,1)}, u32[]{:S(2)}) copy-start(bf16[1,192,1024]{2,1,0:T(8,128)(2,1)} %param.5) | copy-start | bytes 1179652
  19.8 40.5 %all-to-all-start = ((bf16[16,576,128]{2,1,0:T(8,128)(2,1)}), bf16[16,576,128]{2,1,0:T(8,128)(2,1)}, u32[]{:S(2)}, u32[]{:S(2)}) async-start(bf16[16,576,128]{2,1,0:T(8,128)(2,1)} %pad_maximum_fusion.1), calls=%async_computation | async-start | bytes 4718592 | tf_op jit(solution)/shard_map/all_to_all | solution.py:125
  62.4 61.7 %all-to-all-start.2 = ((bf16[16,96,1024]{2,1,0:T(8,128)(2,1)}), bf16[16,96,1024]{2,1,0:T(8,128)(2,1)}, u32[]{:S(2)}, u32[]{:S(2)}) async-start(bf16[16,96,1024]{2,1,0:T(8,128)(2,1)} %bitcast.126), calls=%async_computation.2 | async-start | bytes 6291456 | tf_op jit(solution)/shard_map/all_to_all | solution.py:127
  91.9 28.9 %collective-permute-start = (bf16[16,96,2,128]{3,1,0,2:T(8,128)(2,1)S(1)}, bf16[16,96,2,128]{3,1,0,2:T(8,128)(2,1)}, u32[]{:S(2)}, u32[]{:S(2)}) collective-permute-start(bf16[16,96,2,128]{3,1,0,2:T(8,128)(2,1)S(1)} %fusion.24), channel_id=1, source_target_pairs={{0,1},{1,0},{2,3},{3,2},{4,5},{5,4},{6,7},{7,6},{8,9},{9,8},{10,11... | collective-permute-start | bytes 2359304 | tf_op jit(solution)/shard_map/ppermute | solution.py:13
  93.1 29.5 %copy-start.10 = (bf16[16,96,128]{2,1,0:T(8,128)(2,1)S(1)}, bf16[16,96,128]{2,1,0:T(8,128)(2,1)}, u32[]{:S(2)}) copy-start(bf16[16,96,128]{2,1,0:T(8,128)(2,1)} %get-tuple-element.9) | copy-start | bytes 1179652
  93.1 29.5 %copy-start.11 = (bf16[16,96,128]{2,1,0:T(8,128)(2,1)S(1)}, bf16[16,96,128]{2,1,0:T(8,128)(2,1)}, u32[]{:S(2)}) copy-start(bf16[16,96,128]{2,1,0:T(8,128)(2,1)} %get-tuple-element.8) | copy-start | bytes 1179652
  124.1 28.1 %all-to-all-start.1 = ((bf16[16,96,4,128]{3,1,2,0:T(8,128)(2,1)}), bf16[16,96,4,128]{3,1,2,0:T(8,128)(2,1)}, u32[]{:S(2)}, u32[]{:S(2)}) async-start(bf16[16,96,4,128]{3,1,2,0:T(8,128)(2,1)} %copy.31), calls=%async_computation.1 | async-start | bytes 3145728 | tf_op jit(solution)/shard_map/all_to_all | solution.py:148
  131.4 112.5 %all-gather.2.cloned.1.call-start = ((), (), s32[]{:S(2)}) async-start(), calls=%async_computation.5 | async-start | bytes 1179648 | tf_op jit(solution)/shard_map/all_gather | solution.py:178
  152.1 5.8 %copy-start.5 = (bf16[1,192,1024]{2,1,0:T(8,128)(2,1)S(1)}, bf16[1,192,1024]{2,1,0:T(8,128)(2,1)}, u32[]{:S(2)}) copy-start(bf16[1,192,1024]{2,1,0:T(8,128)(2,1)} %param.9) | copy-start | bytes 1179652
  154.6 1.2 copy-start.3
  155.8 0.9 copy-start.7
  157.9 1.1 copy-start.6
  196.7 1.6 copy-start.1
  229.0 6.0 %copy-start.8 = (bf16[2,96,1,8,128]{4,3,2,1,0:T(8,128)(2,1)S(1)}, bf16[2,96,1,8,128]{4,3,2,1,0:T(8,128)(2,1)}, u32[]{:S(2)}) copy-start(bf16[2,96,1,8,128]{4,3,2,1,0:T(8,128)(2,1)} %copy-done.7) | copy-start | bytes 1179652
Sparse Core Ops, SparseCore 0:
  223.7 20.1 all-gather.1

commit v11 on v8

--- a/solution.py
+++ b/solution.py
@@ -157,26 +157,21 @@
         normed_recv, back[:, :, 1:], over_frames, preferred_element_type=jnp.float32
     ).reshape(width, 3 * head_size)
     out_part = jnp.dot(context.T, grad_rows, preferred_element_type=jnp.float32)
-    share_rows = width // seq_count
+    batch_count = lax.axis_size("batch")
+    piece_rows = width // (seq_count * batch_count)
     parts = jnp.concatenate([qkv_part, out_part], axis=1).astype(jnp.bfloat16)
     gathered = lax.all_to_all(
-        parts.reshape(seq_count, share_rows, parts.shape[1]), "seq", split_axis=0, concat_axis=0, tiled=True
+        parts.reshape(seq_count * batch_count, piece_rows, parts.shape[1]),
+        ("seq", "batch"),
+        split_axis=0,
+        concat_axis=0,
+        tiled=True,
     )
-    qkv_rows = (
-        jnp.sum(gathered[:, :, : 3 * head_size].astype(jnp.float32).reshape(H, groups, share_rows, 3 * head_size), axis=1)
-        .reshape(H, share_rows, 3, head_size)
-        .transpose(1, 2, 0, 3)
-        .reshape(share_rows, 3 * width)
-    )
+    qkv_in = gathered[:, :, : 3 * head_size].astype(jnp.float32)
+    qkv_in = jnp.sum(qkv_in.reshape(H, groups * batch_count, piece_rows, 3 * head_size), axis=1)
+    qkv_rows = qkv_in.reshape(H, piece_rows, 3, head_size).transpose(1, 2, 0, 3).reshape(piece_rows, 3 * width)
     out_rows = jnp.sum(gathered[:, :, 3 * head_size :].astype(jnp.float32), axis=0)
-    batch_count = lax.axis_size("batch")
-    piece_rows = share_rows // batch_count
-    shares = jnp.concatenate([qkv_rows, out_rows], axis=1).astype(jnp.bfloat16)
-    pieces = lax.all_to_all(
-        shares.reshape(batch_count, piece_rows, shares.shape[1]), "batch", split_axis=0, concat_axis=0, tiled=True
-    )
-    summed = jnp.sum(pieces.astype(jnp.float32), axis=0)
-    summed = lax.all_gather(summed, "batch", axis=0, tiled=True)
+    summed = lax.all_gather(jnp.concatenate([qkv_rows, out_rows], axis=1), "batch", axis=0, tiled=True)
     grad_qkv = summed[:, : 3 * width]
     grad_out = summed[:, 3 * width :]
     dnormed = jnp.dot(dqkv, w_qkv.T, preferred_element_type=jnp.float32)

time: 255 us -> 242 us (0.949)
  blocking collectives: 55.2 us -> 48 us
  other arithmetic: 13.8 us -> 11.2 us
    all_to_all x2 -> x1, blocking collectives: 55.2 us -> 48 us  [per_device(): lax.all_to_all(parts.reshape(seq_count * batch_count, piece_rows, parts.s...]
    concatenate x1 -> x3, local copies, waits for them, and re-layouts: 1.44 us -> 5.18 us  [per_device(): parts = jnp.concatenate([qkv_part, out_part], axis=1).astype(jnp.bfloat16)]
  transfers between devices with their start and end apart: 5 -> 5, of which waited for: 4 -> 4; matrix products, arithmetic and copies ran while one was open for 10% -> 11% of each run, Pallas kernels for 9% -> 9%
where the time goes in v11:
time: 242 us; the launch traced here: 241 us
  waiting for transfers between devices  77.9 us (32%)
  blocking collectives  48 us (20%)
  local copies, waits for them, and re-layouts  27.2 us (11%)
  Pallas kernels  22.9 us (9%)
  starting transfers between devices  21.8 us (9%)
  matrix products  16.8 us (7%)
  between operations  15 us (6%)
  other arithmetic  11.2 us (5%)
    all_to_all x1, blocking collectives, per_device(): lax.all_to_all(parts.reshape(seq_count * batch_count, piece_rows, parts.s...  48 us
    all_to_all x1, waiting for transfers between devices, per_device(): recv = lax.all_to_all(send, 'seq', split_axis=0, concat_axis=0, tiled=True)  31.5 us
    ppermute x1, waiting for transfers between devices, from_partner(): lax.ppermute(array, axis, [(i, i ^ 1 << stride) for i in range(lax.axis_s...  27.7 us
    pallas_call x1, Pallas kernels, attn_pass(): pl.pallas_call(kernel, grid=(sources // block_sources,), in_specs=[pl.Blo...  22.9 us
    all_to_all x1, waiting for transfers between devices, per_device(): lax.all_to_all(back, 'seq', split_axis=0, concat_axis=0, tiled=True)  12.5 us
    all_to_all x1, starting transfers between devices, per_device(): recv = lax.all_to_all(send, 'seq', split_axis=0, concat_axis=0, tiled=True)  8.6 us
    all_to_all x1, starting transfers between devices, per_device(): lax.all_to_all(back, 'seq', split_axis=0, concat_axis=0, tiled=True)  7.29 us
    all_gather x1, waiting for transfers between devices, per_device(): lax.all_gather(jnp.concatenate([qkv_rows, out_rows], axis=1), 'batch', ax...  6.21 us
  transfers between devices with their start and end apart: 5, of which 4 were waited for; matrix products, arithmetic and copies ran while one was open for 11% of the time, Pallas kernels for 9%

profile of v11, /device:TPU:1, one launch (start us, length us, event | category | flops | bytes accessed | tf_op | source)
XLA Modules:
  0.0 240.9 jit_solution(12870076498194811854)
XLA Ops:
  7.2 0.0 copy-start
  7.2 1.3 convert_reduce_fusion.2
  8.5 1.2 multiply_reduce_fusion.1
  9.7 4.4 %fusion.11 = bf16[24,8,24,128]{3,1,2,0:T(8,128)(2,1)S(1)} fusion(bf16[1024,3072]{1,0:T(8,128)(2,1)} %param.7, bf16[1,192,1024]{2,1,0:T(8,128)(2,1)} %param.5, f32[192]{0:T(256)S(1)} %fusion.36, f32[192]{0:T(256)S(1)} %broadcast_multiply_fusion), kind=kOutput, calls=%fused_computation.22 | convolution fusion | flops 1209335808 | bytes 7865856 | tf_op jit(solution)/shard_map/dot_general | solution.py:100
  14.2 0.2 copy.59
  14.4 0.0 copy-start.3
  14.4 0.2 fusion.39
  14.6 0.1 copy.40
  14.6 0.8 copy.41
  15.5 0.1 copy.38
  16.2 0.9 fusion.15
  17.1 0.0 copy-start.8
  17.1 0.1 copy.60
  17.2 0.1 copy.39
  17.2 0.1 broadcast_in_dim.22
  17.4 0.7 copy-done.8
  18.1 0.1 broadcast_in_dim.23
  18.2 1.6 pad_maximum_fusion.1
  19.8 8.6 %all-to-all-start = ((bf16[16,576,128]{2,1,0:T(8,128)(2,1)}), bf16[16,576,128]{2,1,0:T(8,128)(2,1)}, u32[]{:S(2)}, u32[]{:S(2)}) async-start(bf16[16,576,128]{2,1,0:T(8,128)(2,1)} %pad_maximum_fusion.1), calls=%async_computation | async-start | bytes 4718592 | tf_op jit(solution)/shard_map/all_to_all | solution.py:126
  28.4 0.1 rsqrt.16
  28.5 0.1 div.27
  28.6 0.2 multiply_convert_fusion
  28.8 31.5 %all-to-all-done.q_ref.do_ref.k_ref.v_ref = bf16[16,576,128]{2,1,0:T(8,128)(2,1)} async-done(((bf16[16,576,128]{2,1,0:T(8,128)(2,1)}), bf16[16,576,128]{2,1,0:T(8,128)(2,1)}, u32[]{:S(2)}, u32[]{:S(2)}) %all-to-all-start) | async-done | bytes 2359328 | tf_op jit(solution)/shard_map/all_to_all | solution.py:126
  60.3 2.1 broadcast_in_dim.51
  62.4 4.5 %all-to-all-start.2 = ((bf16[16,96,1024]{2,1,0:T(8,128)(2,1)}), bf16[16,96,1024]{2,1,0:T(8,128)(2,1)}, u32[]{:S(2)}, u32[]{:S(2)}) async-start(bf16[16,96,1024]{2,1,0:T(8,128)(2,1)} %bitcast.132), calls=%async_computation.2 | async-start | bytes 6291456 | tf_op jit(solution)/shard_map/all_to_all | solution.py:128
  66.9 0.6 compare_select_fusion.bias_ref
  67.5 22.9 %shard_map.84 = (bf16[16,96,128]{2,1,0:T(8,128)(2,1)}, bf16[16,96,128]{2,1,0:T(8,128)(2,1)}, f32[3072,128]{1,0:T(8,128)}, f32[3072,128]{1,0:T(8,128)}) custom-call(bf16[16,576,128]{2,1,0:T(8,128)(2,1)} %all-to-all-done.q_ref.do_ref.k_ref.v_ref, bf16[16,576,128]{2,1,0:T(8,128)(2,1)} %all-to-all-done.q_ref.do_ref.k_ref.v_ref, ...), custom_call_target="tpu_custom_call" | custom-call | tf_op jit(solution)/shard_map/pallas_call | solution.py:61
  90.4 1.5 fusion.24
  91.9 1.3 collective-permute-start
  93.1 27.7 %collective-permute-done = bf16[16,96,2,128]{3,1,0,2:T(8,128)(2,1)} collective-permute-done((bf16[16,96,2,128]{3,1,0,2:T(8,128)(2,1)S(1)}, bf16[16,96,2,128]{3,1,0,2:T(8,128)(2,1)}, u32[]{:S(2)}, u32[]{:S(2)}) %collective-permute-start) | collective-permute-done | bytes 786464 | tf_op jit(solution)/shard_map/ppermute | solution.py:13
  120.8 1.8 fusion.8
  122.6 0.2 pad_maximum_fusion.2
  122.8 1.3 copy.44
  124.1 7.3 %all-to-all-start.1 = ((bf16[16,96,4,128]{3,1,2,0:T(8,128)(2,1)}), bf16[16,96,4,128]{3,1,2,0:T(8,128)(2,1)}, u32[]{:S(2)}, u32[]{:S(2)}) async-start(bf16[16,96,4,128]{3,1,2,0:T(8,128)(2,1)} %copy.44), calls=%async_computation.1 | async-start | bytes 3145728 | tf_op jit(solution)/shard_map/all_to_all | solution.py:149
  131.4 0.2 all-gather.2.cloned.1.call-start
  131.6 3.8 %bitcast_convert_fusion = bf16[1024,3,128]{2,0,1:T(8,128)(2,1)S(1)} fusion(bf16[16,96,1024]{2,1,0:T(8,128)(2,1)} %all-to-all-done.2, bf16[16,96,2,128]{3,1,0,2:T(8,128)(2,1)S(1)} %fusion.8, bf16[16,96,1,128]{3,1,0,2:T(8,128)(2,1)} %bitcast.150), kind=kOutput, calls=%fused_computation.20 | convolution fusion | flops 1210712064 | bytes 5111808 | tf_op jit(solution)/shard_map/dot_general | solution.py:156
  135.4 0.7 copy.46
  136.1 1.4 concatenate.23
  137.5 2.1 copy.49
  139.6 12.5 %all-to-all-done.1 = bf16[16,96,4,128]{3,1,2,0:T(8,128)(2,1)} async-done(((bf16[16,96,4,128]{3,1,2,0:T(8,128)(2,1)}), bf16[16,96,4,128]{3,1,2,0:T(8,128)(2,1)}, u32[]{:S(2)}, u32[]{:S(2)}) %all-to-all-start.1) | async-done | bytes 1572896 | tf_op jit(solution)/shard_map/all_to_all | solution.py:149
  152.1 2.5 %copy.73 = bf16[8,2,96,4,128]{4,0,3,2,1:T(8,128)(2,1)S(1)} copy(bf16[8,2,96,4,128]{4,2,3,1,0:T(8,128)(2,1)} %bitcast.20) | data formatting | bytes 3145728 | tf_op jit(solution)/shard_map/reshape | solution.py:150
  154.6 1.1 copy-done.2
  155.8 0.1 slice.41
  155.8 0.0 copy-start.6
  155.8 0.9 copy.74
  156.7 1.2 copy.47
  157.9 0.8 convolution_convert_fusion.1
  158.7 0.3 copy-done.5
  159.0 0.3 pad_maximum_fusion
  159.3 1.6 copy.50
  161.0 48.0 %all_to_all.20 = bf16[128,8,1408]{2,1,0:T(8,128)(2,1)S(1)} all-to-all(bf16[128,8,1408]{2,1,0:T(8,128)(2,1)S(1)} %copy.50), channel_id=1, replica_groups=mesh['batch'=8,'seq'=16] {'seq','batch'}, dimensions={0} | all-to-all | bytes 5767168 | tf_op jit(solution)/shard_map/all_to_all | solution.py:163
  209.0 0.1 convert_reduce_fusion.1
  209.1 0.4 convert_reduce_fusion
  209.5 0.7 pad_maximum_fusion.3
  210.1 0.0 all-gather.2.cloned.1.call-update
  210.2 2.5 %slice.42 = bf16[2,96,3,8,128]{4,3,2,1,0:T(8,128)(2,1)} slice(bf16[2,96,4,8,128]{4,3,2,1,0:T(8,128)(2,1)} %bitcast.135), slice={[0:2], [0:96], [1:4], [0:8], [0:128]} | slice | bytes 2359296 | tf_op jit(solution)/shard_map/slice | solution.py:152
  212.6 3.0 %reshape.159 = bf16[192,3072]{1,0:T(8,128)(2,1)} reshape(bf16[2,96,3,8,128]{4,3,2,1,0:T(8,128)(2,1)} %slice.42) | data formatting | bytes 2359296 | tf_op jit(solution)/shard_map/reshape | solution.py:152
  215.6 5.6 %multiply_reduce_fusion = (f32[192]{0:T(256)S(1)}, f32[192,1024]{1,0:T(8,128)S(1)}) fusion(bf16[1,192,1024]{2,1,0:T(8,128)(2,1)S(1)} %copy-done.1, f32[192]{0:T(256)S(1)} %broadcast_multiply_fusion, bf16[192,3072]{1,0:T(8,128)(2,1)} %reshape.159, bf16[1024,3072]{1,0:T(8,128)(2,1)} %param.7), kind=kOutput, calls=%fused_computation.43 | convolution fusion | flops 1208745728 | bytes 8652288 | tf_op jit(solution)/shard_map/dot_general | solution.py:177
  221.3 0.4 fusion.38
  221.7 1.3 fusion.14
  223.0 1.1 fusion.28
  224.1 6.2 %all-gather.2.cloned.1.call-done = f32[64,4096]{1,0:T(8,128)} async-done(((f32[8,4096]{1,0:T(8,128)}), f32[64,4096]{1,0:T(8,128)}) %all-gather.2.cloned.1.call-update) | async-done | bytes 1048592 | tf_op jit(solution)/shard_map/all_gather | solution.py:174
  230.3 2.1 slice.45
  232.3 1.7 slice.46
  (23 shorter events, 0.1 us)
Async XLA Ops:
  7.2 9.0 %copy-start = (bf16[1024,1024]{1,0:T(8,128)(2,1)S(1)}, bf16[1024,1024]{1,0:T(8,128)(2,1)}, u32[]{:S(2)}) copy-start(bf16[1024,1024]{1,0:T(8,128)(2,1)} %param.8) | copy-start | bytes 6291460
  14.4 1.8 copy-start.3
  17.1 1.0 copy-start.8
  19.8 8.8 %copy-start.1 = (bf16[1,192,1024]{2,1,0:T(8,128)(2,1)S(1)}, bf16[1,192,1024]{2,1,0:T(8,128)(2,1)}, u32[]{:S(2)}) copy-start(bf16[1,192,1024]{2,1,0:T(8,128)(2,1)} %param.5) | copy-start | bytes 1179652
  19.8 40.5 %all-to-all-start = ((bf16[16,576,128]{2,1,0:T(8,128)(2,1)}), bf16[16,576,128]{2,1,0:T(8,128)(2,1)}, u32[]{:S(2)}, u32[]{:S(2)}) async-start(bf16[16,576,128]{2,1,0:T(8,128)(2,1)} %pad_maximum_fusion.1), calls=%async_computation | async-start | bytes 4718592 | tf_op jit(solution)/shard_map/all_to_all | solution.py:126
  62.4 61.7 %all-to-all-start.2 = ((bf16[16,96,1024]{2,1,0:T(8,128)(2,1)}), bf16[16,96,1024]{2,1,0:T(8,128)(2,1)}, u32[]{:S(2)}, u32[]{:S(2)}) async-start(bf16[16,96,1024]{2,1,0:T(8,128)(2,1)} %bitcast.132), calls=%async_computation.2 | async-start | bytes 6291456 | tf_op jit(solution)/shard_map/all_to_all | solution.py:128
  91.9 28.9 %collective-permute-start = (bf16[16,96,2,128]{3,1,0,2:T(8,128)(2,1)S(1)}, bf16[16,96,2,128]{3,1,0,2:T(8,128)(2,1)}, u32[]{:S(2)}, u32[]{:S(2)}) collective-permute-start(bf16[16,96,2,128]{3,1,0,2:T(8,128)(2,1)S(1)} %fusion.24), channel_id=1, source_target_pairs={{0,1},{1,0},{2,3},{3,2},{4,5},{5,4},{6,7},{7,6},{8,9},{9,8},{10,11... | collective-permute-start | bytes 2359304 | tf_op jit(solution)/shard_map/ppermute | solution.py:13
  93.1 29.5 %copy-start.9 = (bf16[16,96,128]{2,1,0:T(8,128)(2,1)S(1)}, bf16[16,96,128]{2,1,0:T(8,128)(2,1)}, u32[]{:S(2)}) copy-start(bf16[16,96,128]{2,1,0:T(8,128)(2,1)} %get-tuple-element.9) | copy-start | bytes 1179652
  93.1 29.5 %copy-start.10 = (bf16[16,96,128]{2,1,0:T(8,128)(2,1)S(1)}, bf16[16,96,128]{2,1,0:T(8,128)(2,1)}, u32[]{:S(2)}) copy-start(bf16[16,96,128]{2,1,0:T(8,128)(2,1)} %get-tuple-element.8) | copy-start | bytes 1179652
  124.1 28.1 %all-to-all-start.1 = ((bf16[16,96,4,128]{3,1,2,0:T(8,128)(2,1)}), bf16[16,96,4,128]{3,1,2,0:T(8,128)(2,1)}, u32[]{:S(2)}, u32[]{:S(2)}) async-start(bf16[16,96,4,128]{3,1,2,0:T(8,128)(2,1)} %copy.44), calls=%async_computation.1 | async-start | bytes 3145728 | tf_op jit(solution)/shard_map/all_to_all | solution.py:149
  131.4 98.9 %all-gather.2.cloned.1.call-start = ((), (), s32[]{:S(2)}) async-start(), calls=%async_computation.4 | async-start | bytes 1179648 | tf_op jit(solution)/shard_map/all_gather | solution.py:174
  152.1 5.8 %copy-start.4 = (bf16[1,192,1024]{2,1,0:T(8,128)(2,1)S(1)}, bf16[1,192,1024]{2,1,0:T(8,128)(2,1)}, u32[]{:S(2)}) copy-start(bf16[1,192,1024]{2,1,0:T(8,128)(2,1)} %param.9) | copy-start | bytes 1179652
  154.6 1.2 copy-start.2
  155.8 0.9 copy-start.6
  157.9 1.1 copy-start.5
  215.6 6.0 %copy-start.7 = (bf16[2,96,1,8,128]{4,3,2,1,0:T(8,128)(2,1)S(1)}, bf16[2,96,1,8,128]{4,3,2,1,0:T(8,128)(2,1)}, u32[]{:S(2)}) copy-start(bf16[2,96,1,8,128]{4,3,2,1,0:T(8,128)(2,1)} %copy-done.6) | copy-start | bytes 1179652
Sparse Core Ops, SparseCore 0:
  210.3 19.9 all-gather.1

commit v12 on v11

--- a/solution.py
+++ b/solution.py
@@ -1,7 +1,7 @@
 import jax
 import jax.numpy as jnp
 from jax import lax
-from jax.sharding import PartitionSpec as P
+from jax.sharding import Mesh, PartitionSpec as P
 from jax.experimental import pallas as pl
 from jax.experimental.pallas import tpu as pltpu
 import functools
@@ -157,21 +157,28 @@
         normed_recv, back[:, :, 1:], over_frames, preferred_element_type=jnp.float32
     ).reshape(width, 3 * head_size)
     out_part = jnp.dot(context.T, grad_rows, preferred_element_type=jnp.float32)
-    batch_count = lax.axis_size("batch")
-    piece_rows = width // (seq_count * batch_count)
+    y_count = lax.axis_size("y")
+    core_count = lax.axis_size("core")
+    core_index = lax.axis_index("core")
+    piece_rows = width // (seq_count * y_count * core_count)
     parts = jnp.concatenate([qkv_part, out_part], axis=1).astype(jnp.bfloat16)
+    parts = parts.reshape(seq_count, y_count, core_count, piece_rows, parts.shape[1])
+    own = lax.dynamic_index_in_dim(parts, core_index, 2, keepdims=False)
+    other = lax.dynamic_index_in_dim(parts, 1 - core_index, 2, keepdims=False)
+    from_core = lax.ppermute(other, "core", [(0, 1), (1, 0)])
+    chip_sum = (own.astype(jnp.float32) + from_core.astype(jnp.float32)).astype(jnp.bfloat16)
     gathered = lax.all_to_all(
-        parts.reshape(seq_count * batch_count, piece_rows, parts.shape[1]),
-        ("seq", "batch"),
+        chip_sum.reshape(seq_count * y_count, piece_rows, parts.shape[-1]),
+        ("seq", "y"),
         split_axis=0,
         concat_axis=0,
         tiled=True,
     )
     qkv_in = gathered[:, :, : 3 * head_size].astype(jnp.float32)
-    qkv_in = jnp.sum(qkv_in.reshape(H, groups * batch_count, piece_rows, 3 * head_size), axis=1)
+    qkv_in = jnp.sum(qkv_in.reshape(H, groups * y_count, piece_rows, 3 * head_size), axis=1)
     qkv_rows = qkv_in.reshape(H, piece_rows, 3, head_size).transpose(1, 2, 0, 3).reshape(piece_rows, 3 * width)
     out_rows = jnp.sum(gathered[:, :, 3 * head_size :].astype(jnp.float32), axis=0)
-    summed = lax.all_gather(jnp.concatenate([qkv_rows, out_rows], axis=1), "batch", axis=0, tiled=True)
+    summed = lax.all_gather(jnp.concatenate([qkv_rows, out_rows], axis=1), ("y", "core"), axis=0, tiled=True)
     grad_qkv = summed[:, : 3 * width]
     grad_out = summed[:, 3 * width :]
     dnormed = jnp.dot(dqkv, w_qkv.T, preferred_element_type=jnp.float32)
@@ -181,13 +188,16 @@
 
 
 def solution(mesh):
+    batch_size = mesh.shape["batch"]
+    fine = Mesh(mesh.devices.reshape(batch_size // 2, 2, mesh.shape["seq"]), ("y", "core", "seq"))
+    batch = ("y", "core")
     return jax.shard_map(
         per_device,
-        mesh=mesh,
-        in_specs=(P("batch", "seq", None), P("batch"), P(), P(), P("batch", "seq", None)),
+        mesh=fine,
+        in_specs=(P(batch, "seq", None), P(batch), P(), P(), P(batch, "seq", None)),
         out_specs=(
-            P("batch", "seq", None),
-            P("batch", "seq", None),
+            P(batch, "seq", None),
+            P(batch, "seq", None),
             P("seq", None),
             P("seq", None),
         ),

time: 242 us -> 234 us (0.967)
  blocking collectives: 48 us -> 27.4 us
  waiting for transfers between devices: 77.9 us -> 82.5 us
  starting transfers between devices: 21.8 us -> 25.9 us
  other arithmetic: 11.2 us -> 14.2 us
    all_to_all x1, blocking collectives: 48 us -> 27.4 us  [per_device(): lax.all_to_all(chip_sum.reshape(seq_count * y_count, piece_rows, parts.sh...]
    ppermute x0 -> x1, starting transfers between devices: none -> 4.02 us  [per_device(): from_core = lax.ppermute(other, 'core', [(0, 1), (1, 0)])]
    ppermute x0 -> x1, waiting for transfers between devices: none -> 3.19 us  [per_device(): from_core = lax.ppermute(other, 'core', [(0, 1), (1, 0)])]
    concatenate x3 -> x1, local copies, waits for them, and re-layouts: 5.18 us -> 2.45 us  [per_device(): parts = jnp.concatenate([qkv_part, out_part], axis=1).astype(jnp.bfloat16)]
  transfers between devices with their start and end apart: 5 -> 6, of which waited for: 4 -> 5; matrix products, arithmetic and copies ran while one was open for 11% -> 12% of each run, Pallas kernels for 9% -> 10%
where the time goes in v12:
time: 234 us; the launch traced here: 233 us
  waiting for transfers between devices  82.5 us (35%)
  blocking collectives  27.4 us (12%)
  local copies, waits for them, and re-layouts  26.9 us (11%)
  starting transfers between devices  25.9 us (11%)
  Pallas kernels  22.9 us (10%)
  matrix products  18 us (8%)
  between operations  15 us (6%)
  other arithmetic  14.2 us (6%)
    all_to_all x1, waiting for transfers between devices, per_device(): recv = lax.all_to_all(send, 'seq', split_axis=0, concat_axis=0, tiled=True)  31.5 us
    ppermute x1, waiting for transfers between devices, from_partner(): lax.ppermute(array, axis, [(i, i ^ 1 << stride) for i in range(lax.axis_s...  27.7 us
    all_to_all x1, blocking collectives, per_device(): lax.all_to_all(chip_sum.reshape(seq_count * y_count, piece_rows, parts.sh...  27.4 us
    pallas_call x1, Pallas kernels, attn_pass(): pl.pallas_call(kernel, grid=(sources // block_sources,), in_specs=[pl.Blo...  22.9 us
    all_to_all x1, waiting for transfers between devices, per_device(): lax.all_to_all(back, 'seq', split_axis=0, concat_axis=0, tiled=True)  12.6 us
    all_to_all x1, starting transfers between devices, per_device(): recv = lax.all_to_all(send, 'seq', split_axis=0, concat_axis=0, tiled=True)  8.6 us
    all_gather x1, waiting for transfers between devices, per_device(): lax.all_gather(jnp.concatenate([qkv_rows, out_rows], axis=1), ('y', 'core...  7.55 us
    all_to_all x1, starting transfers between devices, per_device(): lax.all_to_all(back, 'seq', split_axis=0, concat_axis=0, tiled=True)  7.29 us
  transfers between devices with their start and end apart: 6, of which 5 were waited for; matrix products, arithmetic and copies ran while one was open for 12% of the time, Pallas kernels for 10%

profile of v12, /device:TPU:1, one launch (start us, length us, event | category | flops | bytes accessed | tf_op | source)
XLA Modules:
  0.0 232.8 jit_solution(1583968184324999667)
XLA Ops:
  7.2 0.0 copy-start
  7.2 1.3 convert_reduce_fusion.2
  8.5 1.2 multiply_reduce_fusion.1
  9.7 4.4 %fusion.16 = bf16[24,8,24,128]{3,1,2,0:T(8,128)(2,1)S(1)} fusion(bf16[1024,3072]{1,0:T(8,128)(2,1)} %param.7, bf16[1,192,1024]{2,1,0:T(8,128)(2,1)} %param.5, f32[192]{0:T(256)S(1)} %fusion.40, f32[192]{0:T(256)S(1)} %broadcast_multiply_fusion), kind=kOutput, calls=%fused_computation.30 | convolution fusion | flops 1209335808 | bytes 7865856 | tf_op jit(solution)/shard_map/dot_general | solution.py:100
  14.2 0.2 copy.50
  14.4 0.0 copy-start.4
  14.4 0.2 fusion.43
  14.6 0.1 copy.36
  14.6 0.8 copy.37
  15.5 0.1 copy.34
  16.2 0.9 fusion.20
  17.1 0.1 copy.51
  17.2 0.1 copy.35
  17.2 0.1 broadcast_in_dim.22
  17.4 0.7 copy-done.8
  18.1 0.1 broadcast_in_dim.23
  18.2 1.6 pad_maximum_fusion
  19.8 8.6 %all-to-all-start = ((bf16[16,576,128]{2,1,0:T(8,128)(2,1)}), bf16[16,576,128]{2,1,0:T(8,128)(2,1)}, u32[]{:S(2)}, u32[]{:S(2)}) async-start(bf16[16,576,128]{2,1,0:T(8,128)(2,1)} %pad_maximum_fusion), calls=%async_computation | async-start | bytes 4718592 | tf_op jit(solution)/shard_map/all_to_all | solution.py:126
  28.4 0.1 rsqrt.16
  28.5 0.1 div.27
  28.6 0.2 multiply_convert_fusion
  28.8 31.5 %all-to-all-done.q_ref.do_ref.k_ref.v_ref = bf16[16,576,128]{2,1,0:T(8,128)(2,1)} async-done(((bf16[16,576,128]{2,1,0:T(8,128)(2,1)}), bf16[16,576,128]{2,1,0:T(8,128)(2,1)}, u32[]{:S(2)}, u32[]{:S(2)}) %all-to-all-start) | async-done | bytes 2359328 | tf_op jit(solution)/shard_map/all_to_all | solution.py:126
  60.3 2.1 broadcast_in_dim.51
  62.4 4.5 %all-to-all-start.2 = ((bf16[16,96,1024]{2,1,0:T(8,128)(2,1)}), bf16[16,96,1024]{2,1,0:T(8,128)(2,1)}, u32[]{:S(2)}, u32[]{:S(2)}) async-start(bf16[16,96,1024]{2,1,0:T(8,128)(2,1)} %bitcast.144), calls=%async_computation.2 | async-start | bytes 6291456 | tf_op jit(solution)/shard_map/all_to_all | solution.py:128
  66.9 0.6 compare_select_fusion.bias_ref
  67.5 22.9 %shard_map.84 = (bf16[16,96,128]{2,1,0:T(8,128)(2,1)}, bf16[16,96,128]{2,1,0:T(8,128)(2,1)}, f32[3072,128]{1,0:T(8,128)}, f32[3072,128]{1,0:T(8,128)}) custom-call(bf16[16,576,128]{2,1,0:T(8,128)(2,1)} %all-to-all-done.q_ref.do_ref.k_ref.v_ref, bf16[16,576,128]{2,1,0:T(8,128)(2,1)} %all-to-all-done.q_ref.do_ref.k_ref.v_ref, ...), custom_call_target="tpu_custom_call" | custom-call | tf_op jit(solution)/shard_map/pallas_call | solution.py:61
  90.4 1.5 fusion.29
  91.9 1.3 collective-permute-start
  93.1 27.7 %collective-permute-done = bf16[16,96,2,128]{3,1,0,2:T(8,128)(2,1)} collective-permute-done((bf16[16,96,2,128]{3,1,0,2:T(8,128)(2,1)S(1)}, bf16[16,96,2,128]{3,1,0,2:T(8,128)(2,1)}, u32[]{:S(2)}, u32[]{:S(2)}) %collective-permute-start) | collective-permute-done | bytes 786464 | tf_op jit(solution)/shard_map/ppermute | solution.py:13
  120.8 1.8 fusion.9
  122.6 0.2 pad_maximum_fusion.1
  122.8 1.3 copy.40
  124.1 7.3 %all-to-all-start.1 = ((bf16[16,96,4,128]{3,1,2,0:T(8,128)(2,1)}), bf16[16,96,4,128]{3,1,2,0:T(8,128)(2,1)}, u32[]{:S(2)}, u32[]{:S(2)}) async-start(bf16[16,96,4,128]{3,1,2,0:T(8,128)(2,1)} %copy.40), calls=%async_computation.1 | async-start | bytes 3145728 | tf_op jit(solution)/shard_map/all_to_all | solution.py:149
  131.4 0.2 all-gather.2.cloned.1.call-start
  131.6 3.8 %bitcast_convert_fusion = bf16[1024,3,128]{2,0,1:T(8,128)(2,1)S(1)} fusion(bf16[16,96,1024]{2,1,0:T(8,128)(2,1)} %all-to-all-done.2, bf16[16,96,2,128]{3,1,0,2:T(8,128)(2,1)S(1)} %fusion.9, bf16[16,96,1,128]{3,1,0,2:T(8,128)(2,1)} %bitcast.163), kind=kOutput, calls=%fused_computation.24 | convolution fusion | flops 1210712064 | bytes 5111808 | tf_op jit(solution)/shard_map/dot_general | solution.py:156
  135.4 1.7 copy.42
  137.1 2.4 %concatenate.23 = bf16[16,4,2,8,384]{4,3,2,1,0:T(8,128)(2,1)S(1)} reshape(bf16[1024,3,128]{2,1,0:T(4,128)(2,1)} %copy.42) | data formatting | bytes 1572864 | tf_op jit(solution)/shard_map/concatenate | solution.py:164
  139.5 12.6 %all-to-all-done.1 = bf16[16,96,4,128]{3,1,2,0:T(8,128)(2,1)} async-done(((bf16[16,96,4,128]{3,1,2,0:T(8,128)(2,1)}), bf16[16,96,4,128]{3,1,2,0:T(8,128)(2,1)}, u32[]{:S(2)}, u32[]{:S(2)}) %all-to-all-start.1) | async-done | bytes 1572896 | tf_op jit(solution)/shard_map/all_to_all | solution.py:149
  152.1 2.4 %copy.62 = bf16[8,2,96,4,128]{4,0,3,2,1:T(8,128)(2,1)S(1)} copy(bf16[8,2,96,4,128]{4,2,3,1,0:T(8,128)(2,1)} %bitcast.20) | data formatting | bytes 3145728 | tf_op jit(solution)/shard_map/reshape | solution.py:150
  154.6 1.1 copy-done.3
  155.7 0.1 slice.41
  155.8 0.7 copy-done.6
  156.5 0.8 copy.63
  157.3 2.0 copy.43
  159.3 1.9 convolution_convert_fusion.1
  161.3 1.4 fusion.13
  162.7 0.3 copy-done.1
  163.0 4.0 %collective-permute-start.1 = (bf16[16,4,8,1408]{3,2,1,0:T(8,128)(2,1)}, bf16[16,4,8,1408]{3,2,1,0:T(8,128)(2,1)}, u32[]{:S(2)}, u32[]{:S(2)}) collective-permute-start(bf16[16,4,8,1408]{3,2,1,0:T(8,128)(2,1)} %fusion.13), channel_id=1, source_target_pairs={{0,16},{16,0},{1,17},{17,1},{2,18},{18,2},{3,19},{19,3},{4,20},{20... | collective-permute-start | bytes 4325384 | tf_op jit(solution)/shard_map/ppermute | solution.py:168
  167.1 3.2 %collective-permute-done.1 = bf16[16,4,8,1408]{3,2,1,0:T(8,128)(2,1)} collective-permute-done((bf16[16,4,8,1408]{3,2,1,0:T(8,128)(2,1)}, bf16[16,4,8,1408]{3,2,1,0:T(8,128)(2,1)}, u32[]{:S(2)}, u32[]{:S(2)}) %collective-permute-start.1) | collective-permute-done | bytes 1441824 | tf_op jit(solution)/shard_map/ppermute | solution.py:168
  170.3 2.0 fusion.2
  172.3 27.4 %all_to_all.20 = bf16[64,8,1408]{2,1,0:T(8,128)(2,1)S(1)} all-to-all(bf16[64,8,1408]{2,1,0:T(8,128)(2,1)S(1)} %bitcast.152), channel_id=1, replica_groups=mesh['y'=4,'core'=2,'seq'=16] {'seq','y'}, dimensions={0} | all-to-all | bytes 2883584 | tf_op jit(solution)/shard_map/all_to_all | solution.py:170
  199.7 0.1 convert_reduce_fusion.1
  199.8 0.2 convert_reduce_fusion
  200.0 0.7 pad_maximum_fusion.2
  200.6 0.0 all-gather.2.cloned.1.call-update
  200.7 2.5 %slice.42 = bf16[2,96,3,8,128]{4,3,2,1,0:T(8,128)(2,1)} slice(bf16[2,96,4,8,128]{4,3,2,1,0:T(8,128)(2,1)} %bitcast.147), slice={[0:2], [0:96], [1:4], [0:8], [0:128]} | slice | bytes 2359296 | tf_op jit(solution)/shard_map/slice | solution.py:152
  203.2 3.0 %reshape.164 = bf16[192,3072]{1,0:T(8,128)(2,1)} reshape(bf16[2,96,3,8,128]{4,3,2,1,0:T(8,128)(2,1)} %slice.42) | data formatting | bytes 2359296 | tf_op jit(solution)/shard_map/reshape | solution.py:152
  206.2 5.7 %multiply_reduce_fusion = (f32[192]{0:T(256)S(1)}, f32[192,1024]{1,0:T(8,128)S(1)}) fusion(bf16[1,192,1024]{2,1,0:T(8,128)(2,1)S(1)} %copy-done.2, f32[192]{0:T(256)S(1)} %broadcast_multiply_fusion, bf16[192,3072]{1,0:T(8,128)(2,1)} %reshape.164, bf16[1024,3072]{1,0:T(8,128)(2,1)} %param.7), kind=kOutput, calls=%fused_computation.52 | convolution fusion | flops 1208745728 | bytes 8652288 | tf_op jit(solution)/shard_map/dot_general | solution.py:184
  211.9 0.4 fusion.42
  212.3 1.3 fusion.19
  213.6 1.1 fusion.32
  214.7 7.6 %all-gather.2.cloned.1.call-done = f32[64,4096]{1,0:T(8,128)} async-done(((f32[8,4096]{1,0:T(8,128)}), f32[64,4096]{1,0:T(8,128)}) %all-gather.2.cloned.1.call-update) | async-done | bytes 1048592 | tf_op jit(solution)/shard_map/all_gather | solution.py:181
  222.2 2.1 slice.45
  224.3 1.7 slice.46
  (24 shorter events, 0.1 us)
Async XLA Ops:
  7.2 9.0 %copy-start = (bf16[1024,1024]{1,0:T(8,128)(2,1)S(1)}, bf16[1024,1024]{1,0:T(8,128)(2,1)}, u32[]{:S(2)}) copy-start(bf16[1024,1024]{1,0:T(8,128)(2,1)} %param.8) | copy-start | bytes 6291460
  14.4 1.8 copy-start.4
  17.1 1.0 copy-start.8
  19.8 8.8 %copy-start.2 = (bf16[1,192,1024]{2,1,0:T(8,128)(2,1)S(1)}, bf16[1,192,1024]{2,1,0:T(8,128)(2,1)}, u32[]{:S(2)}) copy-start(bf16[1,192,1024]{2,1,0:T(8,128)(2,1)} %param.5) | copy-start | bytes 1179652
  19.8 40.5 %all-to-all-start = ((bf16[16,576,128]{2,1,0:T(8,128)(2,1)}), bf16[16,576,128]{2,1,0:T(8,128)(2,1)}, u32[]{:S(2)}, u32[]{:S(2)}) async-start(bf16[16,576,128]{2,1,0:T(8,128)(2,1)} %pad_maximum_fusion), calls=%async_computation | async-start | bytes 4718592 | tf_op jit(solution)/shard_map/all_to_all | solution.py:126
  62.4 61.7 %all-to-all-start.2 = ((bf16[16,96,1024]{2,1,0:T(8,128)(2,1)}), bf16[16,96,1024]{2,1,0:T(8,128)(2,1)}, u32[]{:S(2)}, u32[]{:S(2)}) async-start(bf16[16,96,1024]{2,1,0:T(8,128)(2,1)} %bitcast.144), calls=%async_computation.2 | async-start | bytes 6291456 | tf_op jit(solution)/shard_map/all_to_all | solution.py:128
  91.9 28.9 %collective-permute-start = (bf16[16,96,2,128]{3,1,0,2:T(8,128)(2,1)S(1)}, bf16[16,96,2,128]{3,1,0,2:T(8,128)(2,1)}, u32[]{:S(2)}, u32[]{:S(2)}) collective-permute-start(bf16[16,96,2,128]{3,1,0,2:T(8,128)(2,1)S(1)} %fusion.29), channel_id=1, source_target_pairs={{0,1},{1,0},{2,3},{3,2},{4,5},{5,4},{6,7},{7,6},{8,9},{9,8},{10,11... | collective-permute-start | bytes 2359304 | tf_op jit(solution)/shard_map/ppermute | solution.py:13
  93.1 29.5 %copy-start.9 = (bf16[16,96,128]{2,1,0:T(8,128)(2,1)S(1)}, bf16[16,96,128]{2,1,0:T(8,128)(2,1)}, u32[]{:S(2)}) copy-start(bf16[16,96,128]{2,1,0:T(8,128)(2,1)} %get-tuple-element.9) | copy-start | bytes 1179652
  93.1 29.5 %copy-start.10 = (bf16[16,96,128]{2,1,0:T(8,128)(2,1)S(1)}, bf16[16,96,128]{2,1,0:T(8,128)(2,1)}, u32[]{:S(2)}) copy-start(bf16[16,96,128]{2,1,0:T(8,128)(2,1)} %get-tuple-element.8) | copy-start | bytes 1179652
  124.1 28.1 %all-to-all-start.1 = ((bf16[16,96,4,128]{3,1,2,0:T(8,128)(2,1)}), bf16[16,96,4,128]{3,1,2,0:T(8,128)(2,1)}, u32[]{:S(2)}, u32[]{:S(2)}) async-start(bf16[16,96,4,128]{3,1,2,0:T(8,128)(2,1)} %copy.40), calls=%async_computation.1 | async-start | bytes 3145728 | tf_op jit(solution)/shard_map/all_to_all | solution.py:149
  131.4 90.9 %all-gather.2.cloned.1.call-start = ((), (), s32[]{:S(2)}) async-start(), calls=%async_computation.4 | async-start | bytes 1179648 | tf_op jit(solution)/shard_map/all_gather | solution.py:181
  154.6 1.1 copy-start.3
  155.8 0.7 copy-start.6
  161.3 1.8 copy-start.1
  163.0 7.2 %collective-permute-start.1 = (bf16[16,4,8,1408]{3,2,1,0:T(8,128)(2,1)}, bf16[16,4,8,1408]{3,2,1,0:T(8,128)(2,1)}, u32[]{:S(2)}, u32[]{:S(2)}) collective-permute-start(bf16[16,4,8,1408]{3,2,1,0:T(8,128)(2,1)} %fusion.13), channel_id=1, source_target_pairs={{0,16},{16,0},{1,17},{17,1},{2,18},{18,2},{3,19},{19,3},{4,20},{20... | collective-permute-start | bytes 4325384 | tf_op jit(solution)/shard_map/ppermute | solution.py:168
  206.2 6.1 %copy-start.7 = (bf16[2,96,1,8,128]{4,3,2,1,0:T(8,128)(2,1)S(1)}, bf16[2,96,1,8,128]{4,3,2,1,0:T(8,128)(2,1)}, u32[]{:S(2)}) copy-start(bf16[2,96,1,8,128]{4,3,2,1,0:T(8,128)(2,1)} %copy-done.6) | copy-start | bytes 1179652
  211.9 1.7 copy-start.5
Sparse Core Ops, SparseCore 0:
  200.8 21.3 all-gather.1

commit v13 on v12

--- a/solution.py
+++ b/solution.py
@@ -147,7 +147,8 @@
         axis=2,
     )
     returned = lax.all_to_all(back, "seq", split_axis=0, concat_axis=0, tiled=True)
-    returned = returned.reshape(H, groups, part_rows, 4, head_size).transpose(1, 2, 3, 0, 4)
+    returned_heads = returned.reshape(H, groups, part_rows, 4, head_size)
+    returned = returned_heads.transpose(1, 2, 3, 0, 4)
     context = returned[:, :, 0].reshape(tok_rows, width)
     dqkv = returned[:, :, 1:].reshape(tok_rows, 3 * width)
     branch = jnp.dot(context, w_out, preferred_element_type=jnp.float32)
@@ -181,7 +182,12 @@
     summed = lax.all_gather(jnp.concatenate([qkv_rows, out_rows], axis=1), ("y", "core"), axis=0, tiled=True)
     grad_qkv = summed[:, : 3 * width]
     grad_out = summed[:, 3 * width :]
-    dnormed = jnp.dot(dqkv, w_qkv.T, preferred_element_type=jnp.float32)
+    dnormed = lax.dot_general(
+        returned_heads[:, :, :, 1:],
+        w_qkv.reshape(width, 3, H, head_size),
+        (((0, 3, 4), (2, 1, 3)), ((), ())),
+        preferred_element_type=jnp.float32,
+    ).reshape(tok_rows, width)
     unused, pull = jax.vjp(layer_norm, inputs)
     grad_input = (cotangent[0].astype(jnp.float32) + pull(dnormed)[0]).astype(jnp.bfloat16)
     return (output[None], grad_input[None], grad_qkv, grad_out)

time: 234 us -> 233 us (level)
  matrix products: 18 us -> 14.7 us
  waiting for transfers between devices: 82.5 us -> 85.2 us
    unnamed x26, local copies, waits for them, and re-layouts: 4.06 us -> 7.78 us
    dot_general x1, matrix products: 5.7 us -> 2.34 us  [per_device(): lax.dot_general(returned_heads[:, :, :, 1:], w_qkv.reshape(width, 3, H, h...]
    reshape x2 -> x1, local copies, waits for them, and re-layouts: 5.41 us -> 2.42 us  [per_device(): returned_heads = returned.reshape(H, groups, part_rows, 4, head_size)]
    all_gather x1, waiting for transfers between devices: 7.55 us -> 10.2 us  [per_device(): lax.all_gather(jnp.concatenate([qkv_rows, out_rows], axis=1), ('y', 'core...]
  transfers between devices with their start and end apart: 6 -> 6, of which waited for: 5 -> 5; matrix products, arithmetic and copies ran while one was open for 12% -> 11% of each run, Pallas kernels for 10% -> 10%
where the time goes in v13:
time: 233 us; the launch traced here: 232 us
  waiting for transfers between devices  85.2 us (37%)
  blocking collectives  27.4 us (12%)
  local copies, waits for them, and re-layouts  26.5 us (11%)
  starting transfers between devices  25.9 us (11%)
  Pallas kernels  22.8 us (10%)
  between operations  15 us (6%)
  matrix products  14.7 us (6%)
  other arithmetic  14.2 us (6%)
    all_to_all x1, waiting for transfers between devices, per_device(): recv = lax.all_to_all(send, 'seq', split_axis=0, concat_axis=0, tiled=True)  31.5 us
    ppermute x1, waiting for transfers between devices, from_partner(): lax.ppermute(array, axis, [(i, i ^ 1 << stride) for i in range(lax.axis_s...  27.7 us
    all_to_all x1, blocking collectives, per_device(): lax.all_to_all(chip_sum.reshape(seq_count * y_count, piece_rows, parts.sh...  27.4 us
    pallas_call x1, Pallas kernels, attn_pass(): pl.pallas_call(kernel, grid=(sources // block_sources,), in_specs=[pl.Blo...  22.8 us
    all_to_all x1, waiting for transfers between devices, per_device(): lax.all_to_all(back, 'seq', split_axis=0, concat_axis=0, tiled=True)  12.6 us
    all_gather x1, waiting for transfers between devices, per_device(): lax.all_gather(jnp.concatenate([qkv_rows, out_rows], axis=1), ('y', 'core...  10.2 us
    all_to_all x1, starting transfers between devices, per_device(): recv = lax.all_to_all(send, 'seq', split_axis=0, concat_axis=0, tiled=True)  8.6 us
    unnamed x26, local copies, waits for them, and re-layouts  7.78 us
  transfers between devices with their start and end apart: 6, of which 5 were waited for; matrix products, arithmetic and copies ran while one was open for 11% of the time, Pallas kernels for 10%

profile of v13, /device:TPU:1, one launch (start us, length us, event | category | flops | bytes accessed | tf_op | source)
XLA Modules:
  0.0 231.7 jit_solution(6832662194457667207)
XLA Ops:
  7.2 0.0 copy-start
  7.2 1.3 convert_reduce_fusion.2
  8.5 1.2 multiply_reduce_fusion.1
  9.7 4.4 %fusion.18 = bf16[24,8,24,128]{3,1,2,0:T(8,128)(2,1)S(1)} fusion(bf16[1024,3072]{1,0:T(8,128)(2,1)} %param.7, bf16[1,192,1024]{2,1,0:T(8,128)(2,1)} %param.5, f32[192]{0:T(256)S(1)} %fusion.45, f32[192]{0:T(256)S(1)} %broadcast_multiply_fusion), kind=kOutput, calls=%fused_computation.32 | convolution fusion | flops 1209335808 | bytes 7865856 | tf_op jit(solution)/shard_map/dot_general | solution.py:100
  14.2 0.2 copy.60
  14.4 0.0 copy-start.3
  14.4 0.2 fusion.48
  14.6 0.1 copy.42
  14.6 0.8 copy.43
  15.5 0.1 copy.40
  16.2 0.9 fusion.25
  17.1 0.0 copy-start.7
  17.1 0.1 copy.61
  17.2 0.1 copy.41
  17.2 0.1 broadcast_in_dim.22
  17.4 0.7 copy-done.7
  18.1 0.1 broadcast_in_dim.23
  18.2 1.6 pad_maximum_fusion
  19.8 8.6 %all-to-all-start = ((bf16[16,576,128]{2,1,0:T(8,128)(2,1)}), bf16[16,576,128]{2,1,0:T(8,128)(2,1)}, u32[]{:S(2)}, u32[]{:S(2)}) async-start(bf16[16,576,128]{2,1,0:T(8,128)(2,1)} %pad_maximum_fusion), calls=%async_computation | async-start | bytes 4718592 | tf_op jit(solution)/shard_map/all_to_all | solution.py:126
  28.4 0.1 rsqrt.16
  28.5 0.1 div.27
  28.6 0.2 multiply_convert_fusion
  28.8 31.5 %all-to-all-done.q_ref.do_ref.k_ref.v_ref = bf16[16,576,128]{2,1,0:T(8,128)(2,1)} async-done(((bf16[16,576,128]{2,1,0:T(8,128)(2,1)}), bf16[16,576,128]{2,1,0:T(8,128)(2,1)}, u32[]{:S(2)}, u32[]{:S(2)}) %all-to-all-start) | async-done | bytes 2359328 | tf_op jit(solution)/shard_map/all_to_all | solution.py:126
  60.3 2.1 broadcast_in_dim.51
  62.4 4.5 %all-to-all-start.2 = ((bf16[16,96,1024]{2,1,0:T(8,128)(2,1)}), bf16[16,96,1024]{2,1,0:T(8,128)(2,1)}, u32[]{:S(2)}, u32[]{:S(2)}) async-start(bf16[16,96,1024]{2,1,0:T(8,128)(2,1)} %bitcast.152), calls=%async_computation.2 | async-start | bytes 6291456 | tf_op jit(solution)/shard_map/all_to_all | solution.py:128
  66.9 0.6 compare_select_fusion.bias_ref
  67.5 22.8 %shard_map.84 = (bf16[16,96,128]{2,1,0:T(8,128)(2,1)}, bf16[16,96,128]{2,1,0:T(8,128)(2,1)}, f32[3072,128]{1,0:T(8,128)}, f32[3072,128]{1,0:T(8,128)}) custom-call(bf16[16,576,128]{2,1,0:T(8,128)(2,1)} %all-to-all-done.q_ref.do_ref.k_ref.v_ref, bf16[16,576,128]{2,1,0:T(8,128)(2,1)} %all-to-all-done.q_ref.do_ref.k_ref.v_ref, ...), custom_call_target="tpu_custom_call" | custom-call | tf_op jit(solution)/shard_map/pallas_call | solution.py:61
  90.4 1.5 fusion.34
  91.9 1.3 collective-permute-start
  93.1 27.7 %collective-permute-done = bf16[16,96,2,128]{3,1,0,2:T(8,128)(2,1)} collective-permute-done((bf16[16,96,2,128]{3,1,0,2:T(8,128)(2,1)S(1)}, bf16[16,96,2,128]{3,1,0,2:T(8,128)(2,1)}, u32[]{:S(2)}, u32[]{:S(2)}) %collective-permute-start) | collective-permute-done | bytes 786464 | tf_op jit(solution)/shard_map/ppermute | solution.py:13
  120.8 1.8 fusion.11
  122.6 0.2 pad_maximum_fusion.1
  122.8 1.3 copy.46
  124.1 7.3 %all-to-all-start.1 = ((bf16[16,96,4,128]{3,1,2,0:T(8,128)(2,1)}), bf16[16,96,4,128]{3,1,2,0:T(8,128)(2,1)}, u32[]{:S(2)}, u32[]{:S(2)}) async-start(bf16[16,96,4,128]{3,1,2,0:T(8,128)(2,1)} %copy.46), calls=%async_computation.1 | async-start | bytes 3145728 | tf_op jit(solution)/shard_map/all_to_all | solution.py:149
  131.4 0.2 all-gather.2.cloned.1.call-start
  131.6 3.8 %bitcast_convert_fusion = bf16[1024,3,128]{2,0,1:T(8,128)(2,1)S(1)} fusion(bf16[16,96,1024]{2,1,0:T(8,128)(2,1)} %all-to-all-done.2, bf16[16,96,2,128]{3,1,0,2:T(8,128)(2,1)S(1)} %fusion.11, bf16[16,96,1,128]{3,1,0,2:T(8,128)(2,1)} %bitcast.173), kind=kOutput, calls=%fused_computation.26 | convolution fusion | flops 1210712064 | bytes 5111808 | tf_op jit(solution)/shard_map/dot_general | solution.py:157
  135.4 1.7 copy.50
  137.1 2.4 %concatenate.23 = bf16[16,4,2,8,384]{4,3,2,1,0:T(8,128)(2,1)S(1)} reshape(bf16[1024,3,128]{2,1,0:T(4,128)(2,1)} %copy.50) | data formatting | bytes 1572864 | tf_op jit(solution)/shard_map/concatenate | solution.py:165
  139.5 12.6 %all-to-all-done.1 = bf16[16,96,4,128]{3,1,2,0:T(8,128)(2,1)} async-done(((bf16[16,96,4,128]{3,1,2,0:T(8,128)(2,1)}), bf16[16,96,4,128]{3,1,2,0:T(8,128)(2,1)}, u32[]{:S(2)}, u32[]{:S(2)}) %all-to-all-start.1) | async-done | bytes 1572896 | tf_op jit(solution)/shard_map/all_to_all | solution.py:149
  152.1 2.4 %copy.79 = bf16[8,2,96,4,128]{4,0,2,1,3:T(8,128)(2,1)S(1)} copy(bf16[8,2,96,4,128]{4,2,3,1,0:T(8,128)(2,1)} %bitcast.20) | data formatting | bytes 3145728 | tf_op jit(solution)/shard_map/reshape | solution.py:150
  154.6 0.7 copy-done.5
  155.4 0.8 copy.80
  156.2 2.0 copy.51
  158.2 1.9 convolution_convert_fusion.1
  160.1 1.4 fusion.15
  161.5 0.4 copy-done.1
  161.9 4.0 %collective-permute-start.1 = (bf16[16,4,8,1408]{3,2,1,0:T(8,128)(2,1)}, bf16[16,4,8,1408]{3,2,1,0:T(8,128)(2,1)}, u32[]{:S(2)}, u32[]{:S(2)}) collective-permute-start(bf16[16,4,8,1408]{3,2,1,0:T(8,128)(2,1)} %fusion.15), channel_id=1, source_target_pairs={{0,16},{16,0},{1,17},{17,1},{2,18},{18,2},{3,19},{19,3},{4,20},{20... | collective-permute-start | bytes 4325384 | tf_op jit(solution)/shard_map/ppermute | solution.py:169
  165.9 3.2 %collective-permute-done.1 = bf16[16,4,8,1408]{3,2,1,0:T(8,128)(2,1)} collective-permute-done((bf16[16,4,8,1408]{3,2,1,0:T(8,128)(2,1)}, bf16[16,4,8,1408]{3,2,1,0:T(8,128)(2,1)}, u32[]{:S(2)}, u32[]{:S(2)}) %collective-permute-start.1) | collective-permute-done | bytes 1441824 | tf_op jit(solution)/shard_map/ppermute | solution.py:169
  169.1 2.0 fusion.4
  171.1 27.4 %all_to_all.20 = bf16[64,8,1408]{2,1,0:T(8,128)(2,1)S(1)} all-to-all(bf16[64,8,1408]{2,1,0:T(8,128)(2,1)S(1)} %bitcast.160), channel_id=1, replica_groups=mesh['y'=4,'core'=2,'seq'=16] {'seq','y'}, dimensions={0} | all-to-all | bytes 2883584 | tf_op jit(solution)/shard_map/all_to_all | solution.py:171
  198.6 0.1 convert_reduce_fusion.1
  198.7 0.2 convert_reduce_fusion
  198.8 0.7 pad_maximum_fusion.2
  199.5 0.0 all-gather.2.cloned.1.call-update
  199.5 4.7 %copy.63 = bf16[128,8,24,128]{3,2,1,0:T(8,128)(2,1)S(1)} copy(bf16[128,8,24,128]{3,1,2,0:T(8,128)(2,1)} %bitcast.154) | data formatting | bytes 12582912
  204.3 1.4 slice.42
  205.6 0.1 copy.59
  205.8 2.3 %multiply_reduce_fusion = (f32[192]{0:T(256)S(1)}, f32[192,1024]{1,0:T(8,128)S(1)}) fusion(bf16[1,192,1024]{2,1,0:T(8,128)(2,1)S(1)} %copy-done.2, f32[192]{0:T(256)S(1)} %broadcast_multiply_fusion, bf16[192,8,3,128]{3,0,2,1:T(8,128)(2,1)S(1)} %bitcast.172, bf16[1024,3,8,128]{3,2,1,0:T(8,128)(2,1)S(1)} %bitcast.155), kind=kOutput, calls=%fused_computation.55 | convolution fusion | flops 1208745728 | bytes 8652288 | tf_op jit(solution)/shard_map/dot_general | solution.py:185
  208.1 0.3 fusion.47
  208.5 1.3 fusion.24
  209.8 1.1 fusion.37
  210.9 10.2 %all-gather.2.cloned.1.call-done = f32[64,4096]{1,0:T(8,128)} async-done(((f32[8,4096]{1,0:T(8,128)}), f32[64,4096]{1,0:T(8,128)}) %all-gather.2.cloned.1.call-update) | async-done | bytes 1048592 | tf_op jit(solution)/shard_map/all_gather | solution.py:182
  221.1 2.1 slice.45
  223.2 1.7 slice.46
  (23 shorter events, 0.1 us)
Async XLA Ops:
  7.2 9.0 %copy-start = (bf16[1024,1024]{1,0:T(8,128)(2,1)S(1)}, bf16[1024,1024]{1,0:T(8,128)(2,1)}, u32[]{:S(2)}) copy-start(bf16[1024,1024]{1,0:T(8,128)(2,1)} %param.8) | copy-start | bytes 6291460
  14.4 1.8 copy-start.3
  17.1 1.0 copy-start.7
  19.8 8.8 %copy-start.2 = (bf16[1,192,1024]{2,1,0:T(8,128)(2,1)S(1)}, bf16[1,192,1024]{2,1,0:T(8,128)(2,1)}, u32[]{:S(2)}) copy-start(bf16[1,192,1024]{2,1,0:T(8,128)(2,1)} %param.5) | copy-start | bytes 1179652
  19.8 40.5 %all-to-all-start = ((bf16[16,576,128]{2,1,0:T(8,128)(2,1)}), bf16[16,576,128]{2,1,0:T(8,128)(2,1)}, u32[]{:S(2)}, u32[]{:S(2)}) async-start(bf16[16,576,128]{2,1,0:T(8,128)(2,1)} %pad_maximum_fusion), calls=%async_computation | async-start | bytes 4718592 | tf_op jit(solution)/shard_map/all_to_all | solution.py:126
  62.4 61.7 %all-to-all-start.2 = ((bf16[16,96,1024]{2,1,0:T(8,128)(2,1)}), bf16[16,96,1024]{2,1,0:T(8,128)(2,1)}, u32[]{:S(2)}, u32[]{:S(2)}) async-start(bf16[16,96,1024]{2,1,0:T(8,128)(2,1)} %bitcast.152), calls=%async_computation.2 | async-start | bytes 6291456 | tf_op jit(solution)/shard_map/all_to_all | solution.py:128
  91.9 28.9 %collective-permute-start = (bf16[16,96,2,128]{3,1,0,2:T(8,128)(2,1)S(1)}, bf16[16,96,2,128]{3,1,0,2:T(8,128)(2,1)}, u32[]{:S(2)}, u32[]{:S(2)}) collective-permute-start(bf16[16,96,2,128]{3,1,0,2:T(8,128)(2,1)S(1)} %fusion.34), channel_id=1, source_target_pairs={{0,1},{1,0},{2,3},{3,2},{4,5},{5,4},{6,7},{7,6},{8,9},{9,8},{10,11... | collective-permute-start | bytes 2359304 | tf_op jit(solution)/shard_map/ppermute | solution.py:13
  93.1 29.5 %copy-start.8 = (bf16[16,96,128]{2,1,0:T(8,128)(2,1)S(1)}, bf16[16,96,128]{2,1,0:T(8,128)(2,1)}, u32[]{:S(2)}) copy-start(bf16[16,96,128]{2,1,0:T(8,128)(2,1)} %get-tuple-element.9) | copy-start | bytes 1179652
  93.1 29.5 %copy-start.9 = (bf16[16,96,128]{2,1,0:T(8,128)(2,1)S(1)}, bf16[16,96,128]{2,1,0:T(8,128)(2,1)}, u32[]{:S(2)}) copy-start(bf16[16,96,128]{2,1,0:T(8,128)(2,1)} %get-tuple-element.8) | copy-start | bytes 1179652
  124.1 28.1 %all-to-all-start.1 = ((bf16[16,96,4,128]{3,1,2,0:T(8,128)(2,1)}), bf16[16,96,4,128]{3,1,2,0:T(8,128)(2,1)}, u32[]{:S(2)}, u32[]{:S(2)}) async-start(bf16[16,96,4,128]{3,1,2,0:T(8,128)(2,1)} %copy.46), calls=%async_computation.1 | async-start | bytes 3145728 | tf_op jit(solution)/shard_map/all_to_all | solution.py:149
  131.4 89.7 %all-gather.2.cloned.1.call-start = ((), (), s32[]{:S(2)}) async-start(), calls=%async_computation.4 | async-start | bytes 1179648 | tf_op jit(solution)/shard_map/all_gather | solution.py:182
  154.6 0.7 copy-start.5
  160.1 1.8 copy-start.1
  161.9 7.2 %collective-permute-start.1 = (bf16[16,4,8,1408]{3,2,1,0:T(8,128)(2,1)}, bf16[16,4,8,1408]{3,2,1,0:T(8,128)(2,1)}, u32[]{:S(2)}, u32[]{:S(2)}) collective-permute-start(bf16[16,4,8,1408]{3,2,1,0:T(8,128)(2,1)} %fusion.15), channel_id=1, source_target_pairs={{0,16},{16,0},{1,17},{17,1},{2,18},{18,2},{3,19},{19,3},{4,20},{20... | collective-permute-start | bytes 4325384 | tf_op jit(solution)/shard_map/ppermute | solution.py:169
  205.7 2.7 %copy-start.6 = (bf16[2,96,1,8,128]{4,3,1,0,2:T(8,128)(2,1)S(1)}, bf16[2,96,1,8,128]{4,3,1,0,2:T(8,128)(2,1)}, u32[]{:S(2)}) copy-start(bf16[2,96,1,8,128]{4,3,1,0,2:T(8,128)(2,1)} %copy-done.5) | copy-start | bytes 1179652
  208.1 1.7 copy-start.4
Sparse Core Ops, SparseCore 0:
  199.7 21.3 all-gather.1

commit v14 on v13

--- a/solution.py
+++ b/solution.py
@@ -148,16 +148,20 @@
     )
     returned = lax.all_to_all(back, "seq", split_axis=0, concat_axis=0, tiled=True)
     returned_heads = returned.reshape(H, groups, part_rows, 4, head_size)
-    returned = returned_heads.transpose(1, 2, 3, 0, 4)
-    context = returned[:, :, 0].reshape(tok_rows, width)
-    dqkv = returned[:, :, 1:].reshape(tok_rows, 3 * width)
-    branch = jnp.dot(context, w_out, preferred_element_type=jnp.float32)
+    context_heads = returned_heads[:, :, :, 0]
+    branch = lax.dot_general(
+        context_heads, w_out.reshape(H, head_size, width), (((0, 3), (0, 1)), ((), ())),
+        preferred_element_type=jnp.float32,
+    ).reshape(tok_rows, width)
     output = (inputs + valid[:, None] * branch).astype(jnp.bfloat16)
     over_frames = (((0, 1), (0, 1)), ((), ()))
     qkv_part = lax.dot_general(
         normed_recv, back[:, :, 1:], over_frames, preferred_element_type=jnp.float32
     ).reshape(width, 3 * head_size)
-    out_part = jnp.dot(context.T, grad_rows, preferred_element_type=jnp.float32)
+    out_part = lax.dot_general(
+        context_heads, grad_rows.reshape(groups, part_rows, width), (((1, 2), (0, 1)), ((), ())),
+        preferred_element_type=jnp.float32,
+    ).reshape(width, width)
     y_count = lax.axis_size("y")
     core_count = lax.axis_size("core")
     core_index = lax.axis_index("core")

time: 233 us -> 237 us (1.017)
  blocking collectives: 27.4 us -> 0 us
  waiting for transfers between devices: 85.2 us -> 98.9 us
  starting transfers between devices: 25.9 us -> 33.9 us
  other arithmetic: 14.2 us -> 18.1 us
  local copies, waits for them, and re-layouts: 26.5 us -> 29.7 us
  matrix products: 14.7 us -> 17.6 us
    all_to_all x1 -> x0, blocking collectives: 27.4 us -> none  [per_device(): lax.all_to_all(chip_sum.reshape(seq_count * y_count, piece_rows, parts.sh...]
    all_to_all x0 -> x1, waiting for transfers between devices: none -> 13.5 us  [per_device(): lax.all_to_all(chip_sum.reshape(seq_count * y_count, piece_rows, parts.sh...]
    all_to_all x0 -> x1, starting transfers between devices: none -> 7.26 us  [per_device(): lax.all_to_all(chip_sum.reshape(seq_count * y_count, piece_rows, parts.sh...]
    dot_general x1 -> x5, local copies, waits for them, and re-layouts: 1.99 us -> 5.73 us  [the longest x3 4.26 us: per_device(): lax.dot_general(context_heads, grad_rows.reshape(groups, part_rows, width...]
    dot_general x1, matrix products: 2.34 us -> 5.17 us  [per_device(): lax.dot_general(returned_heads[:, :, :, 1:], w_qkv.reshape(width, 3, H, h...]
    reshape x1 -> x0, local copies, waits for them, and re-layouts: 2.42 us -> none  [per_device(): returned_heads = returned.reshape(H, groups, part_rows, 4, head_size)]
    unnamed x26 -> x24, local copies, waits for them, and re-layouts: 7.78 us -> 9.74 us
  transfers between devices with their start and end apart: 6 -> 7, of which waited for: 5 -> 6; matrix products, arithmetic and copies ran while one was open for 11% -> 14% of each run, Pallas kernels for 10% -> 10%
where the time goes in v14:
time: 237 us; the launch traced here: 236 us
  waiting for transfers between devices  98.9 us (42%)
  starting transfers between devices  33.9 us (14%)
  local copies, waits for them, and re-layouts  29.7 us (13%)
  Pallas kernels  22.9 us (10%)
  other arithmetic  18.1 us (8%)
  matrix products  17.6 us (7%)
  between operations  15 us (6%)
    all_to_all x1, waiting for transfers between devices, per_device(): recv = lax.all_to_all(send, 'seq', split_axis=0, concat_axis=0, tiled=True)  31.5 us
    ppermute x1, waiting for transfers between devices, from_partner(): lax.ppermute(array, axis, [(i, i ^ 1 << stride) for i in range(lax.axis_s...  26.9 us
    pallas_call x1, Pallas kernels, attn_pass(): pl.pallas_call(kernel, grid=(sources // block_sources,), in_specs=[pl.Blo...  22.9 us
    all_to_all x1, waiting for transfers between devices, per_device(): lax.all_to_all(chip_sum.reshape(seq_count * y_count, piece_rows, parts.sh...  13.5 us
    all_gather x1, waiting for transfers between devices, per_device(): lax.all_gather(jnp.concatenate([qkv_rows, out_rows], axis=1), ('y', 'core...  12.1 us
    all_to_all x1, waiting for transfers between devices, per_device(): lax.all_to_all(back, 'seq', split_axis=0, concat_axis=0, tiled=True)  11.8 us
    unnamed x24, local copies, waits for them, and re-layouts  9.74 us
    all_to_all x1, starting transfers between devices, per_device(): recv = lax.all_to_all(send, 'seq', split_axis=0, concat_axis=0, tiled=True)  8.59 us
  transfers between devices with their start and end apart: 7, of which 6 were waited for; matrix products, arithmetic and copies ran while one was open for 14% of the time, Pallas kernels for 10%

profile of v14, /device:TPU:1, one launch (start us, length us, event | category | flops | bytes accessed | tf_op | source)
XLA Modules:
  0.0 236.2 jit_solution(12546443600932641236)
XLA Ops:
  7.2 1.3 convert_reduce_fusion.2
  8.5 1.2 multiply_reduce_fusion.1
  9.7 4.4 %fusion.18 = bf16[24,8,24,128]{3,1,2,0:T(8,128)(2,1)S(1)} fusion(bf16[1024,3072]{1,0:T(8,128)(2,1)} %param.7, bf16[1,192,1024]{2,1,0:T(8,128)(2,1)} %param.5, f32[192]{0:T(256)S(1)} %fusion.43, f32[192]{0:T(256)S(1)} %broadcast_multiply_fusion), kind=kOutput, calls=%fused_computation.31 | convolution fusion | flops 1209335808 | bytes 7865856 | tf_op jit(solution)/shard_map/dot_general | solution.py:100
  14.2 0.2 copy.93
  14.4 0.2 fusion.46
  14.6 0.1 copy.71
  14.6 0.8 copy.72
  15.5 0.1 copy.69
  16.2 0.9 fusion.26
  17.1 0.1 copy.94
  17.2 0.1 copy.70
  17.2 0.1 broadcast_in_dim.22
  17.4 0.7 copy-done.7
  18.1 0.1 broadcast_in_dim.23
  18.2 1.6 pad_maximum_fusion
  19.8 8.6 %all-to-all-start = ((bf16[16,576,128]{2,1,0:T(8,128)(2,1)}), bf16[16,576,128]{2,1,0:T(8,128)(2,1)}, u32[]{:S(2)}, u32[]{:S(2)}) async-start(bf16[16,576,128]{2,1,0:T(8,128)(2,1)} %pad_maximum_fusion), calls=%async_computation | async-start | bytes 4718592 | tf_op jit(solution)/shard_map/all_to_all | solution.py:126
  28.4 0.1 rsqrt.16
  28.5 0.1 div.27
  28.6 0.2 multiply_convert_fusion
  28.8 31.5 %all-to-all-done.q_ref.do_ref.k_ref.v_ref = bf16[16,576,128]{2,1,0:T(8,128)(2,1)} async-done(((bf16[16,576,128]{2,1,0:T(8,128)(2,1)}), bf16[16,576,128]{2,1,0:T(8,128)(2,1)}, u32[]{:S(2)}, u32[]{:S(2)}) %all-to-all-start) | async-done | bytes 2359328 | tf_op jit(solution)/shard_map/all_to_all | solution.py:126
  60.3 2.1 broadcast_in_dim.51
  62.4 4.5 %all-to-all-start.2 = ((bf16[16,96,1024]{2,1,0:T(8,128)(2,1)}), bf16[16,96,1024]{2,1,0:T(8,128)(2,1)}, u32[]{:S(2)}, u32[]{:S(2)}) async-start(bf16[16,96,1024]{2,1,0:T(8,128)(2,1)} %bitcast.164), calls=%async_computation.2 | async-start | bytes 6291456 | tf_op jit(solution)/shard_map/all_to_all | solution.py:128
  66.9 0.6 compare_select_fusion.bias_ref
  67.5 22.9 %shard_map.84 = (bf16[16,96,128]{2,1,0:T(8,128)(2,1)}, bf16[16,96,128]{2,1,0:T(8,128)(2,1)}, f32[3072,128]{1,0:T(8,128)}, f32[3072,128]{1,0:T(8,128)}) custom-call(bf16[16,576,128]{2,1,0:T(8,128)(2,1)} %all-to-all-done.q_ref.do_ref.k_ref.v_ref, bf16[16,576,128]{2,1,0:T(8,128)(2,1)} %all-to-all-done.q_ref.do_ref.k_ref.v_ref, ...), custom_call_target="tpu_custom_call" | custom-call | tf_op jit(solution)/shard_map/pallas_call | solution.py:61
  90.4 2.4 fusion.35
  92.7 1.2 collective-permute-start
  93.9 26.9 %collective-permute-done = bf16[16,96,2,128]{3,1,0,2:T(8,128)(2,1)} collective-permute-done((bf16[16,96,2,128]{3,1,0,2:T(8,128)(2,1)}, bf16[16,96,2,128]{3,1,0,2:T(8,128)(2,1)}, u32[]{:S(2)}, u32[]{:S(2)}) %collective-permute-start) | collective-permute-done | bytes 786464 | tf_op jit(solution)/shard_map/ppermute | solution.py:13
  120.8 1.8 fusion.11
  122.6 0.9 copy-done.5
  123.5 0.2 pad_maximum_fusion.1
  123.6 1.4 copy.75
  125.0 8.4 %all-to-all-start.1 = ((bf16[16,96,4,128]{3,1,2,0:T(8,128)(2,1)}), bf16[16,96,4,128]{3,1,2,0:T(8,128)(2,1)}, u32[]{:S(2)}, u32[]{:S(2)}) async-start(bf16[16,96,4,128]{3,1,2,0:T(8,128)(2,1)} %copy.75), calls=%async_computation.1 | async-start | bytes 3145728 | tf_op jit(solution)/shard_map/all_to_all | solution.py:149
  133.4 0.1 reshape.204
  133.5 0.9 fusion.34
  134.4 3.9 %bitcast_convert_fusion.1 = bf16[1024,3,128]{2,0,1:T(8,128)(2,1)S(1)} fusion(bf16[16,96,1024]{2,1,0:T(8,128)(2,1)} %all-to-all-done.2, bf16[16,96,2,128]{3,1,0,2:T(8,128)(2,1)} %copy-done.5, bf16[16,96,1,128]{3,1,0,2:T(8,128)(2,1)S(1)} %bitcast.183), kind=kOutput, calls=%fused_computation.26 | convolution fusion | flops 1210712064 | bytes 5111808 | tf_op jit(solution)/shard_map/dot_general | solution.py:158
  138.3 1.6 copy.78
  139.9 2.4 %concatenate.23 = bf16[16,4,2,8,384]{4,3,2,1,0:T(8,128)(2,1)S(1)} reshape(bf16[1024,3,128]{2,1,0:T(4,128)(2,1)} %copy.78) | data formatting | bytes 1572864 | tf_op jit(solution)/shard_map/concatenate | solution.py:169
  142.4 11.8 %all-to-all-done.1 = bf16[16,96,4,128]{3,1,2,0:T(8,128)(2,1)} async-done(((bf16[16,96,4,128]{3,1,2,0:T(8,128)(2,1)}), bf16[16,96,4,128]{3,1,2,0:T(8,128)(2,1)}, u32[]{:S(2)}, u32[]{:S(2)}) %all-to-all-start.1) | async-done | bytes 1572896 | tf_op jit(solution)/shard_map/all_to_all | solution.py:149
  154.1 2.0 slice_bitcast_fusion.3
  156.2 2.0 copy.79
  158.2 1.9 fusion.36
  160.1 0.2 copy.112
  160.3 1.4 fusion.15
  161.7 0.4 copy-done.1
  162.1 4.0 %collective-permute-start.1 = (bf16[16,4,8,1408]{3,2,0,1:T(8,128)(2,1)}, bf16[16,4,8,1408]{3,2,0,1:T(8,128)(2,1)}, u32[]{:S(2)}, u32[]{:S(2)}) collective-permute-start(bf16[16,4,8,1408]{3,2,0,1:T(8,128)(2,1)} %fusion.15), channel_id=1, source_target_pairs={{0,16},{16,0},{1,17},{17,1},{2,18},{18,2},{3,19},{19,3},{4,20},{20... | collective-permute-start | bytes 4325384 | tf_op jit(solution)/shard_map/ppermute | solution.py:173
  166.2 3.2 %collective-permute-done.1 = bf16[16,4,8,1408]{3,2,0,1:T(8,128)(2,1)} collective-permute-done((bf16[16,4,8,1408]{3,2,0,1:T(8,128)(2,1)}, bf16[16,4,8,1408]{3,2,0,1:T(8,128)(2,1)}, u32[]{:S(2)}, u32[]{:S(2)}) %collective-permute-start.1) | collective-permute-done | bytes 1441824 | tf_op jit(solution)/shard_map/ppermute | solution.py:173
  169.4 2.0 fusion.4
  171.4 1.2 copy.82
  172.6 7.3 %all-to-all-start.3 = ((bf16[64,8,1408]{2,1,0:T(8,128)(2,1)}), bf16[64,8,1408]{2,1,0:T(8,128)(2,1)}, u32[]{:S(2)}, u32[]{:S(2)}) async-start(bf16[64,8,1408]{2,1,0:T(8,128)(2,1)} %bitcast.171), calls=%async_computation.3 | async-start | bytes 2883584 | tf_op jit(solution)/shard_map/all_to_all | solution.py:175
  179.9 0.0 all-gather.2.cloned.1.call-start
  179.9 7.4 %copy.95 = bf16[128,8,24,128]{3,2,1,0:T(8,128)(2,1)} copy(bf16[128,8,24,128]{3,1,2,0:T(8,128)(2,1)} %bitcast.165) | data formatting | bytes 12582912
  187.3 13.5 %all-to-all-done.3 = bf16[64,8,1408]{2,1,0:T(8,128)(2,1)} async-done(((bf16[64,8,1408]{2,1,0:T(8,128)(2,1)}), bf16[64,8,1408]{2,1,0:T(8,128)(2,1)}, u32[]{:S(2)}, u32[]{:S(2)}) %all-to-all-start.3) | async-done | bytes 1441824 | tf_op jit(solution)/shard_map/all_to_all | solution.py:175
  200.8 1.1 convert_reduce_fusion.1
  201.9 1.4 convert_reduce_fusion
  203.3 0.7 pad_maximum_fusion.2
  204.0 1.4 slice_bitcast_fusion
  205.4 0.1 copy.76
  205.5 5.2 %multiply_reduce_fusion = (f32[192]{0:T(256)S(1)}, f32[192,1024]{1,0:T(8,128)S(1)}) fusion(bf16[1,192,1024]{2,1,0:T(8,128)(2,1)S(1)} %copy-done.2, f32[192]{0:T(256)S(1)} %broadcast_multiply_fusion, bf16[192,8,3,128]{3,0,2,1:T(8,128)(2,1)S(1)} %bitcast.181, bf16[1024,3,8,128]{3,2,1,0:T(8,128)(2,1)} %bitcast.166), kind=kOutput, calls=%fused_computation.56 | convolution fusion | flops 1208745728 | bytes 8652288 | tf_op jit(solution)/shard_map/dot_general | solution.py:189
  210.7 0.3 fusion.45
  211.1 1.4 fusion.25
  212.5 1.1 fusion.38
  213.5 12.1 %all-gather.2.cloned.1.call-done = f32[64,4096]{1,0:T(8,128)} async-done(((f32[8,4096]{1,0:T(8,128)}), f32[64,4096]{1,0:T(8,128)}) %all-gather.2.cloned.1.call-update) | async-done | bytes 1048592 | tf_op jit(solution)/shard_map/all_gather | solution.py:186
  225.6 2.1 slice.45
  227.7 1.7 slice.46
  (27 shorter events, 0.2 us)
Async XLA Ops:
  7.2 9.0 %copy-start = (bf16[1024,1024]{1,0:T(8,128)(2,1)S(1)}, bf16[1024,1024]{1,0:T(8,128)(2,1)}, u32[]{:S(2)}) copy-start(bf16[1024,1024]{1,0:T(8,128)(2,1)} %param.8) | copy-start | bytes 6291460
  14.4 1.8 copy-start.3
  17.1 1.0 copy-start.7
  19.8 8.8 %copy-start.2 = (bf16[1,192,1024]{2,1,0:T(8,128)(2,1)S(1)}, bf16[1,192,1024]{2,1,0:T(8,128)(2,1)}, u32[]{:S(2)}) copy-start(bf16[1,192,1024]{2,1,0:T(8,128)(2,1)} %param.5) | copy-start | bytes 1179652
  19.8 40.5 %all-to-all-start = ((bf16[16,576,128]{2,1,0:T(8,128)(2,1)}), bf16[16,576,128]{2,1,0:T(8,128)(2,1)}, u32[]{:S(2)}, u32[]{:S(2)}) async-start(bf16[16,576,128]{2,1,0:T(8,128)(2,1)} %pad_maximum_fusion), calls=%async_computation | async-start | bytes 4718592 | tf_op jit(solution)/shard_map/all_to_all | solution.py:126
  62.4 62.6 %all-to-all-start.2 = ((bf16[16,96,1024]{2,1,0:T(8,128)(2,1)}), bf16[16,96,1024]{2,1,0:T(8,128)(2,1)}, u32[]{:S(2)}, u32[]{:S(2)}) async-start(bf16[16,96,1024]{2,1,0:T(8,128)(2,1)} %bitcast.164), calls=%async_computation.2 | async-start | bytes 6291456 | tf_op jit(solution)/shard_map/all_to_all | solution.py:128
  92.7 28.0 %collective-permute-start = (bf16[16,96,2,128]{3,1,0,2:T(8,128)(2,1)}, bf16[16,96,2,128]{3,1,0,2:T(8,128)(2,1)}, u32[]{:S(2)}, u32[]{:S(2)}) collective-permute-start(bf16[16,96,2,128]{3,1,0,2:T(8,128)(2,1)} %fusion.35), channel_id=1, source_target_pairs={{0,1},{1,0},{2,3},{3,2},{4,5},{5,4},{6,7},{7,6},{8,9},{9,8},{10,11... | collective-permute-start | bytes 2359304 | tf_op jit(solution)/shard_map/ppermute | solution.py:13
  93.9 29.5 %copy-start.8 = (bf16[16,96,128]{2,1,0:T(8,128)(2,1)S(1)}, bf16[16,96,128]{2,1,0:T(8,128)(2,1)}, u32[]{:S(2)}) copy-start(bf16[16,96,128]{2,1,0:T(8,128)(2,1)} %get-tuple-element.9) | copy-start | bytes 1179652
  93.9 29.5 %copy-start.9 = (bf16[16,96,128]{2,1,0:T(8,128)(2,1)S(1)}, bf16[16,96,128]{2,1,0:T(8,128)(2,1)}, u32[]{:S(2)}) copy-start(bf16[16,96,128]{2,1,0:T(8,128)(2,1)} %get-tuple-element.8) | copy-start | bytes 1179652
  122.6 0.9 copy-start.5
  125.0 29.1 %all-to-all-start.1 = ((bf16[16,96,4,128]{3,1,2,0:T(8,128)(2,1)}), bf16[16,96,4,128]{3,1,2,0:T(8,128)(2,1)}, u32[]{:S(2)}, u32[]{:S(2)}) async-start(bf16[16,96,4,128]{3,1,2,0:T(8,128)(2,1)} %copy.75), calls=%async_computation.1 | async-start | bytes 3145728 | tf_op jit(solution)/shard_map/all_to_all | solution.py:149
  160.3 1.8 copy-start.1
  162.1 7.2 %collective-permute-start.1 = (bf16[16,4,8,1408]{3,2,0,1:T(8,128)(2,1)}, bf16[16,4,8,1408]{3,2,0,1:T(8,128)(2,1)}, u32[]{:S(2)}, u32[]{:S(2)}) collective-permute-start(bf16[16,4,8,1408]{3,2,0,1:T(8,128)(2,1)} %fusion.15), channel_id=1, source_target_pairs={{0,16},{16,0},{1,17},{17,1},{2,18},{18,2},{3,19},{19,3},{4,20},{20... | collective-permute-start | bytes 4325384 | tf_op jit(solution)/shard_map/ppermute | solution.py:173
  172.6 28.2 %all-to-all-start.3 = ((bf16[64,8,1408]{2,1,0:T(8,128)(2,1)}), bf16[64,8,1408]{2,1,0:T(8,128)(2,1)}, u32[]{:S(2)}, u32[]{:S(2)}) async-start(bf16[64,8,1408]{2,1,0:T(8,128)(2,1)} %bitcast.171), calls=%async_computation.3 | async-start | bytes 2883584 | tf_op jit(solution)/shard_map/all_to_all | solution.py:175
  179.9 45.7 %all-gather.2.cloned.1.call-start = ((), (), s32[]{:S(2)}) async-start(), calls=%async_computation.4 | async-start | bytes 1179648 | tf_op jit(solution)/shard_map/all_gather | solution.py:186
  205.5 5.6 %copy-start.6 = (bf16[8,2,96,1,128]{4,2,3,1,0:T(8,128)(2,1)S(1)}, bf16[8,2,96,1,128]{4,2,3,1,0:T(8,128)(2,1)}, u32[]{:S(2)}) copy-start(bf16[8,2,96,1,128]{4,2,3,1,0:T(8,128)(2,1)} %get-tuple-element.13) | copy-start | bytes 1179652
  210.7 1.8 copy-start.4
Sparse Core Ops, SparseCore 0:
  204.2 21.4 all-gather.1
